TPU v7x, 128 devices: a whole 4x4x4 slice. The times are simulated.
128 devices in a mesh: ev: 32 (over z, x, core), node: 4 (over y).
Axes of the slice: x: 4, y: 4, z: 4, core: 2. Of those that a mesh axis runs over, the one named last changes fastest.
Arguments:
- src_owner: int32 [65536, 1], P(('ev', 'node')), may hold values from 0 to 127; in each aligned block of 512 rows (0 to 511, 512 to 1023, ...) at most 8 rows name the same one
- src_row: int32 [65536], P(('ev', 'node')), may hold values from 0 to 4095
- dst_owner: int32 [65536, 1], P(('ev', 'node')), may hold values from 0 to 127; in each aligned block of 512 rows (0 to 511, 512 to 1023, ...) at most 8 rows name the same one
- dst_row: int32 [65536], P(('ev', 'node')), may hold values from 0 to 4095
- event_time: int32 [65536], P(('ev', 'node')), may hold values from 4096 to 8191
- edge_feat: bfloat16 [65536, 256], P(('ev', 'node')), may hold values from -6 to 6
- memory: bfloat16 [524288, 256], P(('ev', 'node')), may hold values from -3 to 3
- last_update: int32 [524288], P(('ev', 'node')), may hold values from 0 to 4095
- time_freq: float32 [128], replicated, may hold values from 0.0001 to 1
- time_phase: float32 [128], replicated, may hold values from -3.140625 to 3.140625
- w_msg_in: bfloat16 [896, 512], replicated, may hold values from -0.1875 to 0.1875
- b_msg: float32 [512], replicated, may hold values from -3 to 3
- w_msg_out: bfloat16 [512, 256], replicated, may hold values from -0.25 to 0.25
- w_gru_in: bfloat16 [256, 768], replicated, may hold values from -0.375 to 0.375
- b_gru_in: float32 [768], replicated, may hold values from -3 to 3
- w_gru_hid: bfloat16 [256, 768], replicated, may hold values from -0.375 to 0.375
Outputs:
- new_memory: bfloat16 [524288, 256], P(('ev', 'node'))
Inputs may be any that keep to these rules, and one draw needn't show every extreme that they name: `src_owner`: within the events of one device (aligned blocks of 512 rows) no owner is named by more than 8 events, a bound that some block reaches. `dst_owner`: within the events of one device (aligned blocks of 512 rows) no owner is named by more than 8 events, a bound that some block reaches. `event_time`: every event is later than the last update of either of its nodes.
All inputs are finite; a program needn't handle non-finite values.
Results may differ from a plain program's by a relative error of at most 0.0021.
Values may be sent and summed in bfloat16 or wider, within the bound.
No kernel may reach another device: no remote copies, remote signals or barrier semaphores. Data moves between devices by JAX's collectives and lax.ppermute only.
A program may use at most 64 MiB of HBM per device.

v0:
```python
import jax
import jax.numpy as jnp
from jax import lax
from jax.sharding import PartitionSpec as P


def encode(delta_int, time_freq, time_phase):
    delta = delta_int.astype(jnp.float32)
    return jnp.cos(delta[..., None] * time_freq + time_phase).astype(jnp.bfloat16)


def gru_update(mean_msg, state, w_gru_in, b_gru_in, w_gru_hid):
    width = state.shape[-1]
    input_part = jnp.dot(mean_msg, w_gru_in, preferred_element_type=jnp.float32) + b_gru_in
    state_part = jnp.dot(state, w_gru_hid, preferred_element_type=jnp.float32)
    reset = jax.nn.sigmoid(input_part[:, :width] + state_part[:, :width])
    update = jax.nn.sigmoid(input_part[:, width : 2 * width] + state_part[:, width : 2 * width])
    candid = jnp.tanh(input_part[:, 2 * width :] + reset * state_part[:, 2 * width :])
    return ((1.0 - update) * candid + update * state.astype(jnp.float32)).astype(jnp.bfloat16)


def slot_of(owner_ids, owner_count, capacity):
    events_here = owner_ids.shape[0]
    columns = jnp.arange(owner_count, dtype=jnp.int32)
    onehot = (owner_ids[:, None] == columns[None, :]).astype(jnp.bfloat16)
    order = jnp.arange(events_here, dtype=jnp.int32)
    lower = (order[None, :] < order[:, None]).astype(jnp.bfloat16)
    earlier = jnp.dot(lower, onehot, preferred_element_type=jnp.float32)
    position = jnp.sum(earlier * onehot.astype(jnp.float32), axis=1).astype(jnp.int32)
    return owner_ids * capacity + position


def owner_lookup(request_pair, memory, last_update, time_freq, time_phase):
    row_request = request_pair[0]
    time_request = request_pair[1]
    safe_rows = jnp.clip(row_request, 0, memory.shape[0] - 1)
    mem_rows = memory[safe_rows]
    encoded = encode(time_request - last_update[safe_rows], time_freq, time_phase)
    return jnp.concatenate([mem_rows, encoded], axis=-1)


def local(
    src_owner,
    src_row,
    dst_owner,
    dst_row,
    event_time,
    edge_feat,
    memory,
    last_update,
    time_freq,
    time_phase,
    w_msg_in,
    b_msg,
    w_msg_out,
    w_gru_in,
    b_gru_in,
    w_gru_hid,
):
    devices_all = lax.axis_size(("ev", "node"))
    events_here = edge_feat.shape[0]
    capacity = max(2, 2 * events_here // devices_all)
    width = memory.shape[1]
    time_width = time_freq.shape[0]
    hidden_width = w_msg_out.shape[0]
    msg_width = w_msg_out.shape[1]
    rows_count = memory.shape[0]
    slot_total = devices_all * capacity
    slot_ids = jnp.stack(
        [
            slot_of(src_owner[:, 0], devices_all, capacity),
            slot_of(dst_owner[:, 0], devices_all, capacity),
        ]
    )
    slot_range = jnp.arange(slot_total, dtype=jnp.int32)
    placed = slot_ids[:, None, :] == slot_range[None, :, None]
    placement = placed.astype(jnp.bfloat16)
    filled = jnp.any(placed, axis=2)
    rows_pair = jnp.stack([src_row, dst_row])
    row_sum = jnp.sum(jnp.where(placed, rows_pair[:, None, :], 0), axis=2)
    time_sum = jnp.sum(jnp.where(placed, event_time[None, None, :], 0), axis=2)
    row_request = jnp.where(filled, row_sum, -1)
    time_request = jnp.where(filled, time_sum, 0)
    edge_part = (
        jnp.dot(edge_feat, w_msg_in[2 * width + time_width :], preferred_element_type=jnp.float32)
        + b_msg
    )
    flat_shape = (2, devices_all, capacity)
    received = (
        lax.all_to_all(
            row_request.reshape(flat_shape), ("ev", "node"), split_axis=1, concat_axis=1, tiled=True
        ),
        lax.all_to_all(
            time_request.reshape(flat_shape),
            ("ev", "node"),
            split_axis=1,
            concat_axis=1,
            tiled=True,
        ),
    )
    served = owner_lookup(received, memory, last_update, time_freq, time_phase)
    returned = lax.all_to_all(served, ("ev", "node"), split_axis=1, concat_axis=1, tiled=True)
    rows_held = received[0]
    fetched_flat = returned.reshape(2, slot_total, width + time_width)
    picked = jnp.einsum(
        "kse,ksc->kec", placement, fetched_flat, preferred_element_type=jnp.float32
    ).astype(jnp.bfloat16)
    picked_src = picked[0]
    picked_dst = picked[1]
    mem_stack = jnp.concatenate([picked_src[:, :width], picked_dst[:, :width]], axis=0)
    enc_stack = jnp.concatenate([picked_src[:, width:], picked_dst[:, width:]], axis=0)
    paired_weight = jnp.concatenate([w_msg_in[:width], w_msg_in[width : 2 * width]], axis=1)
    projected = jnp.dot(mem_stack, paired_weight, preferred_element_type=jnp.float32)
    time_term = jnp.dot(
        enc_stack, w_msg_in[2 * width : 2 * width + time_width], preferred_element_type=jnp.float32
    )
    self_term = projected[:, :hidden_width]
    other_term = projected[:, hidden_width:]
    crossed = jnp.concatenate([other_term[events_here:], other_term[:events_here]], axis=0)
    edge_both = jnp.concatenate([edge_part, edge_part], axis=0)
    hidden = jax.nn.relu(self_term + crossed + time_term + edge_both).astype(jnp.bfloat16)
    messages = jnp.dot(hidden, w_msg_out, preferred_element_type=jnp.float32).astype(jnp.bfloat16)
    outgoing = jnp.einsum(
        "kse,kec->ksc",
        placement,
        messages.reshape(2, events_here, msg_width),
        preferred_element_type=jnp.float32,
    ).astype(jnp.bfloat16)
    arrived = lax.all_to_all(
        outgoing.reshape(2, devices_all, capacity, msg_width),
        ("ev", "node"),
        split_axis=1,
        concat_axis=1,
        tiled=True,
    )
    row_flat = rows_held.reshape(-1)
    msg_flat = arrived.reshape(-1, msg_width)
    live = row_flat >= 0
    same_row = (row_flat[:, None] == row_flat[None, :]) & live[:, None] & live[None, :]
    same_mask = same_row.astype(jnp.bfloat16)
    total = jnp.dot(same_mask, msg_flat, preferred_element_type=jnp.float32)
    count = jnp.sum(same_mask.astype(jnp.float32), axis=1)
    divisor = jnp.maximum(count, 1.0)
    mean_msg = (total / divisor[:, None]).astype(jnp.bfloat16)
    safe_rows = jnp.clip(row_flat, 0, rows_count - 1)
    new_state = gru_update(mean_msg, memory[safe_rows], w_gru_in, b_gru_in, w_gru_hid)
    slot_order = jnp.arange(row_flat.shape[0], dtype=jnp.int32)
    before = slot_order[None, :] < slot_order[:, None]
    repeated = jnp.any(same_row & before, axis=1)
    first_live = live & jnp.logical_not(repeated)
    row_range = jnp.arange(rows_count, dtype=jnp.int32)
    writes = (row_range[:, None] == row_flat[None, :]) & first_live[None, :]
    write_mask = writes.astype(jnp.bfloat16)
    written = jnp.dot(write_mask, new_state, preferred_element_type=jnp.float32).astype(
        jnp.bfloat16
    )
    touched = jnp.any(writes, axis=1)
    return jnp.where(touched[:, None], written, memory)


def solution(mesh):
    in_specs = (
        P(("ev", "node"), None),
        P(("ev", "node")),
        P(("ev", "node"), None),
        P(("ev", "node")),
        P(("ev", "node")),
        P(("ev", "node"), None),
        P(("ev", "node"), None),
        P(("ev", "node")),
        P(),
        P(),
        P(),
        P(),
        P(),
        P(),
        P(),
        P(),
    )
    out_specs = P(("ev", "node"), None)
    return jax.shard_map(local, mesh=mesh, in_specs=in_specs, out_specs=out_specs, check_vma=False)
```

profile of v0, /device:TPU:1, one launch (start us, length us, event | category | flops | bytes accessed | tf_op | source)
XLA Modules:
  0.0 172.6 jit_solution(2989892138965968090)
XLA Ops:
  0.0 1.1 fusion.52
  1.1 1.1 fusion.51
  4.1 2.0 %select_reduce_fusion = (s32[2,1024]{1,0:T(2,128)S(1)}, s32[2,1024]{1,0:T(2,128)S(1)}) fusion(s32[512]{0:T(512)} %param.20, s32[2,512]{1,0:T(2,128)S(1)} %pad_add_fusion, s32[2,512]{1,0:T(2,128)S(1)} %pad_add_fusion.1), kind=kLoop, calls=%fused_computation.22 | loop fusion | flops 5238784 | bytes 26624 | tf_op jit(solution)/shard_map/reduce_sum | solution.py:81
  6.3 0.8 copy.54
  7.0 11.5 %all-to-all-start = ((s32[2,128,8]{2,0,1:T(2,128)}), s32[2,128,8]{2,0,1:T(2,128)S(1)}, u32[]{:S(2)}, u32[]{:S(2)}) async-start(s32[2,128,8]{2,0,1:T(2,128)} %copy.54), calls=%async_computation | async-start | bytes 262144 | tf_op jit(solution)/shard_map/all_to_all | solution.py:90
  18.5 2.3 %convolution_add_fusion.1 = f32[512,512]{1,0:T(8,128)} fusion(bf16[512,256]{1,0:T(8,128)(2,1)} %param.21, f32[512]{0:T(512)} %param.27, bf16[896,512]{1,0:T(8,128)(2,1)} %param.26), kind=kOutput, calls=%fused_computation.59 | convolution fusion | flops 134479872 | bytes 1574912 | tf_op jit(solution)/shard_map/dot_general | solution.py:85
  20.8 1.9 %fusion.83 = (bf16[256,512]{1,0:T(8,128)(2,1)}, bf16[256,512]{1,0:T(8,128)(2,1)}) fusion(bf16[896,512]{1,0:T(8,128)(2,1)} %param.26), kind=kLoop, calls=%fused_computation.111 | loop fusion | bytes 1048576 | tf_op jit(solution)/shard_map/slice | solution.py:112
  23.6 4.8 %all-to-all-done = s32[2,128,8]{2,0,1:T(2,128)S(1)} async-done(((s32[2,128,8]{2,0,1:T(2,128)}), s32[2,128,8]{2,0,1:T(2,128)S(1)}, u32[]{:S(2)}, u32[]{:S(2)}) %all-to-all-start) | async-done | bytes 8224 | tf_op jit(solution)/shard_map/all_to_all | solution.py:90
  28.4 5.0 %all-to-all-start.1 = ((s32[2,128,8]{2,0,1:T(2,128)}), s32[2,128,8]{2,0,1:T(2,128)S(1)}, u32[]{:S(2)}, u32[]{:S(2)}) async-start(s32[2,128,8]{2,0,1:T(2,128)} %copy.57), calls=%async_computation.1 | async-start | bytes 262144 | tf_op jit(solution)/shard_map/all_to_all | solution.py:93
  33.8 11.8 %gather_fusion.1 = s32[2048]{0:T(1024)S(1)} fusion(s32[4096]{0:T(1024)S(1)} %copy-done.1, s32[2048]{0:T(1024)S(1)} %broadcast_clamp_fusion.2), kind=kCustom, calls=%fused_computation.1 | custom fusion | bytes 24576 | tf_op jit(solution)/shard_map/gather | solution.py:38
  45.8 0.8 copy.60
  47.4 9.0 %gather_fusion = bf16[2048,256]{1,0:T(8,128)(2,1)} fusion(bf16[4096,256]{1,0:T(8,128)(2,1)S(1)} %copy-done.2, s32[2048]{0:T(1024)S(1)} %broadcast_clamp_fusion.2), kind=kCustom, calls=%fused_computation | custom fusion | bytes 2105344 | tf_op jit(solution)/shard_map/gather | solution.py:37
  56.4 8.5 %gather_fusion.2 = bf16[2048,256]{1,0:T(8,128)(2,1)S(1)} fusion(bf16[4096,256]{1,0:T(8,128)(2,1)S(1)} %copy-done.2, s32[2048]{0:T(1024)} %broadcast_clamp_fusion.1), kind=kCustom, calls=%fused_computation.2 | custom fusion | bytes 2105344 | tf_op jit(solution)/shard_map/gather | solution.py:146
  64.9 4.6 %cosine_convert_fusion = bf16[2,128,8,128]{3,2,0,1:T(8,128)(2,1)S(1)} fusion(f32[128]{0:T(128)} %param.25, f32[128]{0:T(128)} %param.24, f32[2,128,8]{2,0,1:T(2,128)} %copy.60), kind=kLoop, calls=%fused_computation.68 | loop fusion | flops 786432 | bytes 533504 | tf_op jit(solution)/shard_map/convert_element_type | solution.py:9
  69.5 2.5 %pad_maximum_fusion = bf16[2,128,8,384]{3,2,0,1:T(8,128)(2,1)} fusion(bf16[2,128,8,128]{3,2,0,1:T(8,128)(2,1)S(1)} %cosine_convert_fusion, bf16[2,128,8,256]{3,2,1,0:T(8,128)(2,1)} %bitcast.32), kind=kLoop, calls=%fused_computation.53 | loop fusion | flops 3145728 | bytes 3145728 | tf_op jit(solution)/shard_map/concatenate | solution.py:39
  72.0 10.2 %all-to-all-start.2 = ((bf16[2,128,8,384]{3,2,0,1:T(8,128)(2,1)}), bf16[2,128,8,384]{3,2,0,1:T(8,128)(2,1)}, u32[]{:S(2)}, u32[]{:S(2)}) async-start(bf16[2,128,8,384]{3,2,0,1:T(8,128)(2,1)} %pad_maximum_fusion), calls=%async_computation.2 | async-start | bytes 3145728 | tf_op jit(solution)/shard_map/all_to_all | solution.py:102
  82.2 6.6 %fusion.6 = pred[2048]{0:T(1024)(128)(4,1)S(1)} fusion(s32[2048]{0:T(1024)S(1)} %eq.83, pred[2048]{0:T(1024)(128)(4,1)S(1)} %broadcast_compare_fusion), kind=kLoop, calls=%fused_computation.11 | loop fusion | flops 25163776 | bytes 12288 | tf_op jit(solution)/shard_map/reduce_or | solution.py:149
  89.4 4.3 %convert_reduce_fusion = f32[2048]{0:T(1024)S(1)} fusion(s32[2048]{0:T(1024)S(1)} %eq.83, pred[2048]{0:T(1024)(128)(4,1)S(1)} %broadcast_compare_fusion), kind=kLoop, calls=%fused_computation.7 | loop fusion | flops 25163776 | bytes 18432 | tf_op jit(solution)/shard_map/reduce_sum | solution.py:142
  94.2 12.6 %all-to-all-done.2 = bf16[2,128,8,384]{3,2,0,1:T(8,128)(2,1)} async-done(((bf16[2,128,8,384]{3,2,0,1:T(8,128)(2,1)}), bf16[2,128,8,384]{3,2,0,1:T(8,128)(2,1)}, u32[]{:S(2)}, u32[]{:S(2)}) %all-to-all-start.2) | async-done | bytes 1572896 | tf_op jit(solution)/shard_map/all_to_all | solution.py:102
  106.8 2.8 %fusion.45 = bf16[2,512,384]{2,1,0:T(8,128)(2,1)S(1)} fusion(bf16[2,128,8,384]{3,2,0,1:T(8,128)(2,1)} %all-to-all-done.2, s32[2,512]{1,0:T(2,128)S(1)} %pad_add_fusion), kind=kOutput, calls=%fused_computation.57 | convolution fusion | flops 806748160 | bytes 2363392 | tf_op jit(solution)/shard_map/kse,ksc->kec/dot_general | solution.py:105
  111.8 1.9 %copy-done.3 = f32[1024,1024]{1,0:T(8,128)} copy-done((f32[1024,1024]{1,0:T(8,128)}, f32[1024,1024]{1,0:T(8,128)S(1)}, u32[]{:S(2)}) %copy-start.3) | copy-done | bytes 4194328
  113.7 1.6 fusion.82
  115.3 4.6 %fusion.50 = bf16[1024,256]{1,0:T(8,128)(2,1)} fusion(bf16[512,256]{1,0:T(8,128)(2,1)} %param.28, f32[1024,1024]{1,0:T(8,128)} %copy-done.3, f32[512,512]{1,0:T(8,128)} %get-tuple-element.8, f32[512,512]{1,0:T(8,128)} %get-tuple-element.7, f32[512,512]{1,0:T(8,128)} %convolution_add_fusion.1, bf16[512,128]{1,0:T(8,128)(2,1)} %slice.93, ...), kind=kOutput, calls=%fused_computation.61 | convolution fusion | flops 407109632 | bytes 6422528 | tf_op jit(solution)/shard_map/dot_general | solution.py:122
  119.9 1.8 %fusion.48 = bf16[2,128,8,256]{3,2,1,0:T(8,128)(2,1)S(1)} fusion(bf16[2,512,256]{2,1,0:T(8,128)(2,1)} %bitcast.41, s32[2,512]{1,0:T(2,128)S(1)} %pad_add_fusion), kind=kOutput, calls=%fused_computation.58 | convolution fusion | flops 538443776 | bytes 1576960 | tf_op jit(solution)/shard_map/kse,kec->ksc/dot_general | solution.py:123
  121.8 1.1 copy.64
  122.8 4.9 %all-to-all-start.3 = ((bf16[2,128,8,256]{3,2,0,1:T(8,128)(2,1)}), bf16[2,128,8,256]{3,2,0,1:T(8,128)(2,1)}, u32[]{:S(2)}, u32[]{:S(2)}) async-start(bf16[2,128,8,256]{3,2,0,1:T(8,128)(2,1)} %copy.64), calls=%async_computation.3 | async-start | bytes 2097152 | tf_op jit(solution)/shard_map/all_to_all | solution.py:129
  127.8 3.6 %fusion.84 = f32[2048,768]{1,0:T(8,128)} fusion(bf16[2048,256]{1,0:T(8,128)(2,1)S(1)} %gather_fusion.2, bf16[256,768]{1,0:T(8,128)(2,1)S(1)} %copy-done), kind=kOutput, calls=%fused_computation.112 | convolution fusion | flops 805306368 | bytes 7733248 | tf_op jit(solution)/shard_map/dot_general | solution.py:15
  131.4 5.1 %fusion.3 = pred[4096]{0:T(1024)(128)(4,1)} fusion(s32[2048]{0:T(1024)S(1)} %eq.83, pred[2048]{0:T(1024)(128)(4,1)S(1)} %copy-done.8), kind=kLoop, calls=%fused_computation.6 | loop fusion | flops 25161728 | bytes 14336 | tf_op jit(solution)/shard_map/reduce_or | solution.py:157
  136.5 10.4 %all-to-all-done.3 = bf16[2,128,8,256]{3,2,0,1:T(8,128)(2,1)} async-done(((bf16[2,128,8,256]{3,2,0,1:T(8,128)(2,1)}), bf16[2,128,8,256]{3,2,0,1:T(8,128)(2,1)}, u32[]{:S(2)}, u32[]{:S(2)}) %all-to-all-start.3) | async-done | bytes 1048608 | tf_op jit(solution)/shard_map/all_to_all | solution.py:129
  146.9 2.3 %copy.65 = bf16[2,128,8,256]{3,2,1,0:T(8,128)(2,1)} copy(bf16[2,128,8,256]{3,2,0,1:T(8,128)(2,1)} %all-to-all-done.3) | data formatting | bytes 2097152 | tf_op jit(solution)/shard_map/all_to_all | solution.py:129
  149.2 8.4 %convolution_add_fusion = f32[2048,768]{1,0:T(8,128)} fusion(bf16[256,768]{1,0:T(8,128)(2,1)} %param.29, f32[768]{0:T(1024)} %param.30, bf16[2048,256]{1,0:T(8,128)(2,1)} %bitcast.33, s32[2048]{0:T(1024)S(1)} %eq.83, pred[2048]{0:T(1024)(128)(4,1)} %copy-done.7, f32[2048]{0:T(1024)S(1)} %copy-done.6), kind=kOutput, calls=%fused_computation.28 | convolution fusion | flops 2967994368 | bytes 7754752 | tf_op jit(solution)/shard_map/dot_general | solution.py:14
  157.5 15.1 %fusion.17 = bf16[4096,256]{1,0:T(8,128)(2,1)} fusion(bf16[4096,256]{1,0:T(8,128)(2,1)S(1)} %copy-done.2, s32[2048]{0:T(1024)S(1)} %eq.83, pred[2048]{0:T(1024)(128)(4,1)} %not_and_fusion, pred[4096]{0:T(1024)(128)(4,1)} %fusion.3, f32[2048,768]{1,0:T(8,128)} %fusion.84, f32[2048,768]{1,0:T(8,128)} %convolution_add_fusion, ...), kind=kOutput, calls=%fused_computation.21 | convolution fusion | flops 4322230272 | bytes 17840128 | tf_op jit(solution)/shard_map/dot_general | solution.py:154
  (51 shorter events, 7.6 us)
Async XLA Ops:
  0.0 127.7 %copy-start = (bf16[256,768]{1,0:T(8,128)(2,1)S(1)}, bf16[256,768]{1,0:T(8,128)(2,1)}, u32[]{:S(2)}) copy-start(bf16[256,768]{1,0:T(8,128)(2,1)} %param.31) | copy-start | bytes 1179652
  0.0 33.8 %copy-start.1 = (s32[4096]{0:T(1024)S(1)}, s32[4096]{0:T(1024)}, u32[]{:S(2)}) copy-start(s32[4096]{0:T(1024)} %param.23) | copy-start | bytes 49156
  7.0 21.3 %all-to-all-start = ((s32[2,128,8]{2,0,1:T(2,128)}), s32[2,128,8]{2,0,1:T(2,128)S(1)}, u32[]{:S(2)}, u32[]{:S(2)}) async-start(s32[2,128,8]{2,0,1:T(2,128)} %copy.54), calls=%async_computation | async-start | bytes 262144 | tf_op jit(solution)/shard_map/all_to_all | solution.py:90
  28.4 17.4 %all-to-all-start.1 = ((s32[2,128,8]{2,0,1:T(2,128)}), s32[2,128,8]{2,0,1:T(2,128)S(1)}, u32[]{:S(2)}, u32[]{:S(2)}) async-start(s32[2,128,8]{2,0,1:T(2,128)} %copy.57), calls=%async_computation.1 | async-start | bytes 262144 | tf_op jit(solution)/shard_map/all_to_all | solution.py:93
  33.8 55.6 %copy-start.7 = (pred[2048]{0:T(1024)(128)(4,1)}, pred[2048]{0:T(1024)(128)(4,1)S(1)}, u32[]{:S(2)}) copy-start(pred[2048]{0:T(1024)(128)(4,1)S(1)} %broadcast_compare_fusion) | copy-start | bytes 6148
  33.8 13.6 %copy-start.2 = (bf16[4096,256]{1,0:T(8,128)(2,1)S(1)}, bf16[4096,256]{1,0:T(8,128)(2,1)}, u32[]{:S(2)}) copy-start(bf16[4096,256]{1,0:T(8,128)(2,1)} %param.22) | copy-start | bytes 6291460
  72.0 34.8 %all-to-all-start.2 = ((bf16[2,128,8,384]{3,2,0,1:T(8,128)(2,1)}), bf16[2,128,8,384]{3,2,0,1:T(8,128)(2,1)}, u32[]{:S(2)}, u32[]{:S(2)}) async-start(bf16[2,128,8,384]{3,2,0,1:T(8,128)(2,1)} %pad_maximum_fusion), calls=%async_computation.2 | async-start | bytes 3145728 | tf_op jit(solution)/shard_map/all_to_all | solution.py:102
  106.8 4.2 %copy-start.4 = (bf16[256,512]{1,0:T(8,128)(2,1)S(1)}, bf16[256,512]{1,0:T(8,128)(2,1)}, u32[]{:S(2)}) copy-start(bf16[256,512]{1,0:T(8,128)(2,1)} %get-tuple-element.9) | copy-start | bytes 786436
  106.8 4.2 %copy-start.5 = (bf16[256,512]{1,0:T(8,128)(2,1)S(1)}, bf16[256,512]{1,0:T(8,128)(2,1)}, u32[]{:S(2)}) copy-start(bf16[256,512]{1,0:T(8,128)(2,1)} %get-tuple-element.10) | copy-start | bytes 786436
  111.8 1.9 %copy-start.3 = (f32[1024,1024]{1,0:T(8,128)}, f32[1024,1024]{1,0:T(8,128)S(1)}, u32[]{:S(2)}) copy-start(f32[1024,1024]{1,0:T(8,128)S(1)} %fusion.56) | copy-start | bytes 12582916
  122.8 24.1 %all-to-all-start.3 = ((bf16[2,128,8,256]{3,2,0,1:T(8,128)(2,1)}), bf16[2,128,8,256]{3,2,0,1:T(8,128)(2,1)}, u32[]{:S(2)}, u32[]{:S(2)}) async-start(bf16[2,128,8,256]{3,2,0,1:T(8,128)(2,1)} %copy.64), calls=%async_computation.3 | async-start | bytes 2097152 | tf_op jit(solution)/shard_map/all_to_all | solution.py:129
  127.7 3.7 %copy-start.8 = (pred[2048]{0:T(1024)(128)(4,1)S(1)}, pred[2048]{0:T(1024)(128)(4,1)}, u32[]{:S(2)}) copy-start(pred[2048]{0:T(1024)(128)(4,1)} %not_and_fusion) | copy-start | bytes 6148
  127.7 21.4 %copy-start.6 = (f32[2048]{0:T(1024)S(1)}, f32[2048]{0:T(1024)}, u32[]{:S(2)}) copy-start(f32[2048]{0:T(1024)} %broadcast_maximum_fusion) | copy-start | bytes 24580
where the time goes:
time: 173 us
  local copies, waits for them, and re-layouts  42.6 us (25%)
  matrix products  41.5 us (24%)
  starting transfers between devices  31.5 us (18%)
  other arithmetic  29 us (17%)
  waiting for transfers between devices  27.8 us (16%)
    dot_general x1, matrix products, local(): jnp.dot(write_mask, new_state, preferred_element_type=jnp.float32)  15.1 us
    all_to_all x1, waiting for transfers between devices, local(): lax.all_to_all(served, ('ev', 'node'), split_axis=1, concat_axis=1, tiled...  12.6 us
    gather x3, local copies, waits for them, and re-layouts, owner_lookup(): last_update[safe_rows]  11.9 us
    all_to_all x1, starting transfers between devices, local(): lax.all_to_all(row_request.reshape(flat_shape), ('ev', 'node'), split_axi...  11.5 us
    all_to_all x1, waiting for transfers between devices, local(): lax.all_to_all(outgoing.reshape(2, devices_all, capacity, msg_width), ('e...  10.4 us
    all_to_all x1, starting transfers between devices, local(): lax.all_to_all(served, ('ev', 'node'), split_axis=1, concat_axis=1, tiled...  10.2 us
    gather x1, local copies, waits for them, and re-layouts, owner_lookup(): mem_rows = memory[safe_rows]  9.04 us
    gather x1, local copies, waits for them, and re-layouts, local(): memory[safe_rows]  8.47 us
  transfers between devices with their start and end apart: 4, of which 3 were waited for; matrix products, arithmetic and copies ran while one was open for 22% of the time, Pallas kernels for 0%

commit v1 on v0

--- a/solution.py
+++ b/solution.py
@@ -31,12 +31,23 @@
 
 
 def owner_lookup(request_pair, memory, last_update, time_freq, time_phase):
-    row_request = request_pair[0]
-    time_request = request_pair[1]
-    safe_rows = jnp.clip(row_request, 0, memory.shape[0] - 1)
-    mem_rows = memory[safe_rows]
-    encoded = encode(time_request - last_update[safe_rows], time_freq, time_phase)
-    return jnp.concatenate([mem_rows, encoded], axis=-1)
+    row_request = request_pair[0].reshape(-1)
+    time_request = request_pair[1].reshape(-1)
+    rows_count = memory.shape[0]
+    row_range = jnp.arange(rows_count, dtype=jnp.int32)
+    select = (row_request[:, None] == row_range[None, :]).astype(jnp.bfloat16)
+    high = (last_update // 64).astype(jnp.bfloat16)
+    low = (last_update % 64).astype(jnp.bfloat16)
+    table = jnp.concatenate([memory, high[:, None], low[:, None]], axis=1)
+    fetched = jnp.dot(select, table, preferred_element_type=jnp.float32)
+    mem_rows = fetched[:, : memory.shape[1]].astype(jnp.bfloat16)
+    stamp = (
+        fetched[:, memory.shape[1]].astype(jnp.int32) * 64
+        + fetched[:, memory.shape[1] + 1].astype(jnp.int32)
+    )
+    encoded = encode(time_request - stamp, time_freq, time_phase)
+    served = jnp.concatenate([mem_rows, encoded], axis=-1)
+    return served.reshape(request_pair.shape[1:] + (served.shape[-1],))
 
 
 def local(
@@ -85,19 +96,8 @@
         jnp.dot(edge_feat, w_msg_in[2 * width + time_width :], preferred_element_type=jnp.float32)
         + b_msg
     )
-    flat_shape = (2, devices_all, capacity)
-    received = (
-        lax.all_to_all(
-            row_request.reshape(flat_shape), ("ev", "node"), split_axis=1, concat_axis=1, tiled=True
-        ),
-        lax.all_to_all(
-            time_request.reshape(flat_shape),
-            ("ev", "node"),
-            split_axis=1,
-            concat_axis=1,
-            tiled=True,
-        ),
-    )
+    request = jnp.stack([row_request, time_request]).reshape((2, 2, devices_all, capacity))
+    received = lax.all_to_all(request, ("ev", "node"), split_axis=2, concat_axis=2, tiled=True)
     served = owner_lookup(received, memory, last_update, time_freq, time_phase)
     returned = lax.all_to_all(served, ("ev", "node"), split_axis=1, concat_axis=1, tiled=True)
     rows_held = received[0]
@@ -135,27 +135,14 @@
     )
     row_flat = rows_held.reshape(-1)
     msg_flat = arrived.reshape(-1, msg_width)
-    live = row_flat >= 0
-    same_row = (row_flat[:, None] == row_flat[None, :]) & live[:, None] & live[None, :]
-    same_mask = same_row.astype(jnp.bfloat16)
-    total = jnp.dot(same_mask, msg_flat, preferred_element_type=jnp.float32)
-    count = jnp.sum(same_mask.astype(jnp.float32), axis=1)
+    row_range = jnp.arange(rows_count, dtype=jnp.int32)
+    hits = row_range[:, None] == row_flat[None, :]
+    total = jnp.dot(hits.astype(jnp.bfloat16), msg_flat, preferred_element_type=jnp.float32)
+    count = jnp.sum(hits.astype(jnp.float32), axis=1)
     divisor = jnp.maximum(count, 1.0)
     mean_msg = (total / divisor[:, None]).astype(jnp.bfloat16)
-    safe_rows = jnp.clip(row_flat, 0, rows_count - 1)
-    new_state = gru_update(mean_msg, memory[safe_rows], w_gru_in, b_gru_in, w_gru_hid)
-    slot_order = jnp.arange(row_flat.shape[0], dtype=jnp.int32)
-    before = slot_order[None, :] < slot_order[:, None]
-    repeated = jnp.any(same_row & before, axis=1)
-    first_live = live & jnp.logical_not(repeated)
-    row_range = jnp.arange(rows_count, dtype=jnp.int32)
-    writes = (row_range[:, None] == row_flat[None, :]) & first_live[None, :]
-    write_mask = writes.astype(jnp.bfloat16)
-    written = jnp.dot(write_mask, new_state, preferred_element_type=jnp.float32).astype(
-        jnp.bfloat16
-    )
-    touched = jnp.any(writes, axis=1)
-    return jnp.where(touched[:, None], written, memory)
+    new_state = gru_update(mean_msg, memory, w_gru_in, b_gru_in, w_gru_hid)
+    return jnp.where((count > 0)[:, None], new_state, memory)
 
 
 def solution(mesh):

time: 173 us -> 151 us (0.87)
  local copies, waits for them, and re-layouts: 42.6 us -> 23.2 us
  waiting for transfers between devices: 27.8 us -> 39.6 us
  starting transfers between devices: 31.5 us -> 20.9 us
  other arithmetic: 29 us -> 24.9 us
    gather x5 -> x0, local copies, waits for them, and re-layouts: 29.4 us -> none  [the longest x3 11.9 us: owner_lookup(): last_update[safe_rows]]
    reduce_or x2 -> x0, other arithmetic: 11.7 us -> none  [the longest x1 6.58 us: local(): repeated = jnp.any(same_row & before, axis=1)]
    select_n x3 -> x2, other arithmetic: 0.17 us -> 11.1 us  [the longest x1 11.1 us: local(): return jnp.where((count > 0)[:, None], new_state, memory)]
    all_to_all x1, waiting for transfers between devices: 12.6 us -> 22.6 us  [local(): lax.all_to_all(served, ('ev', 'node'), split_axis=1, concat_axis=1, tiled...]
    dot_general x1, matrix products: 15.1 us -> 9.11 us  [owner_lookup(): fetched = jnp.dot(select, table, preferred_element_type=jnp.float32)]
    all_to_all x1, starting transfers between devices: 10.2 us -> 5.04 us  [local(): lax.all_to_all(served, ('ev', 'node'), split_axis=1, concat_axis=1, tiled...]
    dot_general x1, matrix products: 8.38 us -> 13.5 us  [gru_update(): jnp.dot(mean_msg, w_gru_in, preferred_element_type=jnp.float32) + b_gru_in]
    all_to_all x2 -> x1, starting transfers between devices: 16.4 us -> 12 us  [local(): lax.all_to_all(request, ('ev', 'node'), split_axis=2, concat_axis=2, tile...]
  transfers between devices with their start and end apart: 4 -> 3, of which waited for: 3 -> 3; matrix products, arithmetic and copies ran while one was open for 22% -> 10% of each run, Pallas kernels for 0% -> 0%
where the time goes in v1:
time: 151 us
  matrix products  41.8 us (28%)
  waiting for transfers between devices  39.6 us (26%)
  other arithmetic  24.9 us (16%)
  local copies, waits for them, and re-layouts  23.2 us (15%)
  starting transfers between devices  20.9 us (14%)
    all_to_all x1, waiting for transfers between devices, local(): lax.all_to_all(served, ('ev', 'node'), split_axis=1, concat_axis=1, tiled...  22.6 us
    dot_general x1, matrix products, gru_update(): jnp.dot(mean_msg, w_gru_in, preferred_element_type=jnp.float32) + b_gru_in  13.5 us
    all_to_all x1, starting transfers between devices, local(): lax.all_to_all(request, ('ev', 'node'), split_axis=2, concat_axis=2, tile...  12 us
    select_n x1, other arithmetic, local(): return jnp.where((count > 0)[:, None], new_state, memory)  11.1 us
    all_to_all x1, waiting for transfers between devices, local(): lax.all_to_all(outgoing.reshape(2, devices_all, capacity, msg_width), ('e...  9.17 us
    dot_general x1, matrix products, owner_lookup(): fetched = jnp.dot(select, table, preferred_element_type=jnp.float32)  9.11 us
    all_to_all x1, waiting for transfers between devices, local(): lax.all_to_all(request, ('ev', 'node'), split_axis=2, concat_axis=2, tile...  7.83 us
    dot_general x1, matrix products, gru_update(): state_part = jnp.dot(state, w_gru_hid, preferred_element_type=jnp.float32)  6.33 us
  transfers between devices with their start and end apart: 3, of which 3 were waited for; matrix products, arithmetic and copies ran while one was open for 10% of the time, Pallas kernels for 0%

profile of v1, /device:TPU:1, one launch (start us, length us, event | category | flops | bytes accessed | tf_op | source)
XLA Modules:
  0.0 150.6 jit_solution(11289886161346799551)
XLA Ops:
  0.0 1.2 fusion.45
  1.2 1.1 fusion.44
  4.2 2.0 %select_reduce_fusion.1 = (s32[2,1024]{1,0:T(2,128)S(1)}, s32[2,1024]{1,0:T(2,128)S(1)}) fusion(s32[2,512]{1,0:T(2,128)S(1)} %pad_add_fusion.2, s32[2,512]{1,0:T(2,128)S(1)} %pad_add_fusion.1, s32[512]{0:T(512)} %param.20), kind=kLoop, calls=%fused_computation.27 | loop fusion | flops 5238784 | bytes 26624 | tf_op jit(solution)/shard_map/reduce_sum | solution.py:91
  6.5 0.9 copy.48
  7.4 12.0 %all-to-all-start = ((s32[2,2,128,8]{3,1,0,2:T(2,128)}), s32[2,2,128,8]{3,1,0,2:T(2,128)}, u32[]{:S(2)}, u32[]{:S(2)}) async-start(s32[2,2,128,8]{3,1,0,2:T(2,128)} %copy.48), calls=%async_computation | async-start | bytes 524288 | tf_op jit(solution)/shard_map/all_to_all | solution.py:100
  20.7 1.6 %broadcast_in_dim.71 = bf16[4096,1]{1,0:T(8,128)(2,1)} reshape(bf16[4096]{0:T(1024)(128)(2,1)S(1)} %get-tuple-element.16) | data formatting | bytes 16384 | tf_op jit(solution)/shard_map/broadcast_in_dim | solution.py:41
  22.3 7.8 %all-to-all-done = s32[2,2,128,8]{3,1,0,2:T(2,128)} async-done(((s32[2,2,128,8]{3,1,0,2:T(2,128)}), s32[2,2,128,8]{3,1,0,2:T(2,128)}, u32[]{:S(2)}, u32[]{:S(2)}) %all-to-all-start) | async-done | bytes 16416 | tf_op jit(solution)/shard_map/all_to_all | solution.py:100
  30.1 1.6 %fusion.83 = (s32[1,2,128,8]{3,1,0,2:T(2,128)S(1)}, s32[1,2,128,8]{3,1,0,2:T(2,128)}) fusion(s32[2,2,128,8]{3,1,0,2:T(2,128)} %all-to-all-done), kind=kLoop, calls=%fused_computation.115 | loop fusion | bytes 32768 | tf_op jit(solution)/shard_map/slice | solution.py:103
  32.4 1.6 %eq.85 = s32[2048]{0:T(1024)} reshape(s32[1,2,128,8]{3,2,1,0:T(8,128)} %copy.49) | data formatting | bytes 16384 | tf_op jit(solution)/shard_map/eq | solution.py:139
  34.0 1.6 %copy.52 = s32[1,2,128,8]{3,2,1,0:T(8,128)} copy(s32[1,2,128,8]{3,1,0,2:T(2,128)} %get-tuple-element.14) | data formatting | bytes 16384 | tf_op jit(solution)/shard_map/slice | solution.py:35
  35.6 1.0 reshape_squeeze.3
  36.7 9.1 %fusion.1 = f32[2048,258]{0,1:T(8,128)S(1)} fusion(s32[2048]{0:T(1024)} %eq.85, bf16[4096,1]{1,0:T(8,128)(2,1)} %broadcast_in_dim.71, bf16[4096,1]{1,0:T(8,128)(2,1)S(1)} %broadcast_in_dim.70, bf16[4096,256]{1,0:T(8,128)(2,1)S(1)} %copy-done.2), kind=kOutput, calls=%fused_computation.4 | convolution fusion | flops 4343250944 | bytes 4235264 | tf_op jit(solution)/shard_map/dot_general | solution.py:42
  46.0 3.7 %cosine_convert_fusion = bf16[2048,128]{0,1:T(8,128)(2,1)S(1)} fusion(f32[128]{0:T(128)S(1)} %copy-done.9, f32[128]{0:T(128)S(1)} %copy-done.10, f32[2048]{0:T(1024)S(1)} %bitcast.38), kind=kLoop, calls=%fused_computation.61 | loop fusion | flops 786432 | bytes 533504 | tf_op jit(solution)/shard_map/convert_element_type | solution.py:9
  49.7 1.2 pad_maximum_fusion
  51.0 2.7 %copy.53 = bf16[2048,384]{1,0:T(8,128)(2,1)} copy(bf16[2048,384]{0,1:T(8,128)(2,1)} %pad_maximum_fusion) | data formatting | bytes 3145728 | tf_op jit(solution)/shard_map/concatenate | solution.py:49
  53.7 2.7 %copy.54 = bf16[2,128,8,384]{3,2,0,1:T(8,128)(2,1)} copy(bf16[2,128,8,384]{3,2,1,0:T(8,128)(2,1)} %bitcast.36) | data formatting | bytes 3145728 | tf_op jit(solution)/shard_map/reshape | solution.py:50
  56.4 5.0 %all-to-all-start.1 = ((bf16[2,128,8,384]{3,2,0,1:T(8,128)(2,1)}), bf16[2,128,8,384]{3,2,0,1:T(8,128)(2,1)}, u32[]{:S(2)}, u32[]{:S(2)}) async-start(bf16[2,128,8,384]{3,2,0,1:T(8,128)(2,1)} %copy.54), calls=%async_computation.1 | async-start | bytes 3145728 | tf_op jit(solution)/shard_map/all_to_all | solution.py:102
  62.3 1.3 convolution_add_fusion.1
  63.6 22.6 %all-to-all-done.1 = bf16[2,128,8,384]{3,2,0,1:T(8,128)(2,1)} async-done(((bf16[2,128,8,384]{3,2,0,1:T(8,128)(2,1)}), bf16[2,128,8,384]{3,2,0,1:T(8,128)(2,1)}, u32[]{:S(2)}, u32[]{:S(2)}) %all-to-all-start.1) | async-done | bytes 1572896 | tf_op jit(solution)/shard_map/all_to_all | solution.py:102
  86.2 2.8 %fusion.38 = bf16[2,512,384]{2,1,0:T(8,128)(2,1)S(1)} fusion(bf16[2,128,8,384]{3,2,0,1:T(8,128)(2,1)} %all-to-all-done.1, s32[2,512]{1,0:T(2,128)S(1)} %pad_add_fusion.1), kind=kOutput, calls=%fused_computation.51 | convolution fusion | flops 806748160 | bytes 2363392 | tf_op jit(solution)/shard_map/kse,ksc->kec/dot_general | solution.py:105
  91.2 1.9 %copy-done.1 = f32[1024,1024]{1,0:T(8,128)} copy-done((f32[1024,1024]{1,0:T(8,128)}, f32[1024,1024]{1,0:T(8,128)S(1)}, u32[]{:S(2)}) %copy-start.1) | copy-done | bytes 4194328
  93.1 1.5 %fusion.81 = (f32[512,512]{1,0:T(8,128)}, f32[512,512]{1,0:T(8,128)}) fusion(f32[1024,1024]{1,0:T(8,128)S(1)} %fusion.47), kind=kLoop, calls=%fused_computation.113 | loop fusion | bytes 4194304 | tf_op jit(solution)/shard_map/slice | solution.py:119
  94.6 4.0 %fusion.43 = bf16[1024,256]{1,0:T(8,128)(2,1)} fusion(bf16[512,256]{1,0:T(8,128)(2,1)} %param.28, f32[1024,1024]{1,0:T(8,128)} %copy-done.1, f32[512,512]{1,0:T(8,128)} %get-tuple-element.8, f32[512,512]{1,0:T(8,128)} %get-tuple-element.7, f32[512,512]{1,0:T(8,128)S(1)} %convolution_add_fusion.1, bf16[512,128]{1,0:T(8,128)(2,1)} %slice.114, ...), kind=kOutput, calls=%fused_computation.55 | convolution fusion | flops 407109632 | bytes 6422528 | tf_op jit(solution)/shard_map/dot_general | solution.py:122
  98.7 1.8 %fusion.41 = bf16[2,128,8,256]{3,2,1,0:T(8,128)(2,1)S(1)} fusion(bf16[2,512,256]{2,1,0:T(8,128)(2,1)} %bitcast.45, s32[2,512]{1,0:T(2,128)S(1)} %pad_add_fusion.1), kind=kOutput, calls=%fused_computation.52 | convolution fusion | flops 538443776 | bytes 1576960 | tf_op jit(solution)/shard_map/kse,kec->ksc/dot_general | solution.py:123
  100.5 1.1 copy.57
  101.6 3.9 %all-to-all-start.2 = ((bf16[2,128,8,256]{3,2,0,1:T(8,128)(2,1)}), bf16[2,128,8,256]{3,2,0,1:T(8,128)(2,1)S(1)}, u32[]{:S(2)}, u32[]{:S(2)}) async-start(bf16[2,128,8,256]{3,2,0,1:T(8,128)(2,1)} %copy.57), calls=%async_computation.2 | async-start | bytes 2097152 | tf_op jit(solution)/shard_map/all_to_all | solution.py:129
  105.4 6.3 %fusion.84 = f32[4096,768]{1,0:T(8,128)} fusion(bf16[4096,256]{1,0:T(8,128)(2,1)S(1)} %copy-done.2, bf16[256,768]{1,0:T(8,128)(2,1)S(1)} %copy-done), kind=kOutput, calls=%fused_computation.116 | convolution fusion | flops 1610612736 | bytes 15073280 | tf_op jit(solution)/shard_map/dot_general | solution.py:15
  111.8 3.4 %convert_reduce_fusion = f32[4096]{0:T(1024)S(1)} fusion(s32[2048]{0:T(1024)S(1)} %copy-done.7), kind=kLoop, calls=%fused_computation.1 | loop fusion | flops 25161728 | bytes 24576 | tf_op jit(solution)/shard_map/reduce_sum | solution.py:141
  115.8 9.2 %all-to-all-done.2 = bf16[2,128,8,256]{3,2,0,1:T(8,128)(2,1)S(1)} async-done(((bf16[2,128,8,256]{3,2,0,1:T(8,128)(2,1)}), bf16[2,128,8,256]{3,2,0,1:T(8,128)(2,1)S(1)}, u32[]{:S(2)}, u32[]{:S(2)}) %all-to-all-start.2) | async-done | bytes 1048608 | tf_op jit(solution)/shard_map/all_to_all | solution.py:129
  124.9 1.0 copy.58
  126.0 13.5 %convolution_add_fusion = f32[4096,768]{1,0:T(8,128)} fusion(bf16[256,768]{1,0:T(8,128)(2,1)} %param.29, f32[768]{0:T(1024)} %param.30, bf16[2048,256]{1,0:T(8,128)(2,1)} %bitcast.37, s32[2048]{0:T(1024)} %eq.85, f32[4096]{0:T(1024)S(1)} %broadcast_maximum_fusion), kind=kOutput, calls=%fused_computation.7 | convolution fusion | flops 5919211520 | bytes 14052352 | tf_op jit(solution)/shard_map/dot_general | solution.py:14
  139.5 11.1 %fusion.27 = bf16[4096,256]{1,0:T(8,128)(2,1)} fusion(bf16[4096,256]{1,0:T(8,128)(2,1)S(1)} %copy-done.2, f32[4096,768]{1,0:T(8,128)} %fusion.84, f32[4096,768]{1,0:T(8,128)} %convolution_add_fusion, pred[4096]{0:T(1024)(128)(4,1)S(1)} %copy-done.6), kind=kLoop, calls=%fused_computation.37 | loop fusion | flops 17825792 | bytes 29364224 | tf_op jit(solution)/shard_map/jit(_where)/select_n | solution.py:145
  (45 shorter events, 8.0 us)
Async XLA Ops:
  0.0 105.4 %copy-start = (bf16[256,768]{1,0:T(8,128)(2,1)S(1)}, bf16[256,768]{1,0:T(8,128)(2,1)}, u32[]{:S(2)}) copy-start(bf16[256,768]{1,0:T(8,128)(2,1)} %param.31) | copy-start | bytes 1179652
  0.0 36.6 %copy-start.2 = (bf16[4096,256]{1,0:T(8,128)(2,1)S(1)}, bf16[4096,256]{1,0:T(8,128)(2,1)}, u32[]{:S(2)}) copy-start(bf16[4096,256]{1,0:T(8,128)(2,1)} %param.22) | copy-start | bytes 6291460
  7.4 22.7 %all-to-all-start = ((s32[2,2,128,8]{3,1,0,2:T(2,128)}), s32[2,2,128,8]{3,1,0,2:T(2,128)}, u32[]{:S(2)}, u32[]{:S(2)}) async-start(s32[2,2,128,8]{3,1,0,2:T(2,128)} %copy.48), calls=%async_computation | async-start | bytes 524288 | tf_op jit(solution)/shard_map/all_to_all | solution.py:100
  36.6 9.3 %copy-start.9 = (f32[128]{0:T(128)S(1)}, f32[128]{0:T(128)}, u32[]{:S(2)}) copy-start(f32[128]{0:T(128)} %param.25) | copy-start | bytes 1540
  36.6 9.3 %copy-start.10 = (f32[128]{0:T(128)S(1)}, f32[128]{0:T(128)}, u32[]{:S(2)}) copy-start(f32[128]{0:T(128)} %param.24) | copy-start | bytes 1540
  51.0 10.5 %copy-start.5 = (bf16[896,512]{1,0:T(8,128)(2,1)S(1)}, bf16[896,512]{1,0:T(8,128)(2,1)}, u32[]{:S(2)}) copy-start(bf16[896,512]{1,0:T(8,128)(2,1)} %param.26) | copy-start | bytes 2752516
  53.7 8.6 %copy-start.8 = (f32[512]{0:T(512)S(1)}, f32[512]{0:T(512)}, u32[]{:S(2)}) copy-start(f32[512]{0:T(512)} %param.27) | copy-start | bytes 6148
  56.4 29.8 %all-to-all-start.1 = ((bf16[2,128,8,384]{3,2,0,1:T(8,128)(2,1)}), bf16[2,128,8,384]{3,2,0,1:T(8,128)(2,1)}, u32[]{:S(2)}, u32[]{:S(2)}) async-start(bf16[2,128,8,384]{3,2,0,1:T(8,128)(2,1)} %copy.54), calls=%async_computation.1 | async-start | bytes 3145728 | tf_op jit(solution)/shard_map/all_to_all | solution.py:102
  86.2 4.2 %copy-start.3 = (bf16[256,512]{1,0:T(8,128)(2,1)S(1)}, bf16[256,512]{1,0:T(8,128)(2,1)}, u32[]{:S(2)}) copy-start(bf16[256,512]{1,0:T(8,128)(2,1)} %get-tuple-element.9) | copy-start | bytes 786436
  86.2 4.2 %copy-start.4 = (bf16[256,512]{1,0:T(8,128)(2,1)S(1)}, bf16[256,512]{1,0:T(8,128)(2,1)}, u32[]{:S(2)}) copy-start(bf16[256,512]{1,0:T(8,128)(2,1)} %get-tuple-element.10) | copy-start | bytes 786436
  91.2 1.9 %copy-start.1 = (f32[1024,1024]{1,0:T(8,128)}, f32[1024,1024]{1,0:T(8,128)S(1)}, u32[]{:S(2)}) copy-start(f32[1024,1024]{1,0:T(8,128)S(1)} %fusion.47) | copy-start | bytes 12582916
  101.6 23.4 %all-to-all-start.2 = ((bf16[2,128,8,256]{3,2,0,1:T(8,128)(2,1)}), bf16[2,128,8,256]{3,2,0,1:T(8,128)(2,1)S(1)}, u32[]{:S(2)}, u32[]{:S(2)}) async-start(bf16[2,128,8,256]{3,2,0,1:T(8,128)(2,1)} %copy.57), calls=%async_computation.2 | async-start | bytes 2097152 | tf_op jit(solution)/shard_map/all_to_all | solution.py:129
  105.4 6.3 %copy-start.7 = (s32[2048]{0:T(1024)S(1)}, s32[2048]{0:T(1024)}, u32[]{:S(2)}) copy-start(s32[2048]{0:T(1024)} %eq.85) | copy-start | bytes 24580
  126.0 13.5 %copy-start.6 = (pred[4096]{0:T(1024)(128)(4,1)S(1)}, pred[4096]{0:T(1024)(128)(4,1)}, u32[]{:S(2)}) copy-start(pred[4096]{0:T(1024)(128)(4,1)} %broadcast_compare_fusion) | copy-start | bytes 12292

commit v2 on v1

--- a/solution.py
+++ b/solution.py
@@ -1,6 +1,7 @@
 import jax
 import jax.numpy as jnp
 from jax import lax
+from jax.experimental import pallas as pl
 from jax.sharding import PartitionSpec as P
 
 
@@ -17,6 +18,46 @@
     update = jax.nn.sigmoid(input_part[:, width : 2 * width] + state_part[:, width : 2 * width])
     candid = jnp.tanh(input_part[:, 2 * width :] + reset * state_part[:, 2 * width :])
     return ((1.0 - update) * candid + update * state.astype(jnp.float32)).astype(jnp.bfloat16)
+
+
+def update_kernel(rows_ref, msg_ref, mem_ref, win_ref, bin_ref, whid_ref, out_ref):
+    block = out_ref.shape[0]
+    slots = rows_ref.shape[1]
+    width = mem_ref.shape[1]
+    ids = pl.program_id(0) * block + lax.broadcasted_iota(jnp.int32, (block, slots), 0)
+    hit = ids == rows_ref[...]
+    total = jnp.dot(hit.astype(jnp.bfloat16), msg_ref[...], preferred_element_type=jnp.float32)
+    count = jnp.sum(hit.astype(jnp.float32), axis=1, keepdims=True)
+    mean_msg = (total / jnp.maximum(count, 1.0)).astype(jnp.bfloat16)
+    state = mem_ref[...]
+    input_part = jnp.dot(mean_msg, win_ref[...], preferred_element_type=jnp.float32) + bin_ref[...]
+    state_part = jnp.dot(state, whid_ref[...], preferred_element_type=jnp.float32)
+    reset = jax.nn.sigmoid(input_part[:, :width] + state_part[:, :width])
+    update = jax.nn.sigmoid(input_part[:, width : 2 * width] + state_part[:, width : 2 * width])
+    candid = jnp.tanh(input_part[:, 2 * width :] + reset * state_part[:, 2 * width :])
+    fresh = (1.0 - update) * candid + update * state.astype(jnp.float32)
+    out_ref[...] = jnp.where(count > 0, fresh, state.astype(jnp.float32)).astype(out_ref.dtype)
+
+
+def owner_update(row_flat, msg_flat, memory, w_gru_in, b_gru_in, w_gru_hid):
+    rows_count, width = memory.shape
+    slots, msg_width = msg_flat.shape
+    block = 512
+    gates = w_gru_in.shape[1]
+    return pl.pallas_call(
+        update_kernel,
+        grid=(rows_count // block,),
+        in_specs=[
+            pl.BlockSpec((1, slots), lambda i: (0, 0)),
+            pl.BlockSpec((slots, msg_width), lambda i: (0, 0)),
+            pl.BlockSpec((block, width), lambda i: (i, 0)),
+            pl.BlockSpec((msg_width, gates), lambda i: (0, 0)),
+            pl.BlockSpec((1, gates), lambda i: (0, 0)),
+            pl.BlockSpec((width, gates), lambda i: (0, 0)),
+        ],
+        out_specs=pl.BlockSpec((block, width), lambda i: (i, 0)),
+        out_shape=jax.ShapeDtypeStruct(memory.shape, memory.dtype),
+    )(row_flat.reshape(1, slots), msg_flat, memory, w_gru_in, b_gru_in.reshape(1, gates), w_gru_hid)
 
 
 def slot_of(owner_ids, owner_count, capacity):
@@ -135,14 +176,7 @@
     )
     row_flat = rows_held.reshape(-1)
     msg_flat = arrived.reshape(-1, msg_width)
-    row_range = jnp.arange(rows_count, dtype=jnp.int32)
-    hits = row_range[:, None] == row_flat[None, :]
-    total = jnp.dot(hits.astype(jnp.bfloat16), msg_flat, preferred_element_type=jnp.float32)
-    count = jnp.sum(hits.astype(jnp.float32), axis=1)
-    divisor = jnp.maximum(count, 1.0)
-    mean_msg = (total / divisor[:, None]).astype(jnp.bfloat16)
-    new_state = gru_update(mean_msg, memory, w_gru_in, b_gru_in, w_gru_hid)
-    return jnp.where((count > 0)[:, None], new_state, memory)
+    return owner_update(row_flat, msg_flat, memory, w_gru_in, b_gru_in, w_gru_hid)
 
 
 def solution(mesh):

time: 151 us -> 132 us (0.87)
  matrix products: 41.8 us -> 18.1 us
  Pallas kernels: 0 us -> 19.3 us
  other arithmetic: 24.9 us -> 7.9 us
  waiting for transfers between devices: 39.6 us -> 50.5 us
  local copies, waits for them, and re-layouts: 23.2 us -> 15.7 us
    dot_general x2 -> x0, matrix products: 19.8 us -> none  [the longest x1 13.5 us: gru_update(): jnp.dot(mean_msg, w_gru_in, preferred_element_type=jnp.float32) + b_gru_in]
    pallas_call x0 -> x1, Pallas kernels: none -> 19.3 us  [owner_update(): pl.pallas_call(update_kernel, grid=(rows_count // block,), in_specs=[pl.B...]
    select_n x1 -> x0, other arithmetic: 11.1 us -> none  [local(): return jnp.where((count > 0)[:, None], new_state, memory)]
    all_to_all x1, waiting for transfers between devices: 9.17 us -> 18.2 us  [local(): lax.all_to_all(outgoing.reshape(2, devices_all, capacity, msg_width), ('e...]
    reduce_sum x1 -> x0, other arithmetic: 3.4 us -> none  [local(): count = jnp.sum(hits.astype(jnp.float32), axis=1)]
    concatenate x1, local copies, waits for them, and re-layouts: 2.68 us -> 0.87 us  [owner_lookup(): served = jnp.concatenate([mem_rows, encoded], axis=-1)]
  transfers between devices with their start and end apart: 3 -> 3, of which waited for: 3 -> 3; matrix products, arithmetic and copies ran while one was open for 10% -> 4% of each run, Pallas kernels for 0% -> 0%
where the time goes in v2:
time: 132 us
  waiting for transfers between devices  50.5 us (38%)
  starting transfers between devices  20 us (15%)
  Pallas kernels  19.3 us (15%)
  matrix products  18.1 us (14%)
  local copies, waits for them, and re-layouts  15.7 us (12%)
  other arithmetic  7.9 us (6%)
    all_to_all x1, waiting for transfers between devices, local(): lax.all_to_all(served, ('ev', 'node'), split_axis=1, concat_axis=1, tiled...  23.7 us
    pallas_call x1, Pallas kernels, owner_update(): pl.pallas_call(update_kernel, grid=(rows_count // block,), in_specs=[pl.B...  19.3 us
    all_to_all x1, waiting for transfers between devices, local(): lax.all_to_all(outgoing.reshape(2, devices_all, capacity, msg_width), ('e...  18.2 us
    all_to_all x1, starting transfers between devices, local(): lax.all_to_all(request, ('ev', 'node'), split_axis=2, concat_axis=2, tile...  12 us
    dot_general x1, matrix products, owner_lookup(): fetched = jnp.dot(select, table, preferred_element_type=jnp.float32)  9.13 us
    all_to_all x1, waiting for transfers between devices, local(): lax.all_to_all(request, ('ev', 'node'), split_axis=2, concat_axis=2, tile...  8.53 us
    all_to_all x1, starting transfers between devices, local(): lax.all_to_all(served, ('ev', 'node'), split_axis=1, concat_axis=1, tiled...  4.17 us
    all_to_all x1, starting transfers between devices, local(): lax.all_to_all(outgoing.reshape(2, devices_all, capacity, msg_width), ('e...  3.85 us
  transfers between devices with their start and end apart: 3, of which 3 were waited for; matrix products, arithmetic and copies ran while one was open for 4% of the time, Pallas kernels for 0%

profile of v2, /device:TPU:1, one launch (start us, length us, event | category | flops | bytes accessed | tf_op | source)
XLA Modules:
  0.0 131.9 jit_solution(672331477542852195)
XLA Ops:
  0.0 1.1 fusion.26
  1.1 1.2 fusion.25
  2.3 0.7 bitcast_add_fusion
  3.5 0.7 pad_add_fusion.2
  4.2 2.0 %select_reduce_fusion.1 = (s32[2,1024]{1,0:T(2,128)S(1)}, s32[2,1024]{1,0:T(2,128)S(1)}) fusion(s32[2,512]{1,0:T(2,128)S(1)} %pad_add_fusion.2, s32[2,512]{1,0:T(2,128)S(1)} %pad_add_fusion.1, s32[512]{0:T(512)} %param.20), kind=kLoop, calls=%fused_computation.4 | loop fusion | flops 5238784 | bytes 26624 | tf_op jit(solution)/shard_map/reduce_sum | solution.py:132
  6.5 0.9 copy.37
  7.4 12.0 %all-to-all-start = ((s32[2,2,128,8]{3,1,0,2:T(2,128)}), s32[2,2,128,8]{3,1,0,2:T(2,128)}, u32[]{:S(2)}, u32[]{:S(2)}) async-start(s32[2,2,128,8]{3,1,0,2:T(2,128)} %copy.37), calls=%async_computation | async-start | bytes 524288 | tf_op jit(solution)/shard_map/all_to_all | solution.py:141
  19.4 0.6 broadcast_in_dim.57
  20.0 1.6 %broadcast_in_dim.58 = bf16[4096,1]{1,0:T(8,128)(2,1)} reshape(bf16[4096]{0:T(1024)(128)(2,1)S(1)} %get-tuple-element.16) | data formatting | bytes 16384 | tf_op jit(solution)/shard_map/broadcast_in_dim | solution.py:82
  21.6 8.5 %all-to-all-done = s32[2,2,128,8]{3,1,0,2:T(2,128)} async-done(((s32[2,2,128,8]{3,1,0,2:T(2,128)}), s32[2,2,128,8]{3,1,0,2:T(2,128)}, u32[]{:S(2)}, u32[]{:S(2)}) %all-to-all-start) | async-done | bytes 16416 | tf_op jit(solution)/shard_map/all_to_all | solution.py:141
  30.1 1.6 %fusion.64 = (s32[1,2,128,8]{3,1,0,2:T(2,128)S(1)}, s32[1,2,128,8]{3,1,0,2:T(2,128)}) fusion(s32[2,2,128,8]{3,1,0,2:T(2,128)} %all-to-all-done), kind=kLoop, calls=%fused_computation.88 | loop fusion | bytes 32768 | tf_op jit(solution)/shard_map/slice | solution.py:76
  31.9 0.9 copy.38
  32.8 0.7 eq.71
  33.5 9.1 %fusion = f32[2048,258]{0,1:T(8,128)S(1)} fusion(s32[2048]{0:T(1024)} %eq.71, bf16[4096,1]{1,0:T(8,128)(2,1)} %broadcast_in_dim.58, bf16[4096,1]{1,0:T(8,128)(2,1)S(1)} %broadcast_in_dim.57, bf16[4096,256]{1,0:T(8,128)(2,1)S(1)} %copy-done.2), kind=kOutput, calls=%fused_computation.1 | convolution fusion | flops 4343250944 | bytes 4235264 | tf_op jit(solution)/shard_map/dot_general | solution.py:83
  42.9 3.7 %cosine_convert_fusion = bf16[2048,128]{0,1:T(8,128)(2,1)S(1)} fusion(f32[128]{0:T(128)S(1)} %copy-done.7, f32[128]{0:T(128)S(1)} %copy-done.8, f32[2048]{0:T(1024)S(1)} %bitcast.36), kind=kLoop, calls=%fused_computation.36 | loop fusion | flops 786432 | bytes 533504 | tf_op jit(solution)/shard_map/convert_element_type | solution.py:10
  46.7 0.9 copy.43
  47.6 1.3 copy.44
  48.9 4.2 %all-to-all-start.1 = ((bf16[2,128,8,384]{3,2,0,1:T(8,128)(2,1)}), bf16[2,128,8,384]{3,2,0,1:T(8,128)(2,1)S(1)}, u32[]{:S(2)}, u32[]{:S(2)}) async-start(bf16[2,128,8,384]{3,2,0,1:T(8,128)(2,1)} %copy.44), calls=%async_computation.1 | async-start | bytes 3145728 | tf_op jit(solution)/shard_map/all_to_all | solution.py:143
  53.2 1.3 convolution_add_fusion
  54.4 23.7 %all-to-all-done.1 = bf16[2,128,8,384]{3,2,0,1:T(8,128)(2,1)S(1)} async-done(((bf16[2,128,8,384]{3,2,0,1:T(8,128)(2,1)}), bf16[2,128,8,384]{3,2,0,1:T(8,128)(2,1)S(1)}, u32[]{:S(2)}, u32[]{:S(2)}) %all-to-all-start.1) | async-done | bytes 1572896 | tf_op jit(solution)/shard_map/all_to_all | solution.py:143
  78.2 1.3 fusion.19
  79.7 0.7 fusion.28
  80.4 1.9 %copy-done.1 = f32[1024,1024]{1,0:T(8,128)} copy-done((f32[1024,1024]{1,0:T(8,128)}, f32[1024,1024]{1,0:T(8,128)S(1)}, u32[]{:S(2)}) %copy-start.1) | copy-done | bytes 4194328
  82.3 1.2 fusion.62
  83.5 2.7 %fusion.24 = bf16[1024,256]{1,0:T(8,128)(2,1)S(1)} fusion(bf16[512,256]{1,0:T(8,128)(2,1)S(1)} %copy-done.9, f32[1024,1024]{1,0:T(8,128)} %copy-done.1, f32[512,512]{1,0:T(8,128)} %get-tuple-element.8, f32[512,512]{1,0:T(8,128)S(1)} %get-tuple-element.7, f32[512,512]{1,0:T(8,128)S(1)} %convolution_add_fusion, bf16[512,128]{1,0:T(8,128)(2,1)S(1)} %slice.90, ...), kind=kOutput, calls=%fused_computation.30 | convolution fusion | flops 407109632 | bytes 6422528 | tf_op jit(solution)/shard_map/dot_general | solution.py:163
  86.3 0.8 fusion.22
  87.1 1.1 copy.47
  88.1 3.9 %all-to-all-start.2 = ((bf16[2,128,8,256]{3,2,0,1:T(8,128)(2,1)}), bf16[2,128,8,256]{3,2,0,1:T(8,128)(2,1)S(1)}, u32[]{:S(2)}, u32[]{:S(2)}) async-start(bf16[2,128,8,256]{3,2,0,1:T(8,128)(2,1)} %copy.47), calls=%async_computation.2 | async-start | bytes 2097152 | tf_op jit(solution)/shard_map/all_to_all | solution.py:170
  92.6 0.7 reshape_reshape_squeeze.3.rows_ref
  93.3 18.2 %all-to-all-done.2 = bf16[2,128,8,256]{3,2,0,1:T(8,128)(2,1)S(1)} async-done(((bf16[2,128,8,256]{3,2,0,1:T(8,128)(2,1)}), bf16[2,128,8,256]{3,2,0,1:T(8,128)(2,1)S(1)}, u32[]{:S(2)}, u32[]{:S(2)}) %all-to-all-start.2) | async-done | bytes 1048608 | tf_op jit(solution)/shard_map/all_to_all | solution.py:170
  111.5 1.0 copy.48
  112.5 19.3 %shard_map.154 = bf16[4096,256]{1,0:T(8,128)(2,1)} custom-call(s32[1,2048]{1,0:T(1,128)} %reshape_reshape_squeeze.3.rows_ref, bf16[2048,256]{1,0:T(8,128)(2,1)} %bitcast.35, bf16[4096,256]{1,0:T(8,128)(2,1)} %mem_ref.1, bf16[256,768]{1,0:T(8,128)(2,1)} %win_ref.1, f32[1,768]{1,0:T(1,128)} %reshape.122.bin_ref, bf16[256,768]{1,0:T(8,128)(2,1)} %whid_ref.1), custom_call_target="tpu_custom_call" | custom-call | tf_op jit(solution)/shard_map/pallas_call | solution.py:47
  (40 shorter events, 2.0 us)
Async XLA Ops:
  0.0 53.2 %copy-start = (bf16[512,256]{1,0:T(8,128)(2,1)S(1)}, bf16[512,256]{1,0:T(8,128)(2,1)}, u32[]{:S(2)}) copy-start(bf16[512,256]{1,0:T(8,128)(2,1)} %param.21) | copy-start | bytes 786436
  0.0 19.4 %copy-start.4 = (s32[4096]{0:T(1024)S(1)}, s32[4096]{0:T(1024)}, u32[]{:S(2)}) copy-start(s32[4096]{0:T(1024)} %param.23) | copy-start | bytes 49156
  1.1 32.4 %copy-start.2 = (bf16[4096,256]{1,0:T(8,128)(2,1)S(1)}, bf16[4096,256]{1,0:T(8,128)(2,1)}, u32[]{:S(2)}) copy-start(bf16[4096,256]{1,0:T(8,128)(2,1)} %mem_ref.1) | copy-start | bytes 6291460
  7.4 22.7 %all-to-all-start = ((s32[2,2,128,8]{3,1,0,2:T(2,128)}), s32[2,2,128,8]{3,1,0,2:T(2,128)}, u32[]{:S(2)}, u32[]{:S(2)}) async-start(s32[2,2,128,8]{3,1,0,2:T(2,128)} %copy.37), calls=%async_computation | async-start | bytes 524288 | tf_op jit(solution)/shard_map/all_to_all | solution.py:141
  33.5 9.3 %copy-start.7 = (f32[128]{0:T(128)S(1)}, f32[128]{0:T(128)}, u32[]{:S(2)}) copy-start(f32[128]{0:T(128)} %param.25) | copy-start | bytes 1540
  33.5 9.3 %copy-start.8 = (f32[128]{0:T(128)S(1)}, f32[128]{0:T(128)}, u32[]{:S(2)}) copy-start(f32[128]{0:T(128)} %param.24) | copy-start | bytes 1540
  47.6 5.6 %copy-start.6 = (f32[512]{0:T(512)S(1)}, f32[512]{0:T(512)}, u32[]{:S(2)}) copy-start(f32[512]{0:T(512)} %param.27) | copy-start | bytes 6148
  48.9 4.2 %copy-start.3 = (bf16[896,512]{1,0:T(8,128)(2,1)S(1)}, bf16[896,512]{1,0:T(8,128)(2,1)}, u32[]{:S(2)}) copy-start(bf16[896,512]{1,0:T(8,128)(2,1)} %param.26) | copy-start | bytes 2752516
  48.9 29.3 %all-to-all-start.1 = ((bf16[2,128,8,384]{3,2,0,1:T(8,128)(2,1)}), bf16[2,128,8,384]{3,2,0,1:T(8,128)(2,1)S(1)}, u32[]{:S(2)}, u32[]{:S(2)}) async-start(bf16[2,128,8,384]{3,2,0,1:T(8,128)(2,1)} %copy.44), calls=%async_computation.1 | async-start | bytes 3145728 | tf_op jit(solution)/shard_map/all_to_all | solution.py:143
  80.4 1.9 %copy-start.1 = (f32[1024,1024]{1,0:T(8,128)}, f32[1024,1024]{1,0:T(8,128)S(1)}, u32[]{:S(2)}) copy-start(f32[1024,1024]{1,0:T(8,128)S(1)} %fusion.28) | copy-start | bytes 12582916
  82.3 1.2 copy-start.9
  86.3 5.7 %copy-start.5 = (f32[768]{0:T(1024)S(1)}, f32[768]{0:T(1024)}, u32[]{:S(2)}) copy-start(f32[768]{0:T(1024)} %param.30) | copy-start | bytes 9220
  88.1 23.4 %all-to-all-start.2 = ((bf16[2,128,8,256]{3,2,0,1:T(8,128)(2,1)}), bf16[2,128,8,256]{3,2,0,1:T(8,128)(2,1)S(1)}, u32[]{:S(2)}, u32[]{:S(2)}) async-start(bf16[2,128,8,256]{3,2,0,1:T(8,128)(2,1)} %copy.47), calls=%async_computation.2 | async-start | bytes 2097152 | tf_op jit(solution)/shard_map/all_to_all | solution.py:170

commit v3 on v2

--- a/solution.py
+++ b/solution.py
@@ -20,20 +20,25 @@
     return ((1.0 - update) * candid + update * state.astype(jnp.float32)).astype(jnp.bfloat16)
 
 
+def gate(x):
+    return 0.5 + 0.5 * jnp.tanh(0.5 * x)
+
+
 def update_kernel(rows_ref, msg_ref, mem_ref, win_ref, bin_ref, whid_ref, out_ref):
     block = out_ref.shape[0]
     slots = rows_ref.shape[1]
     width = mem_ref.shape[1]
     ids = pl.program_id(0) * block + lax.broadcasted_iota(jnp.int32, (block, slots), 0)
-    hit = ids == rows_ref[...]
-    total = jnp.dot(hit.astype(jnp.bfloat16), msg_ref[...], preferred_element_type=jnp.float32)
-    count = jnp.sum(hit.astype(jnp.float32), axis=1, keepdims=True)
+    onehot = (ids == rows_ref[...]).astype(jnp.bfloat16)
+    total = jnp.dot(onehot, msg_ref[...], preferred_element_type=jnp.float32)
+    ones = jnp.ones((slots, 128), jnp.bfloat16)
+    count = jnp.dot(onehot, ones, preferred_element_type=jnp.float32)[:, :1]
     mean_msg = (total / jnp.maximum(count, 1.0)).astype(jnp.bfloat16)
     state = mem_ref[...]
     input_part = jnp.dot(mean_msg, win_ref[...], preferred_element_type=jnp.float32) + bin_ref[...]
     state_part = jnp.dot(state, whid_ref[...], preferred_element_type=jnp.float32)
-    reset = jax.nn.sigmoid(input_part[:, :width] + state_part[:, :width])
-    update = jax.nn.sigmoid(input_part[:, width : 2 * width] + state_part[:, width : 2 * width])
+    reset = gate(input_part[:, :width] + state_part[:, :width])
+    update = gate(input_part[:, width : 2 * width] + state_part[:, width : 2 * width])
     candid = jnp.tanh(input_part[:, 2 * width :] + reset * state_part[:, 2 * width :])
     fresh = (1.0 - update) * candid + update * state.astype(jnp.float32)
     out_ref[...] = jnp.where(count > 0, fresh, state.astype(jnp.float32)).astype(out_ref.dtype)
@@ -42,7 +47,7 @@
 def owner_update(row_flat, msg_flat, memory, w_gru_in, b_gru_in, w_gru_hid):
     rows_count, width = memory.shape
     slots, msg_width = msg_flat.shape
-    block = 512
+    block = 1024
     gates = w_gru_in.shape[1]
     return pl.pallas_call(
         update_kernel,

time: 132 us -> 129 us (0.977)
  Pallas kernels: 19.3 us -> 16.1 us
    pallas_call x1, Pallas kernels: 19.3 us -> 16.1 us  [owner_update(): pl.pallas_call(update_kernel, grid=(rows_count // block,), in_specs=[pl.B...]
where the time goes in v3:
time: 129 us
  waiting for transfers between devices  50.5 us (39%)
  starting transfers between devices  20 us (16%)
  matrix products  18.1 us (14%)
  Pallas kernels  16.1 us (12%)
  local copies, waits for them, and re-layouts  15.7 us (12%)
  other arithmetic  7.9 us (6%)
    all_to_all x1, waiting for transfers between devices, local(): lax.all_to_all(served, ('ev', 'node'), split_axis=1, concat_axis=1, tiled...  23.7 us
    all_to_all x1, waiting for transfers between devices, local(): lax.all_to_all(outgoing.reshape(2, devices_all, capacity, msg_width), ('e...  18.2 us
    pallas_call x1, Pallas kernels, owner_update(): pl.pallas_call(update_kernel, grid=(rows_count // block,), in_specs=[pl.B...  16.1 us
    all_to_all x1, starting transfers between devices, local(): lax.all_to_all(request, ('ev', 'node'), split_axis=2, concat_axis=2, tile...  12 us
    dot_general x1, matrix products, owner_lookup(): fetched = jnp.dot(select, table, preferred_element_type=jnp.float32)  9.13 us
    all_to_all x1, waiting for transfers between devices, local(): lax.all_to_all(request, ('ev', 'node'), split_axis=2, concat_axis=2, tile...  8.53 us
    all_to_all x1, starting transfers between devices, local(): lax.all_to_all(served, ('ev', 'node'), split_axis=1, concat_axis=1, tiled...  4.17 us
    all_to_all x1, starting transfers between devices, local(): lax.all_to_all(outgoing.reshape(2, devices_all, capacity, msg_width), ('e...  3.85 us
  transfers between devices with their start and end apart: 3, of which 3 were waited for; matrix products, arithmetic and copies ran while one was open for 4% of the time, Pallas kernels for 0%

profile of v3, /device:TPU:1, one launch (start us, length us, event | category | flops | bytes accessed | tf_op | source)
XLA Modules:
  0.0 128.6 jit_solution(11328245941094388496)
XLA Ops:
  0.0 1.1 fusion.26
  1.1 1.2 fusion.25
  2.3 0.7 bitcast_add_fusion
  3.5 0.7 pad_add_fusion.2
  4.2 2.0 %select_reduce_fusion.1 = (s32[2,1024]{1,0:T(2,128)S(1)}, s32[2,1024]{1,0:T(2,128)S(1)}) fusion(s32[2,512]{1,0:T(2,128)S(1)} %pad_add_fusion.2, s32[2,512]{1,0:T(2,128)S(1)} %pad_add_fusion.1, s32[512]{0:T(512)} %param.20), kind=kLoop, calls=%fused_computation.4 | loop fusion | flops 5238784 | bytes 26624 | tf_op jit(solution)/shard_map/reduce_sum | solution.py:137
  6.5 0.9 copy.37
  7.4 12.0 %all-to-all-start = ((s32[2,2,128,8]{3,1,0,2:T(2,128)}), s32[2,2,128,8]{3,1,0,2:T(2,128)}, u32[]{:S(2)}, u32[]{:S(2)}) async-start(s32[2,2,128,8]{3,1,0,2:T(2,128)} %copy.37), calls=%async_computation | async-start | bytes 524288 | tf_op jit(solution)/shard_map/all_to_all | solution.py:146
  19.4 0.6 broadcast_in_dim.57
  20.0 1.6 %broadcast_in_dim.58 = bf16[4096,1]{1,0:T(8,128)(2,1)} reshape(bf16[4096]{0:T(1024)(128)(2,1)S(1)} %get-tuple-element.16) | data formatting | bytes 16384 | tf_op jit(solution)/shard_map/broadcast_in_dim | solution.py:87
  21.6 8.5 %all-to-all-done = s32[2,2,128,8]{3,1,0,2:T(2,128)} async-done(((s32[2,2,128,8]{3,1,0,2:T(2,128)}), s32[2,2,128,8]{3,1,0,2:T(2,128)}, u32[]{:S(2)}, u32[]{:S(2)}) %all-to-all-start) | async-done | bytes 16416 | tf_op jit(solution)/shard_map/all_to_all | solution.py:146
  30.1 1.6 %fusion.64 = (s32[1,2,128,8]{3,1,0,2:T(2,128)S(1)}, s32[1,2,128,8]{3,1,0,2:T(2,128)}) fusion(s32[2,2,128,8]{3,1,0,2:T(2,128)} %all-to-all-done), kind=kLoop, calls=%fused_computation.88 | loop fusion | bytes 32768 | tf_op jit(solution)/shard_map/slice | solution.py:81
  31.9 0.9 copy.38
  32.8 0.7 eq.71
  33.5 9.1 %fusion = f32[2048,258]{0,1:T(8,128)S(1)} fusion(s32[2048]{0:T(1024)} %eq.71, bf16[4096,1]{1,0:T(8,128)(2,1)} %broadcast_in_dim.58, bf16[4096,1]{1,0:T(8,128)(2,1)S(1)} %broadcast_in_dim.57, bf16[4096,256]{1,0:T(8,128)(2,1)S(1)} %copy-done.2), kind=kOutput, calls=%fused_computation.1 | convolution fusion | flops 4343250944 | bytes 4235264 | tf_op jit(solution)/shard_map/dot_general | solution.py:88
  42.9 3.7 %cosine_convert_fusion = bf16[2048,128]{0,1:T(8,128)(2,1)S(1)} fusion(f32[128]{0:T(128)S(1)} %copy-done.7, f32[128]{0:T(128)S(1)} %copy-done.8, f32[2048]{0:T(1024)S(1)} %bitcast.36), kind=kLoop, calls=%fused_computation.36 | loop fusion | flops 786432 | bytes 533504 | tf_op jit(solution)/shard_map/convert_element_type | solution.py:10
  46.7 0.9 copy.43
  47.6 1.3 %copy.44 = bf16[2,128,8,384]{3,2,0,1:T(8,128)(2,1)} copy(bf16[2,128,8,384]{3,2,1,0:T(8,128)(2,1)S(1)} %bitcast.34) | data formatting | bytes 3145728 | tf_op jit(solution)/shard_map/reshape | solution.py:96
  48.9 4.2 %all-to-all-start.1 = ((bf16[2,128,8,384]{3,2,0,1:T(8,128)(2,1)}), bf16[2,128,8,384]{3,2,0,1:T(8,128)(2,1)S(1)}, u32[]{:S(2)}, u32[]{:S(2)}) async-start(bf16[2,128,8,384]{3,2,0,1:T(8,128)(2,1)} %copy.44), calls=%async_computation.1 | async-start | bytes 3145728 | tf_op jit(solution)/shard_map/all_to_all | solution.py:148
  53.2 1.3 convolution_add_fusion
  54.4 23.7 %all-to-all-done.1 = bf16[2,128,8,384]{3,2,0,1:T(8,128)(2,1)S(1)} async-done(((bf16[2,128,8,384]{3,2,0,1:T(8,128)(2,1)}), bf16[2,128,8,384]{3,2,0,1:T(8,128)(2,1)S(1)}, u32[]{:S(2)}, u32[]{:S(2)}) %all-to-all-start.1) | async-done | bytes 1572896 | tf_op jit(solution)/shard_map/all_to_all | solution.py:148
  78.2 1.3 %fusion.19 = bf16[2,512,384]{2,1,0:T(8,128)(2,1)S(1)} fusion(bf16[2,128,8,384]{3,2,0,1:T(8,128)(2,1)S(1)} %all-to-all-done.1, s32[2,512]{1,0:T(2,128)S(1)} %pad_add_fusion.1), kind=kOutput, calls=%fused_computation.26 | convolution fusion | flops 806748160 | bytes 2363392 | tf_op jit(solution)/shard_map/kse,ksc->kec/dot_general | solution.py:151
  79.7 0.7 fusion.28
  80.4 1.9 %copy-done.1 = f32[1024,1024]{1,0:T(8,128)} copy-done((f32[1024,1024]{1,0:T(8,128)}, f32[1024,1024]{1,0:T(8,128)S(1)}, u32[]{:S(2)}) %copy-start.1) | copy-done | bytes 4194328
  82.3 1.2 fusion.62
  83.5 2.7 %fusion.24 = bf16[1024,256]{1,0:T(8,128)(2,1)S(1)} fusion(bf16[512,256]{1,0:T(8,128)(2,1)S(1)} %copy-done.9, f32[1024,1024]{1,0:T(8,128)} %copy-done.1, f32[512,512]{1,0:T(8,128)} %get-tuple-element.8, f32[512,512]{1,0:T(8,128)S(1)} %get-tuple-element.7, f32[512,512]{1,0:T(8,128)S(1)} %convolution_add_fusion, bf16[512,128]{1,0:T(8,128)(2,1)S(1)} %slice.90, ...), kind=kOutput, calls=%fused_computation.30 | convolution fusion | flops 407109632 | bytes 6422528 | tf_op jit(solution)/shard_map/dot_general | solution.py:168
  86.3 0.8 fusion.22
  87.1 1.1 copy.47
  88.1 3.9 %all-to-all-start.2 = ((bf16[2,128,8,256]{3,2,0,1:T(8,128)(2,1)}), bf16[2,128,8,256]{3,2,0,1:T(8,128)(2,1)S(1)}, u32[]{:S(2)}, u32[]{:S(2)}) async-start(bf16[2,128,8,256]{3,2,0,1:T(8,128)(2,1)} %copy.47), calls=%async_computation.2 | async-start | bytes 2097152 | tf_op jit(solution)/shard_map/all_to_all | solution.py:175
  92.6 0.7 reshape_reshape_squeeze.3.rows_ref
  93.3 18.2 %all-to-all-done.2 = bf16[2,128,8,256]{3,2,0,1:T(8,128)(2,1)S(1)} async-done(((bf16[2,128,8,256]{3,2,0,1:T(8,128)(2,1)}), bf16[2,128,8,256]{3,2,0,1:T(8,128)(2,1)S(1)}, u32[]{:S(2)}, u32[]{:S(2)}) %all-to-all-start.2) | async-done | bytes 1048608 | tf_op jit(solution)/shard_map/all_to_all | solution.py:175
  111.5 1.0 copy.48
  112.5 16.1 %shard_map.154 = bf16[4096,256]{1,0:T(8,128)(2,1)} custom-call(s32[1,2048]{1,0:T(1,128)} %reshape_reshape_squeeze.3.rows_ref, bf16[2048,256]{1,0:T(8,128)(2,1)} %bitcast.35, bf16[4096,256]{1,0:T(8,128)(2,1)} %mem_ref.1, bf16[256,768]{1,0:T(8,128)(2,1)} %win_ref.1, f32[1,768]{1,0:T(1,128)} %reshape.122.bin_ref, bf16[256,768]{1,0:T(8,128)(2,1)} %whid_ref.1), custom_call_target="tpu_custom_call" | custom-call | tf_op jit(solution)/shard_map/pallas_call | solution.py:52
  (40 shorter events, 2.0 us)
Async XLA Ops:
  0.0 53.2 %copy-start = (bf16[512,256]{1,0:T(8,128)(2,1)S(1)}, bf16[512,256]{1,0:T(8,128)(2,1)}, u32[]{:S(2)}) copy-start(bf16[512,256]{1,0:T(8,128)(2,1)} %param.21) | copy-start | bytes 786436
  0.0 19.4 %copy-start.4 = (s32[4096]{0:T(1024)S(1)}, s32[4096]{0:T(1024)}, u32[]{:S(2)}) copy-start(s32[4096]{0:T(1024)} %param.23) | copy-start | bytes 49156
  1.1 32.4 %copy-start.2 = (bf16[4096,256]{1,0:T(8,128)(2,1)S(1)}, bf16[4096,256]{1,0:T(8,128)(2,1)}, u32[]{:S(2)}) copy-start(bf16[4096,256]{1,0:T(8,128)(2,1)} %mem_ref.1) | copy-start | bytes 6291460
  7.4 22.7 %all-to-all-start = ((s32[2,2,128,8]{3,1,0,2:T(2,128)}), s32[2,2,128,8]{3,1,0,2:T(2,128)}, u32[]{:S(2)}, u32[]{:S(2)}) async-start(s32[2,2,128,8]{3,1,0,2:T(2,128)} %copy.37), calls=%async_computation | async-start | bytes 524288 | tf_op jit(solution)/shard_map/all_to_all | solution.py:146
  33.5 9.3 %copy-start.7 = (f32[128]{0:T(128)S(1)}, f32[128]{0:T(128)}, u32[]{:S(2)}) copy-start(f32[128]{0:T(128)} %param.25) | copy-start | bytes 1540
  33.5 9.3 %copy-start.8 = (f32[128]{0:T(128)S(1)}, f32[128]{0:T(128)}, u32[]{:S(2)}) copy-start(f32[128]{0:T(128)} %param.24) | copy-start | bytes 1540
  47.6 5.6 %copy-start.6 = (f32[512]{0:T(512)S(1)}, f32[512]{0:T(512)}, u32[]{:S(2)}) copy-start(f32[512]{0:T(512)} %param.27) | copy-start | bytes 6148
  48.9 4.2 %copy-start.3 = (bf16[896,512]{1,0:T(8,128)(2,1)S(1)}, bf16[896,512]{1,0:T(8,128)(2,1)}, u32[]{:S(2)}) copy-start(bf16[896,512]{1,0:T(8,128)(2,1)} %param.26) | copy-start | bytes 2752516
  48.9 29.3 %all-to-all-start.1 = ((bf16[2,128,8,384]{3,2,0,1:T(8,128)(2,1)}), bf16[2,128,8,384]{3,2,0,1:T(8,128)(2,1)S(1)}, u32[]{:S(2)}, u32[]{:S(2)}) async-start(bf16[2,128,8,384]{3,2,0,1:T(8,128)(2,1)} %copy.44), calls=%async_computation.1 | async-start | bytes 3145728 | tf_op jit(solution)/shard_map/all_to_all | solution.py:148
  80.4 1.9 %copy-start.1 = (f32[1024,1024]{1,0:T(8,128)}, f32[1024,1024]{1,0:T(8,128)S(1)}, u32[]{:S(2)}) copy-start(f32[1024,1024]{1,0:T(8,128)S(1)} %fusion.28) | copy-start | bytes 12582916
  82.3 1.2 copy-start.9
  86.3 5.7 %copy-start.5 = (f32[768]{0:T(1024)S(1)}, f32[768]{0:T(1024)}, u32[]{:S(2)}) copy-start(f32[768]{0:T(1024)} %param.30) | copy-start | bytes 9220
  88.1 23.4 %all-to-all-start.2 = ((bf16[2,128,8,256]{3,2,0,1:T(8,128)(2,1)}), bf16[2,128,8,256]{3,2,0,1:T(8,128)(2,1)S(1)}, u32[]{:S(2)}, u32[]{:S(2)}) async-start(bf16[2,128,8,256]{3,2,0,1:T(8,128)(2,1)} %copy.47), calls=%async_computation.2 | async-start | bytes 2097152 | tf_op jit(solution)/shard_map/all_to_all | solution.py:175

commit v4 on v3

--- a/solution.py
+++ b/solution.py
@@ -63,6 +63,51 @@
         out_specs=pl.BlockSpec((block, width), lambda i: (i, 0)),
         out_shape=jax.ShapeDtypeStruct(memory.shape, memory.dtype),
     )(row_flat.reshape(1, slots), msg_flat, memory, w_gru_in, b_gru_in.reshape(1, gates), w_gru_hid)
+
+
+def message_kernel(col_ref, row_ref, fetched_ref, edge_ref, w_in_ref, w_out_ref, out_ref):
+    events = edge_ref.shape[0]
+    slot_total = fetched_ref.shape[1]
+    width = out_ref.shape[2]
+    time_width = fetched_ref.shape[2] - width
+    lane_ids = lax.broadcasted_iota(jnp.int32, (events, slot_total), 1)
+    picked = []
+    for side in range(2):
+        pick = (lane_ids == col_ref[:, side : side + 1]).astype(jnp.bfloat16)
+        rows = jnp.dot(pick, fetched_ref[side], preferred_element_type=jnp.float32)
+        picked.append(rows.astype(jnp.bfloat16))
+    mem_src, enc_src = picked[0][:, :width], picked[0][:, width:]
+    mem_dst, enc_dst = picked[1][:, :width], picked[1][:, width:]
+    w_self = w_in_ref[:width]
+    w_other = w_in_ref[width : 2 * width]
+    w_time = w_in_ref[2 * width : 2 * width + time_width]
+    edge = edge_ref[...]
+
+    def message(own, other, enc):
+        hidden = (
+            jnp.dot(own, w_self, preferred_element_type=jnp.float32)
+            + jnp.dot(other, w_other, preferred_element_type=jnp.float32)
+            + jnp.dot(enc, w_time, preferred_element_type=jnp.float32)
+            + edge
+        )
+        hidden = jnp.maximum(hidden, 0.0).astype(jnp.bfloat16)
+        return jnp.dot(hidden, w_out_ref[...], preferred_element_type=jnp.float32).astype(jnp.bfloat16)
+
+    sent = (message(mem_src, mem_dst, enc_src), message(mem_dst, mem_src, enc_dst))
+    sub_ids = lax.broadcasted_iota(jnp.int32, (slot_total, events), 0)
+    for side in range(2):
+        place = (sub_ids == row_ref[side : side + 1, :]).astype(jnp.bfloat16)
+        out_ref[side] = jnp.dot(place, sent[side], preferred_element_type=jnp.float32).astype(out_ref.dtype)
+
+
+def event_messages(slot_ids, fetched, edge_part, w_msg_in, w_msg_out):
+    sides, slot_total, fetched_width = fetched.shape
+    events, hidden_width = edge_part.shape
+    msg_width = w_msg_out.shape[1]
+    return pl.pallas_call(
+        message_kernel,
+        out_shape=jax.ShapeDtypeStruct((sides, slot_total, msg_width), jnp.bfloat16),
+    )(slot_ids.T, slot_ids, fetched, edge_part, w_msg_in, w_msg_out)
 
 
 def slot_of(owner_ids, owner_count, capacity):
@@ -148,30 +193,7 @@
     returned = lax.all_to_all(served, ("ev", "node"), split_axis=1, concat_axis=1, tiled=True)
     rows_held = received[0]
     fetched_flat = returned.reshape(2, slot_total, width + time_width)
-    picked = jnp.einsum(
-        "kse,ksc->kec", placement, fetched_flat, preferred_element_type=jnp.float32
-    ).astype(jnp.bfloat16)
-    picked_src = picked[0]
-    picked_dst = picked[1]
-    mem_stack = jnp.concatenate([picked_src[:, :width], picked_dst[:, :width]], axis=0)
-    enc_stack = jnp.concatenate([picked_src[:, width:], picked_dst[:, width:]], axis=0)
-    paired_weight = jnp.concatenate([w_msg_in[:width], w_msg_in[width : 2 * width]], axis=1)
-    projected = jnp.dot(mem_stack, paired_weight, preferred_element_type=jnp.float32)
-    time_term = jnp.dot(
-        enc_stack, w_msg_in[2 * width : 2 * width + time_width], preferred_element_type=jnp.float32
-    )
-    self_term = projected[:, :hidden_width]
-    other_term = projected[:, hidden_width:]
-    crossed = jnp.concatenate([other_term[events_here:], other_term[:events_here]], axis=0)
-    edge_both = jnp.concatenate([edge_part, edge_part], axis=0)
-    hidden = jax.nn.relu(self_term + crossed + time_term + edge_both).astype(jnp.bfloat16)
-    messages = jnp.dot(hidden, w_msg_out, preferred_element_type=jnp.float32).astype(jnp.bfloat16)
-    outgoing = jnp.einsum(
-        "kse,kec->ksc",
-        placement,
-        messages.reshape(2, events_here, msg_width),
-        preferred_element_type=jnp.float32,
-    ).astype(jnp.bfloat16)
+    outgoing = event_messages(slot_ids, fetched_flat, edge_part, w_msg_in, w_msg_out)
     arrived = lax.all_to_all(
         outgoing.reshape(2, devices_all, capacity, msg_width),
         ("ev", "node"),

time: 129 us -> 131 us (1.016)
  Pallas kernels: 16.1 us -> 22.6 us
  matrix products: 18.1 us -> 13.5 us
  waiting for transfers between devices: 50.5 us -> 48.7 us
  local copies, waits for them, and re-layouts: 15.7 us -> 17.3 us
    pallas_call x0 -> x1, Pallas kernels: none -> 6.48 us  [event_messages(): pl.pallas_call(message_kernel, out_shape=jax.ShapeDtypeStruct((sides, slo...]
    dot_general x4 -> x0, matrix products: 5.52 us -> none  [the longest x1 2.73 us: local(): jnp.dot(hidden, w_msg_out, preferred_element_type=jnp.float32)]
    unnamed x20 -> x16, local copies, waits for them, and re-layouts: 1.98 us -> 0.04 us
    all_to_all x1, waiting for transfers between devices: 23.7 us -> 22 us  [local(): lax.all_to_all(served, ('ev', 'node'), split_axis=1, concat_axis=1, tiled...]
    slice x2, local copies, waits for them, and re-layouts: 1.63 us -> 3.18 us  [owner_lookup(): time_request = request_pair[1].reshape(-1)]
  transfers between devices with their start and end apart: 3 -> 3, of which waited for: 3 -> 3; matrix products, arithmetic and copies ran while one was open for 4% -> 5% of each run, Pallas kernels for 0% -> 0%
where the time goes in v4:
time: 131 us; the launch traced here: 130 us
  waiting for transfers between devices  48.7 us (37%)
  Pallas kernels  22.6 us (17%)
  starting transfers between devices  20 us (15%)
  local copies, waits for them, and re-layouts  17.3 us (13%)
  matrix products  13.5 us (10%)
  other arithmetic  7.9 us (6%)
    all_to_all x1, waiting for transfers between devices, local(): lax.all_to_all(served, ('ev', 'node'), split_axis=1, concat_axis=1, tiled...  22 us
    all_to_all x1, waiting for transfers between devices, local(): lax.all_to_all(outgoing.reshape(2, devices_all, capacity, msg_width), ('e...  18.2 us
    pallas_call x1, Pallas kernels, owner_update(): pl.pallas_call(update_kernel, grid=(rows_count // block,), in_specs=[pl.B...  16.1 us
    all_to_all x1, starting transfers between devices, local(): lax.all_to_all(request, ('ev', 'node'), split_axis=2, concat_axis=2, tile...  12 us
    dot_general x1, matrix products, owner_lookup(): fetched = jnp.dot(select, table, preferred_element_type=jnp.float32)  9.14 us
    all_to_all x1, waiting for transfers between devices, local(): lax.all_to_all(request, ('ev', 'node'), split_axis=2, concat_axis=2, tile...  8.53 us
    pallas_call x1, Pallas kernels, event_messages(): pl.pallas_call(message_kernel, out_shape=jax.ShapeDtypeStruct((sides, slo...  6.48 us
    all_to_all x1, starting transfers between devices, local(): lax.all_to_all(served, ('ev', 'node'), split_axis=1, concat_axis=1, tiled...  4.16 us
  transfers between devices with their start and end apart: 3, of which 3 were waited for; matrix products, arithmetic and copies ran while one was open for 5% of the time, Pallas kernels for 0%

profile of v4, /device:TPU:1, one launch (start us, length us, event | category | flops | bytes accessed | tf_op | source)
XLA Modules:
  0.0 130.3 jit_solution(11981339573481404646)
XLA Ops:
  0.0 1.1 fusion.8
  1.1 1.1 fusion.9
  2.2 0.7 bitcast_add_fusion
  2.9 0.5 fusion.2
  3.4 0.7 pad_add_fusion.2
  4.1 2.0 %select_reduce_fusion.1 = (s32[2,1024]{1,0:T(2,128)S(1)}, s32[2,1024]{1,0:T(2,128)S(1)}) fusion(s32[2,512]{1,0:T(2,128)S(1)} %pad_add_fusion.2, s32[2,512]{1,0:T(2,128)S(1)} %get-tuple-element.12.row_ref, s32[512]{0:T(512)} %param.20), kind=kLoop, calls=%fused_computation.4 | loop fusion | flops 5238784 | bytes 26624 | tf_op jit(solution)/shard_map/reduce_sum | solution.py:182
  6.4 0.9 copy.37
  7.3 12.0 %all-to-all-start = ((s32[2,2,128,8]{3,1,0,2:T(2,128)}), s32[2,2,128,8]{3,1,0,2:T(2,128)}, u32[]{:S(2)}, u32[]{:S(2)}) async-start(s32[2,2,128,8]{3,1,0,2:T(2,128)} %copy.37), calls=%async_computation | async-start | bytes 524288 | tf_op jit(solution)/shard_map/all_to_all | solution.py:191
  19.3 0.6 broadcast_in_dim.57
  19.9 1.6 %broadcast_in_dim.58 = bf16[4096,1]{1,0:T(8,128)(2,1)} reshape(bf16[4096]{0:T(1024)(128)(2,1)S(1)} %get-tuple-element.10) | data formatting | bytes 16384 | tf_op jit(solution)/shard_map/broadcast_in_dim | solution.py:132
  21.5 8.5 %all-to-all-done = s32[2,2,128,8]{3,1,0,2:T(2,128)} async-done(((s32[2,2,128,8]{3,1,0,2:T(2,128)}), s32[2,2,128,8]{3,1,0,2:T(2,128)}, u32[]{:S(2)}, u32[]{:S(2)}) %all-to-all-start) | async-done | bytes 16416 | tf_op jit(solution)/shard_map/all_to_all | solution.py:191
  30.1 1.6 %fusion.25 = (s32[1,2,128,8]{3,1,0,2:T(2,128)}, s32[1,2,128,8]{3,1,0,2:T(2,128)S(1)}) fusion(s32[2,2,128,8]{3,1,0,2:T(2,128)} %all-to-all-done), kind=kLoop, calls=%fused_computation.54 | loop fusion | bytes 32768 | tf_op jit(solution)/shard_map/slice | solution.py:126
  31.7 0.7 eq.71
  32.4 1.6 %copy.42 = s32[1,2,128,8]{3,2,1,0:T(8,128)} copy(s32[1,2,128,8]{3,1,0,2:T(2,128)} %get-tuple-element.7) | data formatting | bytes 16384 | tf_op jit(solution)/shard_map/slice | solution.py:126
  34.0 1.0 reshape_squeeze.3
  35.0 9.1 %fusion = f32[2048,258]{0,1:T(8,128)S(1)} fusion(s32[2048]{0:T(1024)} %eq.71, bf16[4096,1]{1,0:T(8,128)(2,1)} %broadcast_in_dim.58, bf16[4096,1]{1,0:T(8,128)(2,1)S(1)} %broadcast_in_dim.57, bf16[4096,256]{1,0:T(8,128)(2,1)S(1)} %copy-done.1), kind=kOutput, calls=%fused_computation.1 | convolution fusion | flops 4343250944 | bytes 4235264 | tf_op jit(solution)/shard_map/dot_general | solution.py:133
  44.4 3.7 %cosine_convert_fusion = bf16[2048,128]{0,1:T(8,128)(2,1)S(1)} fusion(f32[128]{0:T(128)S(1)} %copy-done.6, f32[128]{0:T(128)S(1)} %copy-done.7, f32[2048]{0:T(1024)S(1)} %bitcast.30), kind=kLoop, calls=%fused_computation.20 | loop fusion | flops 786432 | bytes 533504 | tf_op jit(solution)/shard_map/convert_element_type | solution.py:10
  48.2 0.9 copy.43
  49.1 1.3 copy.44
  50.4 4.2 %all-to-all-start.1 = ((bf16[2,128,8,384]{3,2,0,1:T(8,128)(2,1)}), bf16[2,128,8,384]{3,2,0,1:T(8,128)(2,1)S(1)}, u32[]{:S(2)}, u32[]{:S(2)}) async-start(bf16[2,128,8,384]{3,2,0,1:T(8,128)(2,1)} %copy.44), calls=%async_computation.1 | async-start | bytes 3145728 | tf_op jit(solution)/shard_map/all_to_all | solution.py:193
  54.6 0.9 copy.46.col_ref
  55.4 2.2 %convolution_add_fusion.edge_ref = f32[512,512]{1,0:T(8,128)} fusion(bf16[512,256]{1,0:T(8,128)(2,1)S(1)} %copy-done, f32[512]{0:T(512)S(1)} %copy-done.5, bf16[896,512]{1,0:T(8,128)(2,1)} %w_in_ref.1), kind=kOutput, calls=%fused_computation.15 | convolution fusion | flops 134479872 | bytes 1574912 | tf_op jit(solution)/shard_map/dot_general | solution.py:187
  57.7 22.0 %all-to-all-done.1 = bf16[2,128,8,384]{3,2,0,1:T(8,128)(2,1)S(1)} async-done(((bf16[2,128,8,384]{3,2,0,1:T(8,128)(2,1)}), bf16[2,128,8,384]{3,2,0,1:T(8,128)(2,1)S(1)}, u32[]{:S(2)}, u32[]{:S(2)}) %all-to-all-start.1) | async-done | bytes 1572896 | tf_op jit(solution)/shard_map/all_to_all | solution.py:193
  79.7 1.3 copy.50
  81.0 6.5 %shard_map.154 = bf16[2,1024,256]{2,1,0:T(8,128)(2,1)} custom-call(s32[512,2]{1,0:T(8,128)} %copy.46.col_ref, s32[2,512]{1,0:T(2,128)} %copy-done.2, bf16[2,1024,384]{2,1,0:T(8,128)(2,1)} %bitcast.27, f32[512,512]{1,0:T(8,128)} %convolution_add_fusion.edge_ref, bf16[896,512]{1,0:T(8,128)(2,1)} %w_in_ref.1, bf16[512,256]{1,0:T(8,128)(2,1)} %w_out_ref.1), custom_call_target="tpu_custom_call" | custom-call | tf_op jit(solution)/shard_map/pallas_call | solution.py:107
  87.4 2.3 %copy.47 = bf16[2,128,8,256]{3,2,0,1:T(8,128)(2,1)} copy(bf16[2,128,8,256]{3,2,1,0:T(8,128)(2,1)} %bitcast.28) | data formatting | bytes 2097152 | tf_op jit(solution)/shard_map/reshape | solution.py:198
  89.7 3.9 %all-to-all-start.2 = ((bf16[2,128,8,256]{3,2,0,1:T(8,128)(2,1)}), bf16[2,128,8,256]{3,2,0,1:T(8,128)(2,1)S(1)}, u32[]{:S(2)}, u32[]{:S(2)}) async-start(bf16[2,128,8,256]{3,2,0,1:T(8,128)(2,1)} %copy.47), calls=%async_computation.2 | async-start | bytes 2097152 | tf_op jit(solution)/shard_map/all_to_all | solution.py:197
  93.6 0.6 reshape.118.bin_ref
  94.2 0.7 reshape_reshape_squeeze.3.rows_ref
  94.9 18.2 %all-to-all-done.2 = bf16[2,128,8,256]{3,2,0,1:T(8,128)(2,1)S(1)} async-done(((bf16[2,128,8,256]{3,2,0,1:T(8,128)(2,1)}), bf16[2,128,8,256]{3,2,0,1:T(8,128)(2,1)S(1)}, u32[]{:S(2)}, u32[]{:S(2)}) %all-to-all-start.2) | async-done | bytes 1048608 | tf_op jit(solution)/shard_map/all_to_all | solution.py:197
  113.1 1.0 copy.48
  114.2 16.1 %shard_map.155 = bf16[4096,256]{1,0:T(8,128)(2,1)} custom-call(s32[1,2048]{1,0:T(1,128)} %reshape_reshape_squeeze.3.rows_ref, bf16[2048,256]{1,0:T(8,128)(2,1)} %bitcast.29, bf16[4096,256]{1,0:T(8,128)(2,1)} %mem_ref.1, bf16[256,768]{1,0:T(8,128)(2,1)} %win_ref.1, f32[1,768]{1,0:T(1,128)} %reshape.118.bin_ref, bf16[256,768]{1,0:T(8,128)(2,1)} %whid_ref.1), custom_call_target="tpu_custom_call" | custom-call | tf_op jit(solution)/shard_map/pallas_call | solution.py:52
  (28 shorter events, 0.6 us)
Async XLA Ops:
  0.0 55.4 %copy-start = (bf16[512,256]{1,0:T(8,128)(2,1)S(1)}, bf16[512,256]{1,0:T(8,128)(2,1)}, u32[]{:S(2)}) copy-start(bf16[512,256]{1,0:T(8,128)(2,1)} %param.21) | copy-start | bytes 786436
  0.0 19.3 %copy-start.3 = (s32[4096]{0:T(1024)S(1)}, s32[4096]{0:T(1024)}, u32[]{:S(2)}) copy-start(s32[4096]{0:T(1024)} %param.23) | copy-start | bytes 49156
  2.9 28.8 %copy-start.2 = (s32[2,512]{1,0:T(2,128)}, s32[2,512]{1,0:T(2,128)S(1)}, u32[]{:S(2)}) copy-start(s32[2,512]{1,0:T(2,128)S(1)} %get-tuple-element.12.row_ref) | copy-start | bytes 12292
  6.4 28.6 %copy-start.1 = (bf16[4096,256]{1,0:T(8,128)(2,1)S(1)}, bf16[4096,256]{1,0:T(8,128)(2,1)}, u32[]{:S(2)}) copy-start(bf16[4096,256]{1,0:T(8,128)(2,1)} %mem_ref.1) | copy-start | bytes 6291460
  7.3 22.7 %all-to-all-start = ((s32[2,2,128,8]{3,1,0,2:T(2,128)}), s32[2,2,128,8]{3,1,0,2:T(2,128)}, u32[]{:S(2)}, u32[]{:S(2)}) async-start(s32[2,2,128,8]{3,1,0,2:T(2,128)} %copy.37), calls=%async_computation | async-start | bytes 524288 | tf_op jit(solution)/shard_map/all_to_all | solution.py:191
  35.0 9.4 %copy-start.6 = (f32[128]{0:T(128)S(1)}, f32[128]{0:T(128)}, u32[]{:S(2)}) copy-start(f32[128]{0:T(128)} %param.25) | copy-start | bytes 1540
  35.0 9.4 %copy-start.7 = (f32[128]{0:T(128)S(1)}, f32[128]{0:T(128)}, u32[]{:S(2)}) copy-start(f32[128]{0:T(128)} %param.24) | copy-start | bytes 1540
  50.4 5.0 %copy-start.5 = (f32[512]{0:T(512)S(1)}, f32[512]{0:T(512)}, u32[]{:S(2)}) copy-start(f32[512]{0:T(512)} %param.27) | copy-start | bytes 6148
  50.4 29.3 %all-to-all-start.1 = ((bf16[2,128,8,384]{3,2,0,1:T(8,128)(2,1)}), bf16[2,128,8,384]{3,2,0,1:T(8,128)(2,1)S(1)}, u32[]{:S(2)}, u32[]{:S(2)}) async-start(bf16[2,128,8,384]{3,2,0,1:T(8,128)(2,1)} %copy.44), calls=%async_computation.1 | async-start | bytes 3145728 | tf_op jit(solution)/shard_map/all_to_all | solution.py:193
  87.4 6.2 %copy-start.4 = (f32[768]{0:T(1024)S(1)}, f32[768]{0:T(1024)}, u32[]{:S(2)}) copy-start(f32[768]{0:T(1024)} %param.30) | copy-start | bytes 9220
  89.7 23.4 %all-to-all-start.2 = ((bf16[2,128,8,256]{3,2,0,1:T(8,128)(2,1)}), bf16[2,128,8,256]{3,2,0,1:T(8,128)(2,1)S(1)}, u32[]{:S(2)}, u32[]{:S(2)}) async-start(bf16[2,128,8,256]{3,2,0,1:T(8,128)(2,1)} %copy.47), calls=%async_computation.2 | async-start | bytes 2097152 | tf_op jit(solution)/shard_map/all_to_all | solution.py:197

commit v5 on v4

--- a/solution.py
+++ b/solution.py
@@ -67,14 +67,14 @@
 
 def message_kernel(col_ref, row_ref, fetched_ref, edge_ref, w_in_ref, w_out_ref, out_ref):
     events = edge_ref.shape[0]
-    slot_total = fetched_ref.shape[1]
-    width = out_ref.shape[2]
-    time_width = fetched_ref.shape[2] - width
+    slot_total = fetched_ref.shape[0]
+    width = out_ref.shape[1]
+    time_width = fetched_ref.shape[1] - width
     lane_ids = lax.broadcasted_iota(jnp.int32, (events, slot_total), 1)
     picked = []
     for side in range(2):
         pick = (lane_ids == col_ref[:, side : side + 1]).astype(jnp.bfloat16)
-        rows = jnp.dot(pick, fetched_ref[side], preferred_element_type=jnp.float32)
+        rows = jnp.dot(pick, fetched_ref[...], preferred_element_type=jnp.float32)
         picked.append(rows.astype(jnp.bfloat16))
     mem_src, enc_src = picked[0][:, :width], picked[0][:, width:]
     mem_dst, enc_dst = picked[1][:, :width], picked[1][:, width:]
@@ -95,18 +95,18 @@
 
     sent = (message(mem_src, mem_dst, enc_src), message(mem_dst, mem_src, enc_dst))
     sub_ids = lax.broadcasted_iota(jnp.int32, (slot_total, events), 0)
-    for side in range(2):
-        place = (sub_ids == row_ref[side : side + 1, :]).astype(jnp.bfloat16)
-        out_ref[side] = jnp.dot(place, sent[side], preferred_element_type=jnp.float32).astype(out_ref.dtype)
+    placed = [(sub_ids == row_ref[side : side + 1, :]).astype(jnp.bfloat16) for side in range(2)]
+    out = jnp.dot(placed[0], sent[0], preferred_element_type=jnp.float32)
+    out = out + jnp.dot(placed[1], sent[1], preferred_element_type=jnp.float32)
+    out_ref[...] = out.astype(out_ref.dtype)
 
 
 def event_messages(slot_ids, fetched, edge_part, w_msg_in, w_msg_out):
-    sides, slot_total, fetched_width = fetched.shape
-    events, hidden_width = edge_part.shape
+    slot_total = fetched.shape[0]
     msg_width = w_msg_out.shape[1]
     return pl.pallas_call(
         message_kernel,
-        out_shape=jax.ShapeDtypeStruct((sides, slot_total, msg_width), jnp.bfloat16),
+        out_shape=jax.ShapeDtypeStruct((slot_total, msg_width), jnp.bfloat16),
     )(slot_ids.T, slot_ids, fetched, edge_part, w_msg_in, w_msg_out)
 
 
@@ -121,24 +121,18 @@
     return owner_ids * capacity + position
 
 
-def owner_lookup(request_pair, memory, last_update, time_freq, time_phase):
-    row_request = request_pair[0].reshape(-1)
-    time_request = request_pair[1].reshape(-1)
-    rows_count = memory.shape[0]
+def owner_lookup(row_request, time_request, memory, last_update, time_freq, time_phase):
+    rows_count, width = memory.shape
     row_range = jnp.arange(rows_count, dtype=jnp.int32)
     select = (row_request[:, None] == row_range[None, :]).astype(jnp.bfloat16)
     high = (last_update // 64).astype(jnp.bfloat16)
     low = (last_update % 64).astype(jnp.bfloat16)
     table = jnp.concatenate([memory, high[:, None], low[:, None]], axis=1)
     fetched = jnp.dot(select, table, preferred_element_type=jnp.float32)
-    mem_rows = fetched[:, : memory.shape[1]].astype(jnp.bfloat16)
-    stamp = (
-        fetched[:, memory.shape[1]].astype(jnp.int32) * 64
-        + fetched[:, memory.shape[1] + 1].astype(jnp.int32)
-    )
+    mem_rows = fetched[:, :width].astype(jnp.bfloat16)
+    stamp = fetched[:, width].astype(jnp.int32) * 64 + fetched[:, width + 1].astype(jnp.int32)
     encoded = encode(time_request - stamp, time_freq, time_phase)
-    served = jnp.concatenate([mem_rows, encoded], axis=-1)
-    return served.reshape(request_pair.shape[1:] + (served.shape[-1],))
+    return jnp.concatenate([mem_rows, encoded], axis=-1)
 
 
 def local(
@@ -162,48 +156,43 @@
     devices_all = lax.axis_size(("ev", "node"))
     events_here = edge_feat.shape[0]
     capacity = max(2, 2 * events_here // devices_all)
+    chunk = 2 * capacity
     width = memory.shape[1]
     time_width = time_freq.shape[0]
-    hidden_width = w_msg_out.shape[0]
-    msg_width = w_msg_out.shape[1]
-    rows_count = memory.shape[0]
-    slot_total = devices_all * capacity
+    slot_total = devices_all * chunk
     slot_ids = jnp.stack(
         [
-            slot_of(src_owner[:, 0], devices_all, capacity),
-            slot_of(dst_owner[:, 0], devices_all, capacity),
+            slot_of(src_owner[:, 0], devices_all, chunk),
+            slot_of(dst_owner[:, 0], devices_all, chunk) + capacity,
         ]
     )
+    slot_all = slot_ids.reshape(-1)
+    rows_all = jnp.concatenate([src_row, dst_row])
+    times_all = jnp.concatenate([event_time, event_time])
+    digits = jnp.stack(
+        [rows_all // 64, rows_all % 64, times_all // 64, times_all % 64, jnp.ones_like(rows_all)],
+        axis=1,
+    ).astype(jnp.bfloat16)
     slot_range = jnp.arange(slot_total, dtype=jnp.int32)
-    placed = slot_ids[:, None, :] == slot_range[None, :, None]
-    placement = placed.astype(jnp.bfloat16)
-    filled = jnp.any(placed, axis=2)
-    rows_pair = jnp.stack([src_row, dst_row])
-    row_sum = jnp.sum(jnp.where(placed, rows_pair[:, None, :], 0), axis=2)
-    time_sum = jnp.sum(jnp.where(placed, event_time[None, None, :], 0), axis=2)
-    row_request = jnp.where(filled, row_sum, -1)
-    time_request = jnp.where(filled, time_sum, 0)
+    placed = (slot_range[:, None] == slot_all[None, :]).astype(jnp.bfloat16)
+    gathered = jnp.dot(placed, digits, preferred_element_type=jnp.float32).astype(jnp.int32)
+    filled = gathered[:, 4] > 0
+    row_request = jnp.where(filled, gathered[:, 0] * 64 + gathered[:, 1], -1)
+    time_request = gathered[:, 2] * 64 + gathered[:, 3]
+    request = jnp.stack([row_request, time_request]).reshape(2, devices_all, chunk)
+    request = request.transpose(1, 0, 2)
     edge_part = (
         jnp.dot(edge_feat, w_msg_in[2 * width + time_width :], preferred_element_type=jnp.float32)
         + b_msg
     )
-    request = jnp.stack([row_request, time_request]).reshape((2, 2, devices_all, capacity))
-    received = lax.all_to_all(request, ("ev", "node"), split_axis=2, concat_axis=2, tiled=True)
-    served = owner_lookup(received, memory, last_update, time_freq, time_phase)
-    returned = lax.all_to_all(served, ("ev", "node"), split_axis=1, concat_axis=1, tiled=True)
-    rows_held = received[0]
-    fetched_flat = returned.reshape(2, slot_total, width + time_width)
-    outgoing = event_messages(slot_ids, fetched_flat, edge_part, w_msg_in, w_msg_out)
-    arrived = lax.all_to_all(
-        outgoing.reshape(2, devices_all, capacity, msg_width),
-        ("ev", "node"),
-        split_axis=1,
-        concat_axis=1,
-        tiled=True,
-    )
-    row_flat = rows_held.reshape(-1)
-    msg_flat = arrived.reshape(-1, msg_width)
-    return owner_update(row_flat, msg_flat, memory, w_gru_in, b_gru_in, w_gru_hid)
+    received = lax.all_to_all(request, ("ev", "node"), split_axis=0, concat_axis=0, tiled=True)
+    rows_held = received[:, 0, :].reshape(-1)
+    times_held = received[:, 1, :].reshape(-1)
+    served = owner_lookup(rows_held, times_held, memory, last_update, time_freq, time_phase)
+    returned = lax.all_to_all(served, ("ev", "node"), split_axis=0, concat_axis=0, tiled=True)
+    outgoing = event_messages(slot_ids, returned, edge_part, w_msg_in, w_msg_out)
+    arrived = lax.all_to_all(outgoing, ("ev", "node"), split_axis=0, concat_axis=0, tiled=True)
+    return owner_update(rows_held, arrived, memory, w_gru_in, b_gru_in, w_gru_hid)
 
 
 def solution(mesh):

time: 131 us -> 127 us (0.969)
  local copies, waits for them, and re-layouts: 17.3 us -> 12.4 us
  Pallas kernels: 22.6 us -> 24.2 us
  matrix products: 13.5 us -> 15 us
    reshape x2 -> x0, local copies, waits for them, and re-layouts: 3.59 us -> none  [the longest x1 2.29 us: local(): outgoing.reshape(2, devices_all, capacity, msg_width)]
    all_to_all x2 -> x0, local copies, waits for them, and re-layouts: 2.34 us -> none  [the longest x1 1.3 us: local(): lax.all_to_all(served, ('ev', 'node'), split_axis=1, concat_axis=1, tiled...]
    another operation x2 -> x4, other arithmetic: 0.73 us -> 2.92 us  [the longest x1 0.71 us: local(): rows_pair = jnp.stack([src_row, dst_row])]
    unnamed x16 -> x21, local copies, waits for them, and re-layouts: 0.04 us -> 2.15 us
    reduce_sum x1 -> x0, other arithmetic: 2.03 us -> none  [local(): row_sum = jnp.sum(jnp.where(placed, rows_pair[:, None, :], 0), axis=2)]
    slice x4 -> x2, local copies, waits for them, and re-layouts: 3.34 us -> 1.55 us  [the longest x1 1.4 us: local(): times_held = received[:, 1, :].reshape(-1)]
    pallas_call x1, Pallas kernels: 6.48 us -> 8.17 us  [event_messages(): pl.pallas_call(message_kernel, out_shape=jax.ShapeDtypeStruct((slot_total...]
    dot_general x0 -> x1, matrix products: none -> 1.47 us  [local(): jnp.dot(placed, digits, preferred_element_type=jnp.float32)]
where the time goes in v5:
time: 127 us
  waiting for transfers between devices  47.8 us (38%)
  Pallas kernels  24.2 us (19%)
  starting transfers between devices  19.6 us (15%)
  matrix products  15 us (12%)
  local copies, waits for them, and re-layouts  12.4 us (10%)
  other arithmetic  7.61 us (6%)
    all_to_all x1, waiting for transfers between devices, local(): lax.all_to_all(served, ('ev', 'node'), split_axis=0, concat_axis=0, tiled...  22 us
    all_to_all x1, waiting for transfers between devices, local(): lax.all_to_all(outgoing, ('ev', 'node'), split_axis=0, concat_axis=0, til...  18.2 us
    pallas_call x1, Pallas kernels, owner_update(): pl.pallas_call(update_kernel, grid=(rows_count // block,), in_specs=[pl.B...  16.1 us
    all_to_all x1, starting transfers between devices, local(): lax.all_to_all(request, ('ev', 'node'), split_axis=0, concat_axis=0, tile...  11.5 us
    dot_general x1, matrix products, owner_lookup(): fetched = jnp.dot(select, table, preferred_element_type=jnp.float32)  9.11 us
    pallas_call x1, Pallas kernels, event_messages(): pl.pallas_call(message_kernel, out_shape=jax.ShapeDtypeStruct((slot_total...  8.17 us
    all_to_all x1, waiting for transfers between devices, local(): lax.all_to_all(request, ('ev', 'node'), split_axis=0, concat_axis=0, tile...  7.61 us
    all_to_all x1, starting transfers between devices, local(): lax.all_to_all(served, ('ev', 'node'), split_axis=0, concat_axis=0, tiled...  4.28 us
  transfers between devices with their start and end apart: 3, of which 3 were waited for; matrix products, arithmetic and copies ran while one was open for 5% of the time, Pallas kernels for 0%

profile of v5, /device:TPU:1, one launch (start us, length us, event | category | flops | bytes accessed | tf_op | source)
XLA Modules:
  0.0 126.9 jit_solution(3828215021462266348)
XLA Ops:
  0.0 0.8 fusion.27
  0.8 0.7 fusion.29
  1.5 0.8 fusion.30
  2.3 1.1 fusion.10
  3.4 1.1 fusion.11
  4.5 0.7 fusion.31
  5.2 0.6 pad_add_fusion
  5.9 1.5 %fusion.9 = s32[2048,5]{0,1:T(8,128)S(1)} fusion(bf16[1024,5]{0,1:T(8,128)(2,1)S(1)} %stack.8, s32[1024]{0:T(1024)S(1)} %bitcast.41), kind=kOutput, calls=%fused_computation.11 | convolution fusion | flops 23078912 | bytes 55296 | tf_op jit(solution)/shard_map/dot_general | solution.py:178
  7.6 0.8 copy.30
  8.4 11.5 %all-to-all-start = ((s32[128,2,16]{2,1,0:T(2,128)}), s32[128,2,16]{2,1,0:T(2,128)S(1)}, u32[]{:S(2)}, u32[]{:S(2)}) async-start(s32[128,2,16]{2,1,0:T(2,128)} %copy.30), calls=%async_computation | async-start | bytes 262144 | tf_op jit(solution)/shard_map/all_to_all | solution.py:188
  19.9 0.6 broadcast_in_dim.11
  20.5 1.6 %broadcast_in_dim.12 = bf16[4096,1]{1,0:T(8,128)(2,1)} reshape(bf16[4096]{0:T(1024)(128)(2,1)S(1)} %get-tuple-element.15) | data formatting | bytes 16384 | tf_op jit(solution)/shard_map/broadcast_in_dim | solution.py:130
  22.1 7.6 %all-to-all-done = s32[128,2,16]{2,1,0:T(2,128)S(1)} async-done(((s32[128,2,16]{2,1,0:T(2,128)}), s32[128,2,16]{2,1,0:T(2,128)S(1)}, u32[]{:S(2)}, u32[]{:S(2)}) %all-to-all-start) | async-done | bytes 16416 | tf_op jit(solution)/shard_map/all_to_all | solution.py:188
  29.7 1.4 %slice_reduce_fusion = (s32[128,16]{1,0:T(8,128)}, s32[128,16]{1,0:T(8,128)}, s32[128,1,16]{2,1,0:T(1,128)}) fusion(s32[128,2,16]{2,1,0:T(2,128)S(1)} %all-to-all-done), kind=kLoop, calls=%fused_computation.29 | loop fusion | bytes 40960 | tf_op jit(solution)/shard_map/slice | solution.py:190
  31.1 0.9 eq.77
  32.0 0.9 reshape_squeeze.3
  33.0 9.1 %fusion = f32[2048,258]{0,1:T(8,128)S(1)} fusion(s32[2048]{0:T(1024)S(1)} %eq.77, bf16[4096,1]{1,0:T(8,128)(2,1)} %broadcast_in_dim.12, bf16[4096,1]{1,0:T(8,128)(2,1)S(1)} %broadcast_in_dim.11, bf16[4096,256]{1,0:T(8,128)(2,1)S(1)} %copy-done.3), kind=kOutput, calls=%fused_computation.1 | convolution fusion | flops 4343250944 | bytes 4235264 | tf_op jit(solution)/shard_map/dot_general | solution.py:131
  42.1 0.1 slice.87
  42.3 3.7 %cosine_convert_fusion = bf16[2048,128]{0,1:T(8,128)(2,1)S(1)} fusion(f32[128]{0:T(128)S(1)} %copy-done.8, f32[128]{0:T(128)S(1)} %copy-done.9, f32[2048]{0:T(1024)S(1)} %bitcast.32), kind=kLoop, calls=%fused_computation.19 | loop fusion | flops 786432 | bytes 533504 | tf_op jit(solution)/shard_map/convert_element_type | solution.py:10
  46.2 1.6 %copy.33 = bf16[2048,384]{1,0:T(8,128)(2,1)} copy(bf16[2048,384]{0,1:T(8,128)(2,1)S(1)} %pad_maximum_fusion) | data formatting | bytes 3145728 | tf_op jit(solution)/shard_map/concatenate | solution.py:135
  47.8 4.3 %all-to-all-start.1 = ((bf16[128,16,384]{2,1,0:T(8,128)(2,1)}), bf16[128,16,384]{2,1,0:T(8,128)(2,1)S(1)}, u32[]{:S(2)}, u32[]{:S(2)}) async-start(bf16[128,16,384]{2,1,0:T(8,128)(2,1)} %bitcast.12), calls=%async_computation.1 | async-start | bytes 3145728 | tf_op jit(solution)/shard_map/all_to_all | solution.py:192
  52.0 0.9 copy.34.col_ref
  52.9 2.3 %convolution_add_fusion.edge_ref = f32[512,512]{1,0:T(8,128)} fusion(bf16[512,256]{1,0:T(8,128)(2,1)S(1)} %copy-done, f32[512]{0:T(512)S(1)} %copy-done.7, bf16[896,512]{1,0:T(8,128)(2,1)} %w_in_ref.1), kind=kOutput, calls=%fused_computation.14 | convolution fusion | flops 134479872 | bytes 1574912 | tf_op jit(solution)/shard_map/dot_general | solution.py:185
  55.2 22.0 %all-to-all-done.1 = bf16[128,16,384]{2,1,0:T(8,128)(2,1)S(1)} async-done(((bf16[128,16,384]{2,1,0:T(8,128)(2,1)}), bf16[128,16,384]{2,1,0:T(8,128)(2,1)S(1)}, u32[]{:S(2)}, u32[]{:S(2)}) %all-to-all-start.1) | async-done | bytes 1572896 | tf_op jit(solution)/shard_map/all_to_all | solution.py:192
  77.1 1.1 copy-done.1
  78.3 8.2 %shard_map.154 = bf16[2048,256]{1,0:T(8,128)(2,1)} custom-call(s32[512,2]{1,0:T(8,128)} %copy.34.col_ref, s32[2,512]{1,0:T(2,128)} %get-tuple-element.16.row_ref, bf16[2048,384]{1,0:T(8,128)(2,1)} %bitcast.28, f32[512,512]{1,0:T(8,128)} %convolution_add_fusion.edge_ref, bf16[896,512]{1,0:T(8,128)(2,1)} %w_in_ref.1, bf16[512,256]{1,0:T(8,128)(2,1)} %w_out_ref.1), custom_call_target="tpu_custom_call" | custom-call | tf_op jit(solution)/shard_map/pallas_call | solution.py:107
  86.4 3.9 %all-to-all-start.2 = ((bf16[128,16,256]{2,1,0:T(8,128)(2,1)}), bf16[128,16,256]{2,1,0:T(8,128)(2,1)S(1)}, u32[]{:S(2)}, u32[]{:S(2)}) async-start(bf16[128,16,256]{2,1,0:T(8,128)(2,1)} %bitcast.30), calls=%async_computation.2 | async-start | bytes 2097152 | tf_op jit(solution)/shard_map/all_to_all | solution.py:194
  90.3 0.6 reshape.533.bin_ref
  90.9 0.7 reshape_reshape_squeeze.3.rows_ref
  91.6 18.2 %all-to-all-done.2 = bf16[128,16,256]{2,1,0:T(8,128)(2,1)S(1)} async-done(((bf16[128,16,256]{2,1,0:T(8,128)(2,1)}), bf16[128,16,256]{2,1,0:T(8,128)(2,1)S(1)}, u32[]{:S(2)}, u32[]{:S(2)}) %all-to-all-start.2) | async-done | bytes 1048608 | tf_op jit(solution)/shard_map/all_to_all | solution.py:194
  109.8 1.0 copy-done.2
  110.8 16.1 %shard_map.155 = bf16[4096,256]{1,0:T(8,128)(2,1)} custom-call(s32[1,2048]{1,0:T(1,128)} %reshape_reshape_squeeze.3.rows_ref, bf16[2048,256]{1,0:T(8,128)(2,1)} %bitcast.29, bf16[4096,256]{1,0:T(8,128)(2,1)} %mem_ref.1, bf16[256,768]{1,0:T(8,128)(2,1)} %win_ref.1, f32[1,768]{1,0:T(1,128)} %reshape.533.bin_ref, bf16[256,768]{1,0:T(8,128)(2,1)} %whid_ref.1), custom_call_target="tpu_custom_call" | custom-call | tf_op jit(solution)/shard_map/pallas_call | solution.py:52
  (30 shorter events, 0.5 us)
Async XLA Ops:
  0.0 52.9 %copy-start = (bf16[512,256]{1,0:T(8,128)(2,1)S(1)}, bf16[512,256]{1,0:T(8,128)(2,1)}, u32[]{:S(2)}) copy-start(bf16[512,256]{1,0:T(8,128)(2,1)} %param.21) | copy-start | bytes 786436
  5.9 14.0 %copy-start.5 = (s32[4096]{0:T(1024)S(1)}, s32[4096]{0:T(1024)}, u32[]{:S(2)}) copy-start(s32[4096]{0:T(1024)} %param.23) | copy-start | bytes 49156
  7.3 25.6 %copy-start.3 = (bf16[4096,256]{1,0:T(8,128)(2,1)S(1)}, bf16[4096,256]{1,0:T(8,128)(2,1)}, u32[]{:S(2)}) copy-start(bf16[4096,256]{1,0:T(8,128)(2,1)} %mem_ref.1) | copy-start | bytes 6291460
  8.4 21.4 %all-to-all-start = ((s32[128,2,16]{2,1,0:T(2,128)}), s32[128,2,16]{2,1,0:T(2,128)S(1)}, u32[]{:S(2)}, u32[]{:S(2)}) async-start(s32[128,2,16]{2,1,0:T(2,128)} %copy.30), calls=%async_computation | async-start | bytes 262144 | tf_op jit(solution)/shard_map/all_to_all | solution.py:188
  33.0 9.3 %copy-start.8 = (f32[128]{0:T(128)S(1)}, f32[128]{0:T(128)}, u32[]{:S(2)}) copy-start(f32[128]{0:T(128)} %param.25) | copy-start | bytes 1540
  33.0 9.3 %copy-start.9 = (f32[128]{0:T(128)S(1)}, f32[128]{0:T(128)}, u32[]{:S(2)}) copy-start(f32[128]{0:T(128)} %param.24) | copy-start | bytes 1540
  47.8 5.2 %copy-start.7 = (f32[512]{0:T(512)S(1)}, f32[512]{0:T(512)}, u32[]{:S(2)}) copy-start(f32[512]{0:T(512)} %param.27) | copy-start | bytes 6148
  47.8 29.4 %all-to-all-start.1 = ((bf16[128,16,384]{2,1,0:T(8,128)(2,1)}), bf16[128,16,384]{2,1,0:T(8,128)(2,1)S(1)}, u32[]{:S(2)}, u32[]{:S(2)}) async-start(bf16[128,16,384]{2,1,0:T(8,128)(2,1)} %bitcast.12), calls=%async_computation.1 | async-start | bytes 3145728 | tf_op jit(solution)/shard_map/all_to_all | solution.py:192
  77.1 1.1 copy-start.1
  78.3 12.0 %copy-start.6 = (f32[768]{0:T(1024)S(1)}, f32[768]{0:T(1024)}, u32[]{:S(2)}) copy-start(f32[768]{0:T(1024)} %param.30) | copy-start | bytes 9220
  78.3 12.6 %copy-start.4 = (s32[128,16]{1,0:T(8,128)S(1)}, s32[128,16]{1,0:T(8,128)}, u32[]{:S(2)}) copy-start(s32[128,16]{1,0:T(8,128)} %get-tuple-element.6) | copy-start | bytes 24580
  86.4 23.4 %all-to-all-start.2 = ((bf16[128,16,256]{2,1,0:T(8,128)(2,1)}), bf16[128,16,256]{2,1,0:T(8,128)(2,1)S(1)}, u32[]{:S(2)}, u32[]{:S(2)}) async-start(bf16[128,16,256]{2,1,0:T(8,128)(2,1)} %bitcast.30), calls=%async_computation.2 | async-start | bytes 2097152 | tf_op jit(solution)/shard_map/all_to_all | solution.py:194
  109.8 1.0 copy-start.2

commit v6 on v5

--- a/solution.py
+++ b/solution.py
@@ -24,15 +24,18 @@
     return 0.5 + 0.5 * jnp.tanh(0.5 * x)
 
 
-def update_kernel(rows_ref, msg_ref, mem_ref, win_ref, bin_ref, whid_ref, out_ref):
-    block = out_ref.shape[0]
-    slots = rows_ref.shape[1]
+def onehot_kernel(rows_ref, onehot_ref, count_ref):
+    block, slots = onehot_ref.shape
+    ids = pl.program_id(0) * block + lax.broadcasted_iota(jnp.int32, (block, slots), 0)
+    hit = ids == rows_ref[...]
+    onehot_ref[...] = hit.astype(onehot_ref.dtype)
+    count_ref[...] = jnp.sum(hit.astype(jnp.float32), axis=1, keepdims=True)
+
+
+def update_kernel(onehot_ref, count_ref, msg_ref, mem_ref, win_ref, bin_ref, whid_ref, out_ref):
     width = mem_ref.shape[1]
-    ids = pl.program_id(0) * block + lax.broadcasted_iota(jnp.int32, (block, slots), 0)
-    onehot = (ids == rows_ref[...]).astype(jnp.bfloat16)
-    total = jnp.dot(onehot, msg_ref[...], preferred_element_type=jnp.float32)
-    ones = jnp.ones((slots, 128), jnp.bfloat16)
-    count = jnp.dot(onehot, ones, preferred_element_type=jnp.float32)[:, :1]
+    total = jnp.dot(onehot_ref[...], msg_ref[...], preferred_element_type=jnp.float32)
+    count = count_ref[...]
     mean_msg = (total / jnp.maximum(count, 1.0)).astype(jnp.bfloat16)
     state = mem_ref[...]
     input_part = jnp.dot(mean_msg, win_ref[...], preferred_element_type=jnp.float32) + bin_ref[...]
@@ -44,7 +47,28 @@
     out_ref[...] = jnp.where(count > 0, fresh, state.astype(jnp.float32)).astype(out_ref.dtype)
 
 
-def owner_update(row_flat, msg_flat, memory, w_gru_in, b_gru_in, w_gru_hid):
+def row_onehot(row_flat, rows_count):
+    slots = row_flat.shape[0]
+    block = 512
+    return pl.pallas_call(
+        onehot_kernel,
+        grid=(rows_count // block,),
+        in_specs=[pl.BlockSpec((1, slots), lambda i: (0, 0))],
+        out_specs=[
+            pl.BlockSpec((block, slots), lambda i: (i, 0)),
+            pl.BlockSpec((block, 1), lambda i: (i, 0)),
+        ],
+        out_shape=[
+            jax.ShapeDtypeStruct((rows_count, slots), jnp.bfloat16),
+            jax.ShapeDtypeStruct((rows_count, 1), jnp.float32),
+        ],
+        cost_estimate=pl.CostEstimate(
+            flops=4 * rows_count * slots, transcendentals=0, bytes_accessed=2 * rows_count * slots
+        ),
+    )(row_flat.reshape(1, slots))
+
+
+def owner_update(onehot, count, msg_flat, memory, w_gru_in, b_gru_in, w_gru_hid):
     rows_count, width = memory.shape
     slots, msg_width = msg_flat.shape
     block = 1024
@@ -53,7 +77,8 @@
         update_kernel,
         grid=(rows_count // block,),
         in_specs=[
-            pl.BlockSpec((1, slots), lambda i: (0, 0)),
+            pl.BlockSpec((block, slots), lambda i: (i, 0)),
+            pl.BlockSpec((block, 1), lambda i: (i, 0)),
             pl.BlockSpec((slots, msg_width), lambda i: (0, 0)),
             pl.BlockSpec((block, width), lambda i: (i, 0)),
             pl.BlockSpec((msg_width, gates), lambda i: (0, 0)),
@@ -62,7 +87,7 @@
         ],
         out_specs=pl.BlockSpec((block, width), lambda i: (i, 0)),
         out_shape=jax.ShapeDtypeStruct(memory.shape, memory.dtype),
-    )(row_flat.reshape(1, slots), msg_flat, memory, w_gru_in, b_gru_in.reshape(1, gates), w_gru_hid)
+    )(onehot, count, msg_flat, memory, w_gru_in, b_gru_in.reshape(1, gates), w_gru_hid)
 
 
 def message_kernel(col_ref, row_ref, fetched_ref, edge_ref, w_in_ref, w_out_ref, out_ref):
@@ -190,9 +215,10 @@
     times_held = received[:, 1, :].reshape(-1)
     served = owner_lookup(rows_held, times_held, memory, last_update, time_freq, time_phase)
     returned = lax.all_to_all(served, ("ev", "node"), split_axis=0, concat_axis=0, tiled=True)
+    onehot, count = row_onehot(rows_held, memory.shape[0])
     outgoing = event_messages(slot_ids, returned, edge_part, w_msg_in, w_msg_out)
     arrived = lax.all_to_all(outgoing, ("ev", "node"), split_axis=0, concat_axis=0, tiled=True)
-    return owner_update(rows_held, arrived, memory, w_gru_in, b_gru_in, w_gru_hid)
+    return owner_update(onehot, count, arrived, memory, w_gru_in, b_gru_in, w_gru_hid)
 
 
 def solution(mesh):

time: 127 us -> 130 us (1.024)
  Pallas kernels: 24.2 us -> 36.3 us
  waiting for transfers between devices: 47.8 us -> 38.8 us
    all_to_all x1, waiting for transfers between devices: 18.2 us -> 9.18 us  [local(): lax.all_to_all(outgoing, ('ev', 'node'), split_axis=0, concat_axis=0, til...]
    pallas_call x0 -> x1, Pallas kernels: none -> 9.06 us  [row_onehot(): pl.pallas_call(onehot_kernel, grid=(rows_count // block,), in_specs=[pl.B...]
    pallas_call x1, Pallas kernels: 16.1 us -> 19 us  [owner_update(): pl.pallas_call(update_kernel, grid=(rows_count // block,), in_specs=[pl.B...]
  transfers between devices with their start and end apart: 3 -> 3, of which waited for: 3 -> 3; matrix products, arithmetic and copies ran while one was open for 5% -> 5% of each run, Pallas kernels for 0% -> 7%
where the time goes in v6:
time: 130 us
  waiting for transfers between devices  38.8 us (30%)
  Pallas kernels  36.3 us (28%)
  starting transfers between devices  19.5 us (15%)
  matrix products  14.9 us (11%)
  local copies, waits for them, and re-layouts  12.4 us (10%)
  other arithmetic  7.6 us (6%)
    all_to_all x1, waiting for transfers between devices, local(): lax.all_to_all(served, ('ev', 'node'), split_axis=0, concat_axis=0, tiled...  22 us
    pallas_call x1, Pallas kernels, owner_update(): pl.pallas_call(update_kernel, grid=(rows_count // block,), in_specs=[pl.B...  19 us
    all_to_all x1, starting transfers between devices, local(): lax.all_to_all(request, ('ev', 'node'), split_axis=0, concat_axis=0, tile...  11.5 us
    all_to_all x1, waiting for transfers between devices, local(): lax.all_to_all(outgoing, ('ev', 'node'), split_axis=0, concat_axis=0, til...  9.18 us
    dot_general x1, matrix products, owner_lookup(): fetched = jnp.dot(select, table, preferred_element_type=jnp.float32)  9.11 us
    pallas_call x1, Pallas kernels, row_onehot(): pl.pallas_call(onehot_kernel, grid=(rows_count // block,), in_specs=[pl.B...  9.06 us
    pallas_call x1, Pallas kernels, event_messages(): pl.pallas_call(message_kernel, out_shape=jax.ShapeDtypeStruct((slot_total...  8.19 us
    all_to_all x1, waiting for transfers between devices, local(): lax.all_to_all(request, ('ev', 'node'), split_axis=0, concat_axis=0, tile...  7.61 us
  transfers between devices with their start and end apart: 3, of which 3 were waited for; matrix products, arithmetic and copies ran while one was open for 5% of the time, Pallas kernels for 7%

profile of v6, /device:TPU:1, one launch (start us, length us, event | category | flops | bytes accessed | tf_op | source)
XLA Modules:
  0.0 129.7 jit_solution(7414691682588054249)
XLA Ops:
  0.0 1.1 fusion.11
  1.1 1.1 fusion.10
  2.2 0.7 fusion.31
  2.9 0.6 pad_add_fusion
  3.5 0.8 fusion.27
  4.3 0.7 fusion.29
  5.0 0.8 fusion.30
  5.9 1.5 %fusion.9 = s32[2048,5]{0,1:T(8,128)S(1)} fusion(bf16[1024,5]{0,1:T(8,128)(2,1)S(1)} %stack.8, s32[1024]{0:T(1024)S(1)} %bitcast.41), kind=kOutput, calls=%fused_computation.11 | convolution fusion | flops 23078912 | bytes 55296 | tf_op jit(solution)/shard_map/dot_general | solution.py:203
  7.6 0.7 copy.30
  8.3 11.5 %all-to-all-start = ((s32[128,2,16]{2,1,0:T(2,128)}), s32[128,2,16]{2,1,0:T(2,128)S(1)}, u32[]{:S(2)}, u32[]{:S(2)}) async-start(s32[128,2,16]{2,1,0:T(2,128)} %copy.30), calls=%async_computation | async-start | bytes 262144 | tf_op jit(solution)/shard_map/all_to_all | solution.py:213
  19.9 0.6 broadcast_in_dim.11
  20.5 1.6 %broadcast_in_dim.12 = bf16[4096,1]{1,0:T(8,128)(2,1)} reshape(bf16[4096]{0:T(1024)(128)(2,1)S(1)} %get-tuple-element.19) | data formatting | bytes 16384 | tf_op jit(solution)/shard_map/broadcast_in_dim | solution.py:155
  22.1 7.6 %all-to-all-done = s32[128,2,16]{2,1,0:T(2,128)S(1)} async-done(((s32[128,2,16]{2,1,0:T(2,128)}), s32[128,2,16]{2,1,0:T(2,128)S(1)}, u32[]{:S(2)}, u32[]{:S(2)}) %all-to-all-start) | async-done | bytes 16416 | tf_op jit(solution)/shard_map/all_to_all | solution.py:213
  29.7 1.4 %slice_reduce_fusion = (s32[128,16]{1,0:T(8,128)}, s32[128,16]{1,0:T(8,128)}, s32[128,1,16]{2,1,0:T(1,128)}) fusion(s32[128,2,16]{2,1,0:T(2,128)S(1)} %all-to-all-done), kind=kLoop, calls=%fused_computation.29 | loop fusion | bytes 40960 | tf_op jit(solution)/shard_map/slice | solution.py:215
  31.1 0.9 reshape_squeeze.3
  32.0 0.9 eq.77
  33.0 9.1 %fusion = f32[2048,258]{0,1:T(8,128)S(1)} fusion(s32[2048]{0:T(1024)S(1)} %eq.77, bf16[4096,1]{1,0:T(8,128)(2,1)} %broadcast_in_dim.12, bf16[4096,1]{1,0:T(8,128)(2,1)S(1)} %broadcast_in_dim.11, bf16[4096,256]{1,0:T(8,128)(2,1)S(1)} %copy-done.3), kind=kOutput, calls=%fused_computation.1 | convolution fusion | flops 4343250944 | bytes 4235264 | tf_op jit(solution)/shard_map/dot_general | solution.py:156
  42.3 3.7 %cosine_convert_fusion = bf16[2048,128]{0,1:T(8,128)(2,1)S(1)} fusion(f32[128]{0:T(128)S(1)} %copy-done.8, f32[128]{0:T(128)S(1)} %copy-done.9, f32[2048]{0:T(1024)S(1)} %bitcast.32), kind=kLoop, calls=%fused_computation.19 | loop fusion | flops 786432 | bytes 533504 | tf_op jit(solution)/shard_map/convert_element_type | solution.py:10
  46.2 1.6 %copy.33 = bf16[2048,384]{1,0:T(8,128)(2,1)} copy(bf16[2048,384]{0,1:T(8,128)(2,1)S(1)} %pad_maximum_fusion) | data formatting | bytes 3145728 | tf_op jit(solution)/shard_map/concatenate | solution.py:160
  47.7 4.2 %all-to-all-start.1 = ((bf16[128,16,384]{2,1,0:T(8,128)(2,1)}), bf16[128,16,384]{2,1,0:T(8,128)(2,1)S(1)}, u32[]{:S(2)}, u32[]{:S(2)}) async-start(bf16[128,16,384]{2,1,0:T(8,128)(2,1)} %bitcast.12), calls=%async_computation.1 | async-start | bytes 3145728 | tf_op jit(solution)/shard_map/all_to_all | solution.py:217
  51.9 0.8 copy.34.col_ref
  52.8 2.2 %convolution_add_fusion.edge_ref = f32[512,512]{1,0:T(8,128)} fusion(bf16[512,256]{1,0:T(8,128)(2,1)S(1)} %copy-done, f32[512]{0:T(512)S(1)} %copy-done.7, bf16[896,512]{1,0:T(8,128)(2,1)} %w_in_ref.1), kind=kOutput, calls=%fused_computation.14 | convolution fusion | flops 134479872 | bytes 1574912 | tf_op jit(solution)/shard_map/dot_general | solution.py:210
  55.0 22.0 %all-to-all-done.1 = bf16[128,16,384]{2,1,0:T(8,128)(2,1)S(1)} async-done(((bf16[128,16,384]{2,1,0:T(8,128)(2,1)}), bf16[128,16,384]{2,1,0:T(8,128)(2,1)S(1)}, u32[]{:S(2)}, u32[]{:S(2)}) %all-to-all-start.1) | async-done | bytes 1572896 | tf_op jit(solution)/shard_map/all_to_all | solution.py:217
  77.0 1.1 copy-done.1
  78.1 8.2 %shard_map.155 = bf16[2048,256]{1,0:T(8,128)(2,1)} custom-call(s32[512,2]{1,0:T(8,128)} %copy.34.col_ref, s32[2,512]{1,0:T(2,128)} %get-tuple-element.20.row_ref, bf16[2048,384]{1,0:T(8,128)(2,1)} %bitcast.28, f32[512,512]{1,0:T(8,128)} %convolution_add_fusion.edge_ref, bf16[896,512]{1,0:T(8,128)(2,1)} %w_in_ref.1, bf16[512,256]{1,0:T(8,128)(2,1)} %w_out_ref.1), custom_call_target="tpu_custom_call" | custom-call | tf_op jit(solution)/shard_map/pallas_call | solution.py:132
  86.3 3.9 %all-to-all-start.2 = ((bf16[128,16,256]{2,1,0:T(8,128)(2,1)}), bf16[128,16,256]{2,1,0:T(8,128)(2,1)S(1)}, u32[]{:S(2)}, u32[]{:S(2)}) async-start(bf16[128,16,256]{2,1,0:T(8,128)(2,1)} %bitcast.30), calls=%async_computation.2 | async-start | bytes 2097152 | tf_op jit(solution)/shard_map/all_to_all | solution.py:220
  90.2 0.6 reshape.533.bin_ref
  90.8 0.7 reshape_reshape_squeeze.3.rows_ref
  91.5 9.1 %shard_map.154 = (bf16[4096,2048]{1,0:T(8,128)(2,1)}, f32[4096,1]{1,0:T(8,128)}) custom-call(s32[1,2048]{1,0:T(1,128)} %reshape_reshape_squeeze.3.rows_ref), custom_call_target="tpu_custom_call" | custom-call | flops 33554432 | bytes 16777216 | tf_op jit(solution)/shard_map/pallas_call | solution.py:53
  100.5 9.2 %all-to-all-done.2 = bf16[128,16,256]{2,1,0:T(8,128)(2,1)S(1)} async-done(((bf16[128,16,256]{2,1,0:T(8,128)(2,1)}), bf16[128,16,256]{2,1,0:T(8,128)(2,1)S(1)}, u32[]{:S(2)}, u32[]{:S(2)}) %all-to-all-start.2) | async-done | bytes 1048608 | tf_op jit(solution)/shard_map/all_to_all | solution.py:220
  109.7 1.0 copy-done.2
  110.7 19.0 %shard_map.156 = bf16[4096,256]{1,0:T(8,128)(2,1)} custom-call(bf16[4096,2048]{1,0:T(8,128)(2,1)} %get-tuple-element.7.onehot_ref, f32[4096,1]{1,0:T(8,128)} %get-tuple-element.8.count_ref, bf16[2048,256]{1,0:T(8,128)(2,1)} %bitcast.29, bf16[4096,256]{1,0:T(8,128)(2,1)} %mem_ref.1, bf16[256,768]{1,0:T(8,128)(2,1)} %win_ref.1, f32[1,768]{1,0:T(1,128)} %reshape.533.bin_ref, ...), custom_call_target="tpu_custom_call" | custom-call | tf_op jit(solution)/shard_map/pallas_call | solution.py:76
  (31 shorter events, 0.6 us)
Async XLA Ops:
  0.0 52.7 %copy-start = (bf16[512,256]{1,0:T(8,128)(2,1)S(1)}, bf16[512,256]{1,0:T(8,128)(2,1)}, u32[]{:S(2)}) copy-start(bf16[512,256]{1,0:T(8,128)(2,1)} %param.21) | copy-start | bytes 786436
  0.0 19.9 %copy-start.5 = (s32[4096]{0:T(1024)S(1)}, s32[4096]{0:T(1024)}, u32[]{:S(2)}) copy-start(s32[4096]{0:T(1024)} %param.23) | copy-start | bytes 49156
  5.9 27.1 %copy-start.3 = (bf16[4096,256]{1,0:T(8,128)(2,1)S(1)}, bf16[4096,256]{1,0:T(8,128)(2,1)}, u32[]{:S(2)}) copy-start(bf16[4096,256]{1,0:T(8,128)(2,1)} %mem_ref.1) | copy-start | bytes 6291460
  8.3 21.4 %all-to-all-start = ((s32[128,2,16]{2,1,0:T(2,128)}), s32[128,2,16]{2,1,0:T(2,128)S(1)}, u32[]{:S(2)}, u32[]{:S(2)}) async-start(s32[128,2,16]{2,1,0:T(2,128)} %copy.30), calls=%async_computation | async-start | bytes 262144 | tf_op jit(solution)/shard_map/all_to_all | solution.py:213
  32.9 9.3 %copy-start.8 = (f32[128]{0:T(128)S(1)}, f32[128]{0:T(128)}, u32[]{:S(2)}) copy-start(f32[128]{0:T(128)} %param.25) | copy-start | bytes 1540
  33.0 9.3 %copy-start.9 = (f32[128]{0:T(128)S(1)}, f32[128]{0:T(128)}, u32[]{:S(2)}) copy-start(f32[128]{0:T(128)} %param.24) | copy-start | bytes 1540
  46.2 6.6 %copy-start.7 = (f32[512]{0:T(512)S(1)}, f32[512]{0:T(512)}, u32[]{:S(2)}) copy-start(f32[512]{0:T(512)} %param.27) | copy-start | bytes 6148
  47.7 29.2 %all-to-all-start.1 = ((bf16[128,16,384]{2,1,0:T(8,128)(2,1)}), bf16[128,16,384]{2,1,0:T(8,128)(2,1)S(1)}, u32[]{:S(2)}, u32[]{:S(2)}) async-start(bf16[128,16,384]{2,1,0:T(8,128)(2,1)} %bitcast.12), calls=%async_computation.1 | async-start | bytes 3145728 | tf_op jit(solution)/shard_map/all_to_all | solution.py:217
  77.0 1.1 copy-start.1
  78.1 12.1 %copy-start.6 = (f32[768]{0:T(1024)S(1)}, f32[768]{0:T(1024)}, u32[]{:S(2)}) copy-start(f32[768]{0:T(1024)} %param.30) | copy-start | bytes 9220
  78.1 12.7 %copy-start.4 = (s32[128,16]{1,0:T(8,128)S(1)}, s32[128,16]{1,0:T(8,128)}, u32[]{:S(2)}) copy-start(s32[128,16]{1,0:T(8,128)} %get-tuple-element.10) | copy-start | bytes 24580
  86.3 23.4 %all-to-all-start.2 = ((bf16[128,16,256]{2,1,0:T(8,128)(2,1)}), bf16[128,16,256]{2,1,0:T(8,128)(2,1)S(1)}, u32[]{:S(2)}, u32[]{:S(2)}) async-start(bf16[128,16,256]{2,1,0:T(8,128)(2,1)} %bitcast.30), calls=%async_computation.2 | async-start | bytes 2097152 | tf_op jit(solution)/shard_map/all_to_all | solution.py:220
  109.7 1.0 copy-start.2

commit v7 on v5

--- a/solution.py
+++ b/solution.py
@@ -121,18 +121,52 @@
     return owner_ids * capacity + position
 
 
+def lookup_kernel(rows_ref, times_ref, mem_ref, digits_ref, freq_ref, phase_ref, out_ref):
+    block = out_ref.shape[0]
+    rows_count, width = mem_ref.shape
+    lanes = lax.broadcasted_iota(jnp.int32, (block, rows_count), 1)
+    select = (lanes == rows_ref[...]).astype(jnp.bfloat16)
+    mem_rows = jnp.dot(select, mem_ref[...], preferred_element_type=jnp.float32)
+    parts = jnp.dot(select, digits_ref[...], preferred_element_type=jnp.float32)
+    stamp = parts[:, 0:1].astype(jnp.int32) * 64 + parts[:, 1:2].astype(jnp.int32)
+    delta = (times_ref[...] - stamp).astype(jnp.float32)
+    encoded = jnp.cos(delta * freq_ref[...] + phase_ref[...])
+    out_ref[:, :width] = mem_rows.astype(out_ref.dtype)
+    out_ref[:, width:] = encoded.astype(out_ref.dtype)
+
+
 def owner_lookup(row_request, time_request, memory, last_update, time_freq, time_phase):
     rows_count, width = memory.shape
-    row_range = jnp.arange(rows_count, dtype=jnp.int32)
-    select = (row_request[:, None] == row_range[None, :]).astype(jnp.bfloat16)
-    high = (last_update // 64).astype(jnp.bfloat16)
-    low = (last_update % 64).astype(jnp.bfloat16)
-    table = jnp.concatenate([memory, high[:, None], low[:, None]], axis=1)
-    fetched = jnp.dot(select, table, preferred_element_type=jnp.float32)
-    mem_rows = fetched[:, :width].astype(jnp.bfloat16)
-    stamp = fetched[:, width].astype(jnp.int32) * 64 + fetched[:, width + 1].astype(jnp.int32)
-    encoded = encode(time_request - stamp, time_freq, time_phase)
-    return jnp.concatenate([mem_rows, encoded], axis=-1)
+    slots = row_request.shape[0]
+    time_width = time_freq.shape[0]
+    digit_cols = jnp.arange(time_width, dtype=jnp.int32)
+    digits = jnp.where(
+        digit_cols[None, :] == 0,
+        last_update[:, None] // 64,
+        jnp.where(digit_cols[None, :] == 1, last_update[:, None] % 64, 0),
+    ).astype(jnp.bfloat16)
+    block = 512
+    return pl.pallas_call(
+        lookup_kernel,
+        grid=(slots // block,),
+        in_specs=[
+            pl.BlockSpec((block, 1), lambda i: (i, 0)),
+            pl.BlockSpec((block, 1), lambda i: (i, 0)),
+            pl.BlockSpec((rows_count, width), lambda i: (0, 0)),
+            pl.BlockSpec((rows_count, time_width), lambda i: (0, 0)),
+            pl.BlockSpec((1, time_width), lambda i: (0, 0)),
+            pl.BlockSpec((1, time_width), lambda i: (0, 0)),
+        ],
+        out_specs=pl.BlockSpec((block, width + time_width), lambda i: (i, 0)),
+        out_shape=jax.ShapeDtypeStruct((slots, width + time_width), memory.dtype),
+    )(
+        row_request.reshape(slots, 1),
+        time_request.reshape(slots, 1),
+        memory,
+        digits,
+        time_freq.reshape(1, time_width),
+        time_phase.reshape(1, time_width),
+    )
 
 
 def local(

time: 127 us -> 129 us (1.016)
  Pallas kernels: 24.2 us -> 40.2 us
  matrix products: 15 us -> 5.88 us
  local copies, waits for them, and re-layouts: 12.4 us -> 8.81 us
  other arithmetic: 7.61 us -> 6.24 us
    pallas_call x0 -> x1, Pallas kernels: none -> 16 us  [owner_lookup(): pl.pallas_call(lookup_kernel, grid=(slots // block,), in_specs=[pl.BlockS...]
    dot_general x1 -> x0, matrix products: 9.11 us -> none  [owner_lookup(): fetched = jnp.dot(select, table, preferred_element_type=jnp.float32)]
    another operation x1 -> x2, local copies, waits for them, and re-layouts: 0.93 us -> 3.17 us  [the longest x1 1.61 us: owner_lookup(): time_request.reshape(slots, 1)]
    broadcast_in_dim x2 -> x0, local copies, waits for them, and re-layouts: 2.18 us -> none  [owner_lookup(): table = jnp.concatenate([memory, high[:, None], low[:, None]], axis=1)]
    concatenate x1 -> x0, local copies, waits for them, and re-layouts: 1.57 us -> none  [owner_lookup(): return jnp.concatenate([mem_rows, encoded], axis=-1)]
    convert_element_type x3 -> x1, other arithmetic: 3.79 us -> 2.5 us  [owner_lookup(): digits = jnp.where(digit_cols[None, :] == 0, last_update[:, None] // 64,...]
where the time goes in v7:
time: 129 us; the launch traced here: 128 us
  waiting for transfers between devices  47.5 us (37%)
  Pallas kernels  40.2 us (31%)
  starting transfers between devices  19.7 us (15%)
  local copies, waits for them, and re-layouts  8.81 us (7%)
  other arithmetic  6.24 us (5%)
  matrix products  5.88 us (5%)
    all_to_all x1, waiting for transfers between devices, local(): lax.all_to_all(served, ('ev', 'node'), split_axis=0, concat_axis=0, tiled...  21.9 us
    all_to_all x1, waiting for transfers between devices, local(): lax.all_to_all(outgoing, ('ev', 'node'), split_axis=0, concat_axis=0, til...  18.3 us
    pallas_call x1, Pallas kernels, owner_update(): pl.pallas_call(update_kernel, grid=(rows_count // block,), in_specs=[pl.B...  16.1 us
    pallas_call x1, Pallas kernels, owner_lookup(): pl.pallas_call(lookup_kernel, grid=(slots // block,), in_specs=[pl.BlockS...  16 us
    all_to_all x1, starting transfers between devices, local(): lax.all_to_all(request, ('ev', 'node'), split_axis=0, concat_axis=0, tile...  11.5 us
    pallas_call x1, Pallas kernels, event_messages(): pl.pallas_call(message_kernel, out_shape=jax.ShapeDtypeStruct((slot_total...  8.15 us
    all_to_all x1, waiting for transfers between devices, local(): lax.all_to_all(request, ('ev', 'node'), split_axis=0, concat_axis=0, tile...  7.29 us
    all_to_all x1, starting transfers between devices, local(): lax.all_to_all(served, ('ev', 'node'), split_axis=0, concat_axis=0, tiled...  4.27 us
  transfers between devices with their start and end apart: 3, of which 3 were waited for; matrix products, arithmetic and copies ran while one was open for 5% of the time, Pallas kernels for 0%

profile of v7, /device:TPU:1, one launch (start us, length us, event | category | flops | bytes accessed | tf_op | source)
XLA Modules:
  0.0 128.5 jit_solution(4061190650840249740)
XLA Ops:
  0.0 0.8 fusion.14
  0.8 0.7 fusion.16
  1.5 0.8 fusion.17
  2.3 1.1 fusion.3
  3.4 1.1 fusion.4
  4.5 0.7 fusion.18
  5.2 0.6 pad_add_fusion
  5.9 0.0 copy-start.3
  5.9 1.5 %fusion.2 = s32[2048,5]{0,1:T(8,128)S(1)} fusion(bf16[1024,5]{0,1:T(8,128)(2,1)S(1)} %stack.8, s32[1024]{0:T(1024)S(1)} %bitcast.42), kind=kOutput, calls=%fused_computation.3 | convolution fusion | flops 23078912 | bytes 55296 | tf_op jit(solution)/shard_map/dot_general | solution.py:212
  7.3 0.1 fusion.12
  7.4 0.1 add.124
  7.5 0.1 select_n.88
  7.6 0.8 copy.27
  8.4 11.5 %all-to-all-start = ((s32[128,2,16]{2,1,0:T(2,128)}), s32[128,2,16]{2,1,0:T(2,128)S(1)}, u32[]{:S(2)}, u32[]{:S(2)}) async-start(s32[128,2,16]{2,1,0:T(2,128)} %copy.27), calls=%async_computation | async-start | bytes 262144 | tf_op jit(solution)/shard_map/all_to_all | solution.py:222
  19.9 2.5 %select_convert_fusion.digits_ref = bf16[4096,128]{1,0:T(8,128)(2,1)} fusion(s32[4096]{0:T(1024)S(1)} %get-tuple-element.15, s32[4096]{0:T(1024)S(1)} %get-tuple-element.14, pred[128]{0:T(512)(128)(4,1)S(1)} %get-tuple-element.23, pred[128]{0:T(512)(128)(4,1)S(1)} %get-tuple-element.24), kind=kLoop, calls=%fused_computation.4 | loop fusion | flops 1572864 | bytes 1081600 | tf_op jit(solution)/shard_map/convert_element_type | solution.py:147
  22.4 7.3 %all-to-all-done = s32[128,2,16]{2,1,0:T(2,128)S(1)} async-done(((s32[128,2,16]{2,1,0:T(2,128)}), s32[128,2,16]{2,1,0:T(2,128)S(1)}, u32[]{:S(2)}, u32[]{:S(2)}) %all-to-all-start) | async-done | bytes 16416 | tf_op jit(solution)/shard_map/all_to_all | solution.py:222
  29.7 0.4 slice_reduce_fusion
  30.1 1.6 %reshape_reshape_squeeze.12.rows_ref = s32[2048,1]{1,0:T(8,128)} reshape(s32[128,16]{1,0:T(8,128)S(1)} %bitcast.33) | data formatting | bytes 16384 | tf_op jit(solution)/shard_map/reshape;reshape;squeeze | solution.py:163
  31.6 1.6 %reshape_reshape_squeeze.13.times_ref = s32[2048,1]{1,0:T(8,128)} reshape(s32[128,16]{1,0:T(8,128)S(1)} %get-tuple-element.5) | data formatting | bytes 16384 | tf_op jit(solution)/shard_map/reshape;reshape;squeeze | solution.py:164
  33.3 16.0 %shard_map.154 = bf16[2048,384]{1,0:T(8,128)(2,1)} custom-call(s32[2048,1]{1,0:T(8,128)} %reshape_reshape_squeeze.12.rows_ref, s32[2048,1]{1,0:T(8,128)} %reshape_reshape_squeeze.13.times_ref, bf16[4096,256]{1,0:T(8,128)(2,1)} %mem_ref.3, bf16[4096,128]{1,0:T(8,128)(2,1)} %select_convert_fusion.digits_ref, f32[1,128]{1,0:T(1,128)} %bitcast.45, f32[1,128]{1,0:T(1,128)} %bitcast.46), custom_call_target="tpu_custom_call" | custom-call | tf_op jit(solution)/shard_map/pallas_call | solution.py:149
  49.3 4.3 %all-to-all-start.1 = ((bf16[128,16,384]{2,1,0:T(8,128)(2,1)}), bf16[128,16,384]{2,1,0:T(8,128)(2,1)S(1)}, u32[]{:S(2)}, u32[]{:S(2)}) async-start(bf16[128,16,384]{2,1,0:T(8,128)(2,1)} %bitcast.30), calls=%async_computation.1 | async-start | bytes 3145728 | tf_op jit(solution)/shard_map/all_to_all | solution.py:226
  53.5 0.9 copy.30.col_ref
  54.4 2.3 %convolution_add_fusion.edge_ref = f32[512,512]{1,0:T(8,128)} fusion(bf16[512,256]{1,0:T(8,128)(2,1)S(1)} %copy-done, f32[512]{0:T(512)S(1)} %copy-done.5, bf16[896,512]{1,0:T(8,128)(2,1)} %w_in_ref.1), kind=kOutput, calls=%fused_computation.5 | convolution fusion | flops 134479872 | bytes 1574912 | tf_op jit(solution)/shard_map/dot_general | solution.py:219
  56.7 21.9 %all-to-all-done.1 = bf16[128,16,384]{2,1,0:T(8,128)(2,1)S(1)} async-done(((bf16[128,16,384]{2,1,0:T(8,128)(2,1)}), bf16[128,16,384]{2,1,0:T(8,128)(2,1)S(1)}, u32[]{:S(2)}, u32[]{:S(2)}) %all-to-all-start.1) | async-done | bytes 1572896 | tf_op jit(solution)/shard_map/all_to_all | solution.py:226
  78.6 1.1 copy-done.1
  79.8 8.1 %shard_map.155 = bf16[2048,256]{1,0:T(8,128)(2,1)} custom-call(s32[512,2]{1,0:T(8,128)} %copy.30.col_ref, s32[2,512]{1,0:T(2,128)} %get-tuple-element.16.row_ref, bf16[2048,384]{1,0:T(8,128)(2,1)} %bitcast.29, f32[512,512]{1,0:T(8,128)} %convolution_add_fusion.edge_ref, bf16[896,512]{1,0:T(8,128)(2,1)} %w_in_ref.1, bf16[512,256]{1,0:T(8,128)(2,1)} %w_out_ref.1), custom_call_target="tpu_custom_call" | custom-call | tf_op jit(solution)/shard_map/pallas_call | solution.py:107
  87.9 4.0 %all-to-all-start.2 = ((bf16[128,16,256]{2,1,0:T(8,128)(2,1)}), bf16[128,16,256]{2,1,0:T(8,128)(2,1)S(1)}, u32[]{:S(2)}, u32[]{:S(2)}) async-start(bf16[128,16,256]{2,1,0:T(8,128)(2,1)} %bitcast.32), calls=%async_computation.2 | async-start | bytes 2097152 | tf_op jit(solution)/shard_map/all_to_all | solution.py:228
  91.9 0.6 reshape.573.bin_ref
  92.5 0.7 reshape_reshape_squeeze.9.rows_ref
  93.2 18.3 %all-to-all-done.2 = bf16[128,16,256]{2,1,0:T(8,128)(2,1)S(1)} async-done(((bf16[128,16,256]{2,1,0:T(8,128)(2,1)}), bf16[128,16,256]{2,1,0:T(8,128)(2,1)S(1)}, u32[]{:S(2)}, u32[]{:S(2)}) %all-to-all-start.2) | async-done | bytes 1048608 | tf_op jit(solution)/shard_map/all_to_all | solution.py:228
  111.4 1.0 copy-done.2
  112.4 16.1 %shard_map.156 = bf16[4096,256]{1,0:T(8,128)(2,1)} custom-call(s32[1,2048]{1,0:T(1,128)} %reshape_reshape_squeeze.9.rows_ref, bf16[2048,256]{1,0:T(8,128)(2,1)} %bitcast.31, bf16[4096,256]{1,0:T(8,128)(2,1)} %mem_ref.3, bf16[256,768]{1,0:T(8,128)(2,1)} %win_ref.1, f32[1,768]{1,0:T(1,128)} %reshape.573.bin_ref, bf16[256,768]{1,0:T(8,128)(2,1)} %whid_ref.1), custom_call_target="tpu_custom_call" | custom-call | tf_op jit(solution)/shard_map/pallas_call | solution.py:52
  (17 shorter events, 0.1 us)
Async XLA Ops:
  0.0 54.4 %copy-start = (bf16[512,256]{1,0:T(8,128)(2,1)S(1)}, bf16[512,256]{1,0:T(8,128)(2,1)}, u32[]{:S(2)}) copy-start(bf16[512,256]{1,0:T(8,128)(2,1)} %param.21) | copy-start | bytes 786436
  5.9 14.0 %copy-start.3 = (s32[4096]{0:T(1024)S(1)}, s32[4096]{0:T(1024)}, u32[]{:S(2)}) copy-start(s32[4096]{0:T(1024)} %param.23) | copy-start | bytes 49156
  8.4 21.3 %all-to-all-start = ((s32[128,2,16]{2,1,0:T(2,128)}), s32[128,2,16]{2,1,0:T(2,128)S(1)}, u32[]{:S(2)}, u32[]{:S(2)}) async-start(s32[128,2,16]{2,1,0:T(2,128)} %copy.27), calls=%async_computation | async-start | bytes 262144 | tf_op jit(solution)/shard_map/all_to_all | solution.py:222
  49.3 5.2 %copy-start.5 = (f32[512]{0:T(512)S(1)}, f32[512]{0:T(512)}, u32[]{:S(2)}) copy-start(f32[512]{0:T(512)} %param.27) | copy-start | bytes 6148
  49.3 29.4 %all-to-all-start.1 = ((bf16[128,16,384]{2,1,0:T(8,128)(2,1)}), bf16[128,16,384]{2,1,0:T(8,128)(2,1)S(1)}, u32[]{:S(2)}, u32[]{:S(2)}) async-start(bf16[128,16,384]{2,1,0:T(8,128)(2,1)} %bitcast.30), calls=%async_computation.1 | async-start | bytes 3145728 | tf_op jit(solution)/shard_map/all_to_all | solution.py:226
  78.6 1.1 copy-start.1
  87.9 4.0 %copy-start.4 = (f32[768]{0:T(1024)S(1)}, f32[768]{0:T(1024)}, u32[]{:S(2)}) copy-start(f32[768]{0:T(1024)} %param.30) | copy-start | bytes 9220
  87.9 23.5 %all-to-all-start.2 = ((bf16[128,16,256]{2,1,0:T(8,128)(2,1)}), bf16[128,16,256]{2,1,0:T(8,128)(2,1)S(1)}, u32[]{:S(2)}, u32[]{:S(2)}) async-start(bf16[128,16,256]{2,1,0:T(8,128)(2,1)} %bitcast.32), calls=%async_computation.2 | async-start | bytes 2097152 | tf_op jit(solution)/shard_map/all_to_all | solution.py:228
  111.4 1.0 copy-start.2

commit v8 on v5

--- a/solution.py
+++ b/solution.py
@@ -101,13 +101,67 @@
     out_ref[...] = out.astype(out_ref.dtype)
 
 
-def event_messages(slot_ids, fetched, edge_part, w_msg_in, w_msg_out):
+def event_messages(slot_ids, slot_cols, fetched, edge_part, w_msg_in, w_msg_out):
     slot_total = fetched.shape[0]
     msg_width = w_msg_out.shape[1]
     return pl.pallas_call(
         message_kernel,
         out_shape=jax.ShapeDtypeStruct((slot_total, msg_width), jnp.bfloat16),
-    )(slot_ids.T, slot_ids, fetched, edge_part, w_msg_in, w_msg_out)
+    )(slot_cols, slot_ids, fetched, edge_part, w_msg_in, w_msg_out)
+
+
+def prologue_kernel(owner_ref, rows_ref, time_ref, slot_ref, slot_t_ref, request_ref):
+    events = owner_ref.shape[1]
+    owners = 128
+    capacity = 8
+    slot_total = request_ref.shape[1]
+    chunk = slot_total // owners
+    upper = (
+        lax.broadcasted_iota(jnp.int32, (events, events), 0)
+        < lax.broadcasted_iota(jnp.int32, (events, events), 1)
+    ).astype(jnp.bfloat16)
+    owner_ids = lax.broadcasted_iota(jnp.int32, (owners, events), 0)
+    slots = []
+    for side in range(2):
+        owner_row = owner_ref[side : side + 1, :]
+        onehot = owner_ids == owner_row
+        earlier = jnp.dot(onehot.astype(jnp.bfloat16), upper, preferred_element_type=jnp.float32)
+        position = jnp.sum(jnp.where(onehot, earlier, 0.0), axis=0, keepdims=True)
+        slots.append(owner_row * chunk + side * capacity + position.astype(jnp.int32))
+    slot_all = jnp.concatenate(slots, axis=1)
+    rows_all = jnp.concatenate([rows_ref[0:1, :], rows_ref[1:2, :]], axis=1)
+    times_all = jnp.concatenate([time_ref[...], time_ref[...]], axis=1)
+    zero = jnp.zeros_like(rows_all)
+    digits = jnp.concatenate(
+        [rows_all // 64, rows_all % 64, times_all // 64, times_all % 64, zero + 1, zero, zero, zero],
+        axis=0,
+    ).astype(jnp.float32)
+    stacked = jnp.concatenate([slot_all] + [jnp.zeros_like(slot_all)] * 7, axis=0)
+    columns = jnp.transpose(stacked)
+    slot_col = columns[:, 0:1]
+    lanes = lax.broadcasted_iota(jnp.int32, (2 * events, slot_total), 1)
+    placed = (lanes == slot_col).astype(jnp.bfloat16)
+    got = jnp.dot(digits.astype(jnp.bfloat16), placed, preferred_element_type=jnp.float32)
+    got = got.astype(jnp.int32)
+    row_request = jnp.where(got[4:5] > 0, got[0:1] * 64 + got[1:2], -1)
+    time_request = got[2:3] * 64 + got[3:4]
+    request_ref[...] = jnp.concatenate([row_request, time_request], axis=0)
+    slot_ref[...] = jnp.concatenate(slots, axis=0)
+    slot_t_ref[...] = jnp.concatenate([columns[:events, 0:1], columns[events:, 0:1]], axis=1)
+
+
+def build_requests(src_owner, src_row, dst_owner, dst_row, event_time, slot_total):
+    events = src_row.shape[0]
+    owner_pair = jnp.concatenate([src_owner, dst_owner], axis=1).T
+    rows_pair = jnp.stack([src_row, dst_row])
+    return pl.pallas_call(
+        prologue_kernel,
+        out_shape=[
+            jax.ShapeDtypeStruct((2, events), jnp.int32),
+            jax.ShapeDtypeStruct((events, 2), jnp.int32),
+            jax.ShapeDtypeStruct((2, slot_total), jnp.int32),
+        ],
+    )(owner_pair, rows_pair, event_time.reshape(1, events))
 
 
 def slot_of(owner_ids, owner_count, capacity):
@@ -160,27 +214,10 @@
     width = memory.shape[1]
     time_width = time_freq.shape[0]
     slot_total = devices_all * chunk
-    slot_ids = jnp.stack(
-        [
-            slot_of(src_owner[:, 0], devices_all, chunk),
-            slot_of(dst_owner[:, 0], devices_all, chunk) + capacity,
-        ]
+    slot_ids, slot_cols, request = build_requests(
+        src_owner, src_row, dst_owner, dst_row, event_time, slot_total
     )
-    slot_all = slot_ids.reshape(-1)
-    rows_all = jnp.concatenate([src_row, dst_row])
-    times_all = jnp.concatenate([event_time, event_time])
-    digits = jnp.stack(
-        [rows_all // 64, rows_all % 64, times_all // 64, times_all % 64, jnp.ones_like(rows_all)],
-        axis=1,
-    ).astype(jnp.bfloat16)
-    slot_range = jnp.arange(slot_total, dtype=jnp.int32)
-    placed = (slot_range[:, None] == slot_all[None, :]).astype(jnp.bfloat16)
-    gathered = jnp.dot(placed, digits, preferred_element_type=jnp.float32).astype(jnp.int32)
-    filled = gathered[:, 4] > 0
-    row_request = jnp.where(filled, gathered[:, 0] * 64 + gathered[:, 1], -1)
-    time_request = gathered[:, 2] * 64 + gathered[:, 3]
-    request = jnp.stack([row_request, time_request]).reshape(2, devices_all, chunk)
-    request = request.transpose(1, 0, 2)
+    request = request.reshape(2, devices_all, chunk).transpose(1, 0, 2)
     edge_part = (
         jnp.dot(edge_feat, w_msg_in[2 * width + time_width :], preferred_element_type=jnp.float32)
         + b_msg
@@ -190,7 +227,7 @@
     times_held = received[:, 1, :].reshape(-1)
     served = owner_lookup(rows_held, times_held, memory, last_update, time_freq, time_phase)
     returned = lax.all_to_all(served, ("ev", "node"), split_axis=0, concat_axis=0, tiled=True)
-    outgoing = event_messages(slot_ids, returned, edge_part, w_msg_in, w_msg_out)
+    outgoing = event_messages(slot_ids, slot_cols, returned, edge_part, w_msg_in, w_msg_out)
     arrived = lax.all_to_all(outgoing, ("ev", "node"), split_axis=0, concat_axis=0, tiled=True)
     return owner_update(rows_held, arrived, memory, w_gru_in, b_gru_in, w_gru_hid)
 

time: 127 us -> 126 us (level)
  matrix products: 15 us -> 11.3 us
  Pallas kernels: 24.2 us -> 26.9 us
    dot_general x3 -> x0, matrix products: 3.6 us -> none  [the longest x2 2.13 us: slot_of(): earlier = jnp.dot(lower, onehot, preferred_element_type=jnp.float32)]
    pallas_call x0 -> x1, Pallas kernels: none -> 2.65 us  [build_requests(): pl.pallas_call(prologue_kernel, out_shape=[jax.ShapeDtypeStruct((2, event...]
    another operation x4 -> x1, other arithmetic: 2.92 us -> 1.28 us  [build_requests(): rows_pair = jnp.stack([src_row, dst_row])]
    transpose x1, other arithmetic: 0.01 us -> 1.45 us  [build_requests(): owner_pair = jnp.concatenate([src_owner, dst_owner], axis=1).T]
where the time goes in v8:
time: 126 us; the launch traced here: 125 us
  waiting for transfers between devices  48 us (38%)
  Pallas kernels  26.9 us (21%)
  starting transfers between devices  19.6 us (16%)
  local copies, waits for them, and re-layouts  12.1 us (10%)
  matrix products  11.3 us (9%)
  other arithmetic  7.34 us (6%)
    all_to_all x1, waiting for transfers between devices, local(): lax.all_to_all(served, ('ev', 'node'), split_axis=0, concat_axis=0, tiled...  22.8 us
    all_to_all x1, waiting for transfers between devices, local(): lax.all_to_all(outgoing, ('ev', 'node'), split_axis=0, concat_axis=0, til...  18.2 us
    pallas_call x1, Pallas kernels, owner_update(): pl.pallas_call(update_kernel, grid=(rows_count // block,), in_specs=[pl.B...  16.1 us
    all_to_all x1, starting transfers between devices, local(): lax.all_to_all(request, ('ev', 'node'), split_axis=0, concat_axis=0, tile...  11.5 us
    dot_general x1, matrix products, owner_lookup(): fetched = jnp.dot(select, table, preferred_element_type=jnp.float32)  9.1 us
    pallas_call x1, Pallas kernels, event_messages(): pl.pallas_call(message_kernel, out_shape=jax.ShapeDtypeStruct((slot_total...  8.18 us
    all_to_all x1, waiting for transfers between devices, local(): lax.all_to_all(request, ('ev', 'node'), split_axis=0, concat_axis=0, tile...  6.91 us
    all_to_all x1, starting transfers between devices, local(): lax.all_to_all(served, ('ev', 'node'), split_axis=0, concat_axis=0, tiled...  4.28 us
  transfers between devices with their start and end apart: 3, of which 3 were waited for; matrix products, arithmetic and copies ran while one was open for 5% of the time, Pallas kernels for 0%

profile of v8, /device:TPU:1, one launch (start us, length us, event | category | flops | bytes accessed | tf_op | source)
XLA Modules:
  0.0 125.5 jit_solution(1916540660931251375)
XLA Ops:
  0.0 1.4 %add_bitcast_fusion.owner_ref = s32[2,512]{1,0:T(2,128)} fusion(s32[512,1]{0,1:T(1,128)} %param.18, s32[512,1]{0,1:T(1,128)} %param.16), kind=kLoop, calls=%fused_computation.30 | loop fusion | flops 1024 | bytes 8192 | tf_op jit(solution)/shard_map/transpose | solution.py:155
  1.5 1.3 %pad_add_fusion.rows_ref = s32[2,512]{1,0:T(2,128)} fusion(s32[1,512]{1,0:T(1,128)} %bitcast.20, s32[1,512]{1,0:T(1,128)} %bitcast.21), kind=kLoop, calls=%fused_computation.31 | loop fusion | flops 1024 | bytes 8192 | tf_op jit(solution)/shard_map/stack | solution.py:156
  2.7 2.6 %shard_map.154 = (s32[2,512]{1,0:T(2,128)}, s32[512,2]{1,0:T(8,128)}, s32[2,2048]{1,0:T(2,128)}) custom-call(s32[2,512]{1,0:T(2,128)} %add_bitcast_fusion.owner_ref, s32[2,512]{1,0:T(2,128)} %pad_add_fusion.rows_ref, s32[1,512]{1,0:T(1,128)} %bitcast.19), custom_call_target="tpu_custom_call" | custom-call | tf_op jit(solution)/shard_map/pallas_call | solution.py:157
  5.4 0.8 reshape.19
  6.2 0.8 copy.21
  7.0 11.5 %all-to-all-start = ((s32[128,2,16]{2,1,0:T(2,128)}), s32[128,2,16]{2,1,0:T(2,128)S(1)}, u32[]{:S(2)}, u32[]{:S(2)}) async-start(s32[128,2,16]{2,1,0:T(2,128)} %copy.21), calls=%async_computation | async-start | bytes 262144 | tf_op jit(solution)/shard_map/all_to_all | solution.py:225
  18.5 0.7 fusion.8
  19.2 0.6 broadcast_in_dim.14
  19.8 1.6 %broadcast_in_dim.6 = bf16[4096,1]{1,0:T(8,128)(2,1)} reshape(bf16[4096]{0:T(1024)(128)(2,1)S(1)} %get-tuple-element.14) | data formatting | bytes 16384 | tf_op jit(solution)/shard_map/broadcast_in_dim | solution.py:184
  21.4 6.9 %all-to-all-done = s32[128,2,16]{2,1,0:T(2,128)S(1)} async-done(((s32[128,2,16]{2,1,0:T(2,128)}), s32[128,2,16]{2,1,0:T(2,128)S(1)}, u32[]{:S(2)}, u32[]{:S(2)}) %all-to-all-start) | async-done | bytes 16416 | tf_op jit(solution)/shard_map/all_to_all | solution.py:225
  28.3 1.4 %slice_reduce_fusion = (s32[128,16]{1,0:T(8,128)}, s32[128,16]{1,0:T(8,128)}, s32[128,1,16]{2,1,0:T(1,128)}) fusion(s32[128,2,16]{2,1,0:T(2,128)S(1)} %all-to-all-done), kind=kLoop, calls=%fused_computation.13 | loop fusion | bytes 40960 | tf_op jit(solution)/shard_map/slice | solution.py:227
  29.7 0.9 reshape_squeeze.3
  30.6 0.9 eq.17
  31.6 0.0 copy-start.7
  31.6 0.0 copy-start.8
  31.6 9.1 %fusion = f32[2048,258]{0,1:T(8,128)S(1)} fusion(s32[2048]{0:T(1024)S(1)} %eq.17, bf16[4096,1]{1,0:T(8,128)(2,1)S(1)} %broadcast_in_dim.14, bf16[4096,1]{1,0:T(8,128)(2,1)} %broadcast_in_dim.6, bf16[4096,256]{1,0:T(8,128)(2,1)S(1)} %copy-done.3), kind=kOutput, calls=%fused_computation.1 | convolution fusion | flops 4343250944 | bytes 4235264 | tf_op jit(solution)/shard_map/dot_general | solution.py:185
  40.7 0.1 slice.49
  40.9 3.7 %cosine_convert_fusion = bf16[2048,128]{0,1:T(8,128)(2,1)S(1)} fusion(f32[128]{0:T(128)S(1)} %copy-done.7, f32[128]{0:T(128)S(1)} %copy-done.8, f32[2048]{0:T(1024)S(1)} %bitcast.18), kind=kLoop, calls=%fused_computation.11 | loop fusion | flops 786432 | bytes 533504 | tf_op jit(solution)/shard_map/convert_element_type | solution.py:10
  44.7 0.1 pad_maximum_fusion
  44.8 1.6 %copy.24 = bf16[2048,384]{1,0:T(8,128)(2,1)} copy(bf16[2048,384]{0,1:T(8,128)(2,1)S(1)} %pad_maximum_fusion) | data formatting | bytes 3145728 | tf_op jit(solution)/shard_map/concatenate | solution.py:189
  46.3 4.3 %all-to-all-start.1 = ((bf16[128,16,384]{2,1,0:T(8,128)(2,1)}), bf16[128,16,384]{2,1,0:T(8,128)(2,1)S(1)}, u32[]{:S(2)}, u32[]{:S(2)}) async-start(bf16[128,16,384]{2,1,0:T(8,128)(2,1)} %bitcast.6), calls=%async_computation.1 | async-start | bytes 3145728 | tf_op jit(solution)/shard_map/all_to_all | solution.py:229
  50.6 0.0 copy-done
  50.7 2.2 %convolution_add_fusion.edge_ref = f32[512,512]{1,0:T(8,128)} fusion(bf16[512,256]{1,0:T(8,128)(2,1)S(1)} %copy-done, f32[512]{0:T(512)S(1)} %copy-done.6, bf16[896,512]{1,0:T(8,128)(2,1)} %w_in_ref.1), kind=kOutput, calls=%fused_computation.10 | convolution fusion | flops 134479872 | bytes 1574912 | tf_op jit(solution)/shard_map/dot_general | solution.py:222
  52.9 22.8 %all-to-all-done.1 = bf16[128,16,384]{2,1,0:T(8,128)(2,1)S(1)} async-done(((bf16[128,16,384]{2,1,0:T(8,128)(2,1)}), bf16[128,16,384]{2,1,0:T(8,128)(2,1)S(1)}, u32[]{:S(2)}, u32[]{:S(2)}) %all-to-all-start.1) | async-done | bytes 1572896 | tf_op jit(solution)/shard_map/all_to_all | solution.py:229
  75.7 1.1 copy-done.1
  76.9 8.2 %shard_map.155 = bf16[2048,256]{1,0:T(8,128)(2,1)} custom-call(s32[512,2]{1,0:T(8,128)} %get-tuple-element.9.col_ref, s32[2,512]{1,0:T(2,128)} %get-tuple-element.10.row_ref, bf16[2048,384]{1,0:T(8,128)(2,1)} %bitcast.13, f32[512,512]{1,0:T(8,128)} %convolution_add_fusion.edge_ref, bf16[896,512]{1,0:T(8,128)(2,1)} %w_in_ref.1, bf16[512,256]{1,0:T(8,128)(2,1)} %w_out_ref.1), custom_call_target="tpu_custom_call" | custom-call | tf_op jit(solution)/shard_map/pallas_call | solution.py:107
  85.0 3.9 %all-to-all-start.2 = ((bf16[128,16,256]{2,1,0:T(8,128)(2,1)}), bf16[128,16,256]{2,1,0:T(8,128)(2,1)S(1)}, u32[]{:S(2)}, u32[]{:S(2)}) async-start(bf16[128,16,256]{2,1,0:T(8,128)(2,1)} %bitcast.15), calls=%async_computation.2 | async-start | bytes 2097152 | tf_op jit(solution)/shard_map/all_to_all | solution.py:231
  88.9 0.6 reshape.20.bin_ref
  89.5 0.7 reshape_reshape_squeeze.3.rows_ref
  90.2 18.2 %all-to-all-done.2 = bf16[128,16,256]{2,1,0:T(8,128)(2,1)S(1)} async-done(((bf16[128,16,256]{2,1,0:T(8,128)(2,1)}), bf16[128,16,256]{2,1,0:T(8,128)(2,1)S(1)}, u32[]{:S(2)}, u32[]{:S(2)}) %all-to-all-start.2) | async-done | bytes 1048608 | tf_op jit(solution)/shard_map/all_to_all | solution.py:231
  108.4 1.0 copy-done.2
  109.4 16.1 %shard_map.156 = bf16[4096,256]{1,0:T(8,128)(2,1)} custom-call(s32[1,2048]{1,0:T(1,128)} %reshape_reshape_squeeze.3.rows_ref, bf16[2048,256]{1,0:T(8,128)(2,1)} %bitcast.14, bf16[4096,256]{1,0:T(8,128)(2,1)} %mem_ref.1, bf16[256,768]{1,0:T(8,128)(2,1)} %win_ref.1, f32[1,768]{1,0:T(1,128)} %reshape.20.bin_ref, bf16[256,768]{1,0:T(8,128)(2,1)} %whid_ref.1), custom_call_target="tpu_custom_call" | custom-call | tf_op jit(solution)/shard_map/pallas_call | solution.py:52
  (14 shorter events, 0.1 us)
Async XLA Ops:
  0.0 50.6 %copy-start = (bf16[512,256]{1,0:T(8,128)(2,1)S(1)}, bf16[512,256]{1,0:T(8,128)(2,1)}, u32[]{:S(2)}) copy-start(bf16[512,256]{1,0:T(8,128)(2,1)} %param.21) | copy-start | bytes 786436
  0.0 31.6 %copy-start.3 = (bf16[4096,256]{1,0:T(8,128)(2,1)S(1)}, bf16[4096,256]{1,0:T(8,128)(2,1)}, u32[]{:S(2)}) copy-start(bf16[4096,256]{1,0:T(8,128)(2,1)} %mem_ref.1) | copy-start | bytes 6291460
  7.0 21.3 %all-to-all-start = ((s32[128,2,16]{2,1,0:T(2,128)}), s32[128,2,16]{2,1,0:T(2,128)S(1)}, u32[]{:S(2)}, u32[]{:S(2)}) async-start(s32[128,2,16]{2,1,0:T(2,128)} %copy.21), calls=%async_computation | async-start | bytes 262144 | tf_op jit(solution)/shard_map/all_to_all | solution.py:225
  31.6 9.3 %copy-start.7 = (f32[128]{0:T(128)S(1)}, f32[128]{0:T(128)}, u32[]{:S(2)}) copy-start(f32[128]{0:T(128)} %param.25) | copy-start | bytes 1540
  31.6 9.3 %copy-start.8 = (f32[128]{0:T(128)S(1)}, f32[128]{0:T(128)}, u32[]{:S(2)}) copy-start(f32[128]{0:T(128)} %param.24) | copy-start | bytes 1540
  46.3 4.3 %copy-start.6 = (f32[512]{0:T(512)S(1)}, f32[512]{0:T(512)}, u32[]{:S(2)}) copy-start(f32[512]{0:T(512)} %param.27) | copy-start | bytes 6148
  46.3 29.4 %all-to-all-start.1 = ((bf16[128,16,384]{2,1,0:T(8,128)(2,1)}), bf16[128,16,384]{2,1,0:T(8,128)(2,1)S(1)}, u32[]{:S(2)}, u32[]{:S(2)}) async-start(bf16[128,16,384]{2,1,0:T(8,128)(2,1)} %bitcast.6), calls=%async_computation.1 | async-start | bytes 3145728 | tf_op jit(solution)/shard_map/all_to_all | solution.py:229
  75.7 1.1 copy-start.1
  76.9 12.0 %copy-start.5 = (f32[768]{0:T(1024)S(1)}, f32[768]{0:T(1024)}, u32[]{:S(2)}) copy-start(f32[768]{0:T(1024)} %param.30) | copy-start | bytes 9220
  76.9 12.6 %copy-start.4 = (s32[128,16]{1,0:T(8,128)S(1)}, s32[128,16]{1,0:T(8,128)}, u32[]{:S(2)}) copy-start(s32[128,16]{1,0:T(8,128)} %get-tuple-element.12) | copy-start | bytes 24580
  85.0 23.4 %all-to-all-start.2 = ((bf16[128,16,256]{2,1,0:T(8,128)(2,1)}), bf16[128,16,256]{2,1,0:T(8,128)(2,1)S(1)}, u32[]{:S(2)}, u32[]{:S(2)}) async-start(bf16[128,16,256]{2,1,0:T(8,128)(2,1)} %bitcast.15), calls=%async_computation.2 | async-start | bytes 2097152 | tf_op jit(solution)/shard_map/all_to_all | solution.py:231
  108.4 1.0 copy-start.2

commit v9 on v8

--- a/solution.py
+++ b/solution.py
@@ -110,35 +110,37 @@
     )(slot_cols, slot_ids, fetched, edge_part, w_msg_in, w_msg_out)
 
 
-def prologue_kernel(owner_ref, rows_ref, time_ref, slot_ref, slot_t_ref, request_ref):
-    events = owner_ref.shape[1]
-    owners = 128
+def prologue_kernel(
+    src_owner_ref, dst_owner_ref, src_row_ref, dst_row_ref, time_ref, slot_ref, slot_t_ref, request_ref
+):
+    events = src_owner_ref.shape[0]
+    slot_total = request_ref.shape[1]
     capacity = 8
-    slot_total = request_ref.shape[1]
-    chunk = slot_total // owners
-    upper = (
+    owners = slot_total // (2 * capacity)
+    chunk = 2 * capacity
+    lower = (
         lax.broadcasted_iota(jnp.int32, (events, events), 0)
-        < lax.broadcasted_iota(jnp.int32, (events, events), 1)
+        > lax.broadcasted_iota(jnp.int32, (events, events), 1)
     ).astype(jnp.bfloat16)
-    owner_ids = lax.broadcasted_iota(jnp.int32, (owners, events), 0)
-    slots = []
-    for side in range(2):
-        owner_row = owner_ref[side : side + 1, :]
-        onehot = owner_ids == owner_row
-        earlier = jnp.dot(onehot.astype(jnp.bfloat16), upper, preferred_element_type=jnp.float32)
-        position = jnp.sum(jnp.where(onehot, earlier, 0.0), axis=0, keepdims=True)
-        slots.append(owner_row * chunk + side * capacity + position.astype(jnp.int32))
-    slot_all = jnp.concatenate(slots, axis=1)
-    rows_all = jnp.concatenate([rows_ref[0:1, :], rows_ref[1:2, :]], axis=1)
+    owner_ids = lax.broadcasted_iota(jnp.int32, (events, owners), 1)
+    columns = []
+    for side, owner_ref in enumerate((src_owner_ref, dst_owner_ref)):
+        owner_col = owner_ref[...]
+        onehot = owner_ids == owner_col
+        earlier = jnp.dot(lower, onehot.astype(jnp.bfloat16), preferred_element_type=jnp.float32)
+        position = jnp.sum(jnp.where(onehot, earlier, 0.0), axis=1, keepdims=True)
+        columns.append(owner_col * chunk + side * capacity + position.astype(jnp.int32))
+    slot_t_ref[...] = jnp.concatenate(columns, axis=1)
+    padded = jnp.concatenate(columns + [jnp.zeros_like(columns[0])] * 6, axis=1)
+    slot_ref[...] = jnp.transpose(padded)[0:2, :]
+    slot_col = jnp.concatenate(columns, axis=0)
+    rows_all = jnp.concatenate([src_row_ref[...], dst_row_ref[...]], axis=1)
     times_all = jnp.concatenate([time_ref[...], time_ref[...]], axis=1)
     zero = jnp.zeros_like(rows_all)
     digits = jnp.concatenate(
         [rows_all // 64, rows_all % 64, times_all // 64, times_all % 64, zero + 1, zero, zero, zero],
         axis=0,
     ).astype(jnp.float32)
-    stacked = jnp.concatenate([slot_all] + [jnp.zeros_like(slot_all)] * 7, axis=0)
-    columns = jnp.transpose(stacked)
-    slot_col = columns[:, 0:1]
     lanes = lax.broadcasted_iota(jnp.int32, (2 * events, slot_total), 1)
     placed = (lanes == slot_col).astype(jnp.bfloat16)
     got = jnp.dot(digits.astype(jnp.bfloat16), placed, preferred_element_type=jnp.float32)
@@ -146,14 +148,10 @@
     row_request = jnp.where(got[4:5] > 0, got[0:1] * 64 + got[1:2], -1)
     time_request = got[2:3] * 64 + got[3:4]
     request_ref[...] = jnp.concatenate([row_request, time_request], axis=0)
-    slot_ref[...] = jnp.concatenate(slots, axis=0)
-    slot_t_ref[...] = jnp.concatenate([columns[:events, 0:1], columns[events:, 0:1]], axis=1)
 
 
 def build_requests(src_owner, src_row, dst_owner, dst_row, event_time, slot_total):
     events = src_row.shape[0]
-    owner_pair = jnp.concatenate([src_owner, dst_owner], axis=1).T
-    rows_pair = jnp.stack([src_row, dst_row])
     return pl.pallas_call(
         prologue_kernel,
         out_shape=[
@@ -161,7 +159,13 @@
             jax.ShapeDtypeStruct((events, 2), jnp.int32),
             jax.ShapeDtypeStruct((2, slot_total), jnp.int32),
         ],
-    )(owner_pair, rows_pair, event_time.reshape(1, events))
+    )(
+        src_owner,
+        dst_owner,
+        src_row.reshape(1, events),
+        dst_row.reshape(1, events),
+        event_time.reshape(1, events),
+    )
 
 
 def slot_of(owner_ids, owner_count, capacity):

time: 126 us -> 127 us (level)
  local copies, waits for them, and re-layouts: 12.1 us -> 15.4 us
  other arithmetic: 7.34 us -> 4.62 us
    unnamed x18 -> x20, local copies, waits for them, and re-layouts: 2.15 us -> 5.37 us
    transpose x1 -> x0, other arithmetic: 1.45 us -> none  [build_requests(): owner_pair = jnp.concatenate([src_owner, dst_owner], axis=1).T]
    another operation x1 -> x0, other arithmetic: 1.28 us -> none  [build_requests(): rows_pair = jnp.stack([src_row, dst_row])]
where the time goes in v9:
time: 127 us
  waiting for transfers between devices  48 us (38%)
  Pallas kernels  27.4 us (22%)
  starting transfers between devices  19.6 us (15%)
  local copies, waits for them, and re-layouts  15.4 us (12%)
  matrix products  11.3 us (9%)
  other arithmetic  4.62 us (4%)
    all_to_all x1, waiting for transfers between devices, local(): lax.all_to_all(served, ('ev', 'node'), split_axis=0, concat_axis=0, tiled...  22.8 us
    all_to_all x1, waiting for transfers between devices, local(): lax.all_to_all(outgoing, ('ev', 'node'), split_axis=0, concat_axis=0, til...  18.2 us
    pallas_call x1, Pallas kernels, owner_update(): pl.pallas_call(update_kernel, grid=(rows_count // block,), in_specs=[pl.B...  16.1 us
    all_to_all x1, starting transfers between devices, local(): lax.all_to_all(request, ('ev', 'node'), split_axis=0, concat_axis=0, tile...  11.5 us
    dot_general x1, matrix products, owner_lookup(): fetched = jnp.dot(select, table, preferred_element_type=jnp.float32)  9.1 us
    pallas_call x1, Pallas kernels, event_messages(): pl.pallas_call(message_kernel, out_shape=jax.ShapeDtypeStruct((slot_total...  8.18 us
    all_to_all x1, waiting for transfers between devices, local(): lax.all_to_all(request, ('ev', 'node'), split_axis=0, concat_axis=0, tile...  6.91 us
    unnamed x20, local copies, waits for them, and re-layouts  5.37 us
  transfers between devices with their start and end apart: 3, of which 3 were waited for; matrix products, arithmetic and copies ran while one was open for 5% of the time, Pallas kernels for 0%

profile of v9, /device:TPU:1, one launch (start us, length us, event | category | flops | bytes accessed | tf_op | source)
XLA Modules:
  0.0 126.5 jit_solution(14611455925447476177)
XLA Ops:
  0.0 1.7 %copy.25.src_owner_ref = s32[512,1]{1,0:T(8,128)} copy(s32[512,1]{0,1:T(1,128)} %param.16) | data formatting | bytes 4096 | tf_op args[0]
  1.7 1.5 %copy.26.dst_owner_ref = s32[512,1]{1,0:T(8,128)} copy(s32[512,1]{0,1:T(1,128)} %param.18) | data formatting | bytes 4096 | tf_op args[2]
  3.2 3.2 %shard_map.154 = (s32[2,512]{1,0:T(2,128)}, s32[512,2]{1,0:T(8,128)}, s32[2,2048]{1,0:T(2,128)}) custom-call(s32[512,1]{1,0:T(8,128)} %copy.25.src_owner_ref, s32[512,1]{1,0:T(8,128)} %copy.26.dst_owner_ref, s32[1,512]{1,0:T(1,128)} %bitcast.17, s32[1,512]{1,0:T(1,128)} %bitcast.18, s32[1,512]{1,0:T(1,128)} %bitcast.19), custom_call_target="tpu_custom_call" | custom-call | tf_op jit(solution)/shard_map/pallas_call | solution.py:155
  6.4 0.8 reshape.27
  7.2 0.8 copy.27
  8.0 11.5 %all-to-all-start = ((s32[128,2,16]{2,1,0:T(2,128)}), s32[128,2,16]{2,1,0:T(2,128)S(1)}, u32[]{:S(2)}, u32[]{:S(2)}) async-start(s32[128,2,16]{2,1,0:T(2,128)} %copy.27), calls=%async_computation | async-start | bytes 262144 | tf_op jit(solution)/shard_map/all_to_all | solution.py:229
  19.5 0.7 fusion.8
  20.2 0.6 broadcast_in_dim.14
  20.8 1.6 %broadcast_in_dim.6 = bf16[4096,1]{1,0:T(8,128)(2,1)} reshape(bf16[4096]{0:T(1024)(128)(2,1)S(1)} %get-tuple-element.14) | data formatting | bytes 16384 | tf_op jit(solution)/shard_map/broadcast_in_dim | solution.py:188
  22.4 6.9 %all-to-all-done = s32[128,2,16]{2,1,0:T(2,128)S(1)} async-done(((s32[128,2,16]{2,1,0:T(2,128)}), s32[128,2,16]{2,1,0:T(2,128)S(1)}, u32[]{:S(2)}, u32[]{:S(2)}) %all-to-all-start) | async-done | bytes 16416 | tf_op jit(solution)/shard_map/all_to_all | solution.py:229
  29.3 1.4 %slice_reduce_fusion = (s32[128,16]{1,0:T(8,128)}, s32[128,16]{1,0:T(8,128)}, s32[128,1,16]{2,1,0:T(1,128)}) fusion(s32[128,2,16]{2,1,0:T(2,128)S(1)} %all-to-all-done), kind=kLoop, calls=%fused_computation.13 | loop fusion | bytes 40960 | tf_op jit(solution)/shard_map/slice | solution.py:231
  30.7 0.9 reshape_squeeze.3
  31.7 0.9 eq.17
  32.6 0.0 copy-done.3
  32.6 0.0 copy-start.7
  32.6 0.0 copy-start.8
  32.6 9.1 %fusion = f32[2048,258]{0,1:T(8,128)S(1)} fusion(s32[2048]{0:T(1024)S(1)} %eq.17, bf16[4096,1]{1,0:T(8,128)(2,1)S(1)} %broadcast_in_dim.14, bf16[4096,1]{1,0:T(8,128)(2,1)} %broadcast_in_dim.6, bf16[4096,256]{1,0:T(8,128)(2,1)S(1)} %copy-done.3), kind=kOutput, calls=%fused_computation.1 | convolution fusion | flops 4343250944 | bytes 4235264 | tf_op jit(solution)/shard_map/dot_general | solution.py:189
  41.7 0.1 slice.49
  41.9 3.7 %cosine_convert_fusion = bf16[2048,128]{0,1:T(8,128)(2,1)S(1)} fusion(f32[128]{0:T(128)S(1)} %copy-done.7, f32[128]{0:T(128)S(1)} %copy-done.8, f32[2048]{0:T(1024)S(1)} %bitcast.16), kind=kLoop, calls=%fused_computation.11 | loop fusion | flops 786432 | bytes 533504 | tf_op jit(solution)/shard_map/convert_element_type | solution.py:10
  45.7 0.1 pad_maximum_fusion
  45.8 1.6 %copy.30 = bf16[2048,384]{1,0:T(8,128)(2,1)} copy(bf16[2048,384]{0,1:T(8,128)(2,1)S(1)} %pad_maximum_fusion) | data formatting | bytes 3145728 | tf_op jit(solution)/shard_map/concatenate | solution.py:193
  47.4 4.3 %all-to-all-start.1 = ((bf16[128,16,384]{2,1,0:T(8,128)(2,1)}), bf16[128,16,384]{2,1,0:T(8,128)(2,1)S(1)}, u32[]{:S(2)}, u32[]{:S(2)}) async-start(bf16[128,16,384]{2,1,0:T(8,128)(2,1)} %bitcast.5), calls=%async_computation.1 | async-start | bytes 3145728 | tf_op jit(solution)/shard_map/all_to_all | solution.py:233
  51.7 2.2 %convolution_add_fusion.edge_ref = f32[512,512]{1,0:T(8,128)} fusion(bf16[512,256]{1,0:T(8,128)(2,1)S(1)} %copy-done, f32[512]{0:T(512)S(1)} %copy-done.6, bf16[896,512]{1,0:T(8,128)(2,1)} %w_in_ref.1), kind=kOutput, calls=%fused_computation.10 | convolution fusion | flops 134479872 | bytes 1574912 | tf_op jit(solution)/shard_map/dot_general | solution.py:226
  53.9 22.8 %all-to-all-done.1 = bf16[128,16,384]{2,1,0:T(8,128)(2,1)S(1)} async-done(((bf16[128,16,384]{2,1,0:T(8,128)(2,1)}), bf16[128,16,384]{2,1,0:T(8,128)(2,1)S(1)}, u32[]{:S(2)}, u32[]{:S(2)}) %all-to-all-start.1) | async-done | bytes 1572896 | tf_op jit(solution)/shard_map/all_to_all | solution.py:233
  76.7 1.1 copy-done.1
  77.9 8.2 %shard_map.155 = bf16[2048,256]{1,0:T(8,128)(2,1)} custom-call(s32[512,2]{1,0:T(8,128)} %get-tuple-element.9.col_ref, s32[2,512]{1,0:T(2,128)} %get-tuple-element.10.row_ref, bf16[2048,384]{1,0:T(8,128)(2,1)} %bitcast.11, f32[512,512]{1,0:T(8,128)} %convolution_add_fusion.edge_ref, bf16[896,512]{1,0:T(8,128)(2,1)} %w_in_ref.1, bf16[512,256]{1,0:T(8,128)(2,1)} %w_out_ref.1), custom_call_target="tpu_custom_call" | custom-call | tf_op jit(solution)/shard_map/pallas_call | solution.py:107
  86.1 3.9 %all-to-all-start.2 = ((bf16[128,16,256]{2,1,0:T(8,128)(2,1)}), bf16[128,16,256]{2,1,0:T(8,128)(2,1)S(1)}, u32[]{:S(2)}, u32[]{:S(2)}) async-start(bf16[128,16,256]{2,1,0:T(8,128)(2,1)} %bitcast.13), calls=%async_computation.2 | async-start | bytes 2097152 | tf_op jit(solution)/shard_map/all_to_all | solution.py:235
  89.9 0.6 reshape.28.bin_ref
  90.5 0.7 reshape_reshape_squeeze.3.rows_ref
  91.2 18.2 %all-to-all-done.2 = bf16[128,16,256]{2,1,0:T(8,128)(2,1)S(1)} async-done(((bf16[128,16,256]{2,1,0:T(8,128)(2,1)}), bf16[128,16,256]{2,1,0:T(8,128)(2,1)S(1)}, u32[]{:S(2)}, u32[]{:S(2)}) %all-to-all-start.2) | async-done | bytes 1048608 | tf_op jit(solution)/shard_map/all_to_all | solution.py:235
  109.5 1.0 copy-done.2
  110.4 16.1 %shard_map.156 = bf16[4096,256]{1,0:T(8,128)(2,1)} custom-call(s32[1,2048]{1,0:T(1,128)} %reshape_reshape_squeeze.3.rows_ref, bf16[2048,256]{1,0:T(8,128)(2,1)} %bitcast.12, bf16[4096,256]{1,0:T(8,128)(2,1)} %mem_ref.1, bf16[256,768]{1,0:T(8,128)(2,1)} %win_ref.1, f32[1,768]{1,0:T(1,128)} %reshape.28.bin_ref, bf16[256,768]{1,0:T(8,128)(2,1)} %whid_ref.1), custom_call_target="tpu_custom_call" | custom-call | tf_op jit(solution)/shard_map/pallas_call | solution.py:52
  (14 shorter events, 0.1 us)
Async XLA Ops:
  0.0 51.7 %copy-start = (bf16[512,256]{1,0:T(8,128)(2,1)S(1)}, bf16[512,256]{1,0:T(8,128)(2,1)}, u32[]{:S(2)}) copy-start(bf16[512,256]{1,0:T(8,128)(2,1)} %param.21) | copy-start | bytes 786436
  0.0 32.6 %copy-start.3 = (bf16[4096,256]{1,0:T(8,128)(2,1)S(1)}, bf16[4096,256]{1,0:T(8,128)(2,1)}, u32[]{:S(2)}) copy-start(bf16[4096,256]{1,0:T(8,128)(2,1)} %mem_ref.1) | copy-start | bytes 6291460
  8.0 21.4 %all-to-all-start = ((s32[128,2,16]{2,1,0:T(2,128)}), s32[128,2,16]{2,1,0:T(2,128)S(1)}, u32[]{:S(2)}, u32[]{:S(2)}) async-start(s32[128,2,16]{2,1,0:T(2,128)} %copy.27), calls=%async_computation | async-start | bytes 262144 | tf_op jit(solution)/shard_map/all_to_all | solution.py:229
  32.6 9.3 %copy-start.7 = (f32[128]{0:T(128)S(1)}, f32[128]{0:T(128)}, u32[]{:S(2)}) copy-start(f32[128]{0:T(128)} %param.25) | copy-start | bytes 1540
  32.6 9.3 %copy-start.8 = (f32[128]{0:T(128)S(1)}, f32[128]{0:T(128)}, u32[]{:S(2)}) copy-start(f32[128]{0:T(128)} %param.24) | copy-start | bytes 1540
  47.4 4.3 %copy-start.6 = (f32[512]{0:T(512)S(1)}, f32[512]{0:T(512)}, u32[]{:S(2)}) copy-start(f32[512]{0:T(512)} %param.27) | copy-start | bytes 6148
  47.4 29.4 %all-to-all-start.1 = ((bf16[128,16,384]{2,1,0:T(8,128)(2,1)}), bf16[128,16,384]{2,1,0:T(8,128)(2,1)S(1)}, u32[]{:S(2)}, u32[]{:S(2)}) async-start(bf16[128,16,384]{2,1,0:T(8,128)(2,1)} %bitcast.5), calls=%async_computation.1 | async-start | bytes 3145728 | tf_op jit(solution)/shard_map/all_to_all | solution.py:233
  76.7 1.1 copy-start.1
  77.9 12.0 %copy-start.5 = (f32[768]{0:T(1024)S(1)}, f32[768]{0:T(1024)}, u32[]{:S(2)}) copy-start(f32[768]{0:T(1024)} %param.30) | copy-start | bytes 9220
  77.9 12.6 %copy-start.4 = (s32[128,16]{1,0:T(8,128)S(1)}, s32[128,16]{1,0:T(8,128)}, u32[]{:S(2)}) copy-start(s32[128,16]{1,0:T(8,128)} %get-tuple-element.12) | copy-start | bytes 24580
  86.1 23.4 %all-to-all-start.2 = ((bf16[128,16,256]{2,1,0:T(8,128)(2,1)}), bf16[128,16,256]{2,1,0:T(8,128)(2,1)S(1)}, u32[]{:S(2)}, u32[]{:S(2)}) async-start(bf16[128,16,256]{2,1,0:T(8,128)(2,1)} %bitcast.13), calls=%async_computation.2 | async-start | bytes 2097152 | tf_op jit(solution)/shard_map/all_to_all | solution.py:235
  109.5 1.0 copy-start.2

commit v10 on v8

--- a/solution.py
+++ b/solution.py
@@ -110,7 +110,7 @@
     )(slot_cols, slot_ids, fetched, edge_part, w_msg_in, w_msg_out)
 
 
-def prologue_kernel(owner_ref, rows_ref, time_ref, slot_ref, slot_t_ref, request_ref):
+def prologue_kernel(owner_ref, src_row_ref, dst_row_ref, time_ref, slot_ref, slot_t_ref, request_ref):
     events = owner_ref.shape[1]
     owners = 128
     capacity = 8
@@ -129,7 +129,7 @@
         position = jnp.sum(jnp.where(onehot, earlier, 0.0), axis=0, keepdims=True)
         slots.append(owner_row * chunk + side * capacity + position.astype(jnp.int32))
     slot_all = jnp.concatenate(slots, axis=1)
-    rows_all = jnp.concatenate([rows_ref[0:1, :], rows_ref[1:2, :]], axis=1)
+    rows_all = jnp.concatenate([src_row_ref[...], dst_row_ref[...]], axis=1)
     times_all = jnp.concatenate([time_ref[...], time_ref[...]], axis=1)
     zero = jnp.zeros_like(rows_all)
     digits = jnp.concatenate(
@@ -153,7 +153,6 @@
 def build_requests(src_owner, src_row, dst_owner, dst_row, event_time, slot_total):
     events = src_row.shape[0]
     owner_pair = jnp.concatenate([src_owner, dst_owner], axis=1).T
-    rows_pair = jnp.stack([src_row, dst_row])
     return pl.pallas_call(
         prologue_kernel,
         out_shape=[
@@ -161,7 +160,7 @@
             jax.ShapeDtypeStruct((events, 2), jnp.int32),
             jax.ShapeDtypeStruct((2, slot_total), jnp.int32),
         ],
-    )(owner_pair, rows_pair, event_time.reshape(1, events))
+    )(owner_pair, src_row.reshape(1, events), dst_row.reshape(1, events), event_time.reshape(1, events))
 
 
 def slot_of(owner_ids, owner_count, capacity):
@@ -217,14 +216,14 @@
     slot_ids, slot_cols, request = build_requests(
         src_owner, src_row, dst_owner, dst_row, event_time, slot_total
     )
-    request = request.reshape(2, devices_all, chunk).transpose(1, 0, 2)
+    request = request.reshape(2, devices_all, chunk)
     edge_part = (
         jnp.dot(edge_feat, w_msg_in[2 * width + time_width :], preferred_element_type=jnp.float32)
         + b_msg
     )
-    received = lax.all_to_all(request, ("ev", "node"), split_axis=0, concat_axis=0, tiled=True)
-    rows_held = received[:, 0, :].reshape(-1)
-    times_held = received[:, 1, :].reshape(-1)
+    received = lax.all_to_all(request, ("ev", "node"), split_axis=1, concat_axis=1, tiled=True)
+    rows_held = received[0].reshape(-1)
+    times_held = received[1].reshape(-1)
     served = owner_lookup(rows_held, times_held, memory, last_update, time_freq, time_phase)
     returned = lax.all_to_all(served, ("ev", "node"), split_axis=0, concat_axis=0, tiled=True)
     outgoing = event_messages(slot_ids, slot_cols, returned, edge_part, w_msg_in, w_msg_out)

time: 126 us -> 125 us (level)
  other arithmetic: 7.34 us -> 6.06 us
    another operation x1 -> x0, other arithmetic: 1.28 us -> none  [build_requests(): rows_pair = jnp.stack([src_row, dst_row])]
where the time goes in v10:
time: 125 us; the launch traced here: 124 us
  waiting for transfers between devices  48 us (38%)
  Pallas kernels  26.9 us (22%)
  starting transfers between devices  19.6 us (16%)
  local copies, waits for them, and re-layouts  12.1 us (10%)
  matrix products  11.3 us (9%)
  other arithmetic  6.06 us (5%)
    all_to_all x1, waiting for transfers between devices, local(): lax.all_to_all(served, ('ev', 'node'), split_axis=0, concat_axis=0, tiled...  22.8 us
    all_to_all x1, waiting for transfers between devices, local(): lax.all_to_all(outgoing, ('ev', 'node'), split_axis=0, concat_axis=0, til...  18.2 us
    pallas_call x1, Pallas kernels, owner_update(): pl.pallas_call(update_kernel, grid=(rows_count // block,), in_specs=[pl.B...  16.1 us
    all_to_all x1, starting transfers between devices, local(): lax.all_to_all(request, ('ev', 'node'), split_axis=1, concat_axis=1, tile...  11.5 us
    dot_general x1, matrix products, owner_lookup(): fetched = jnp.dot(select, table, preferred_element_type=jnp.float32)  9.1 us
    pallas_call x1, Pallas kernels, event_messages(): pl.pallas_call(message_kernel, out_shape=jax.ShapeDtypeStruct((slot_total...  8.18 us
    all_to_all x1, waiting for transfers between devices, local(): lax.all_to_all(request, ('ev', 'node'), split_axis=1, concat_axis=1, tile...  6.91 us
    all_to_all x1, starting transfers between devices, local(): lax.all_to_all(served, ('ev', 'node'), split_axis=0, concat_axis=0, tiled...  4.26 us
  transfers between devices with their start and end apart: 3, of which 3 were waited for; matrix products, arithmetic and copies ran while one was open for 5% of the time, Pallas kernels for 0%

profile of v10, /device:TPU:1, one launch (start us, length us, event | category | flops | bytes accessed | tf_op | source)
XLA Modules:
  0.0 124.2 jit_solution(12212918379757104099)
XLA Ops:
  0.0 1.4 %add_bitcast_fusion.owner_ref = s32[2,512]{1,0:T(2,128)} fusion(s32[512,1]{0,1:T(1,128)} %param.18, s32[512,1]{0,1:T(1,128)} %param.16), kind=kLoop, calls=%fused_computation.30 | loop fusion | flops 1024 | bytes 8192 | tf_op jit(solution)/shard_map/transpose | solution.py:155
  1.5 2.7 %shard_map.154 = (s32[2,512]{1,0:T(2,128)}, s32[512,2]{1,0:T(8,128)}, s32[2,2048]{1,0:T(2,128)}) custom-call(s32[2,512]{1,0:T(2,128)} %add_bitcast_fusion.owner_ref, s32[1,512]{1,0:T(1,128)} %bitcast.17, s32[1,512]{1,0:T(1,128)} %bitcast.18, s32[1,512]{1,0:T(1,128)} %bitcast.19), custom_call_target="tpu_custom_call" | custom-call | tf_op jit(solution)/shard_map/pallas_call | solution.py:156
  4.1 0.8 reshape.27
  5.0 0.8 copy.21
  5.7 11.5 %all-to-all-start = ((s32[2,128,16]{2,0,1:T(2,128)}), s32[2,128,16]{2,0,1:T(2,128)S(1)}, u32[]{:S(2)}, u32[]{:S(2)}) async-start(s32[2,128,16]{2,0,1:T(2,128)} %copy.21), calls=%async_computation | async-start | bytes 262144 | tf_op jit(solution)/shard_map/all_to_all | solution.py:224
  17.2 0.7 fusion.8
  18.0 0.6 broadcast_in_dim.14
  18.6 1.6 %broadcast_in_dim.6 = bf16[4096,1]{1,0:T(8,128)(2,1)} reshape(bf16[4096]{0:T(1024)(128)(2,1)S(1)} %get-tuple-element.14) | data formatting | bytes 16384 | tf_op jit(solution)/shard_map/broadcast_in_dim | solution.py:183
  20.1 6.9 %all-to-all-done = s32[2,128,16]{2,0,1:T(2,128)S(1)} async-done(((s32[2,128,16]{2,0,1:T(2,128)}), s32[2,128,16]{2,0,1:T(2,128)S(1)}, u32[]{:S(2)}, u32[]{:S(2)}) %all-to-all-start) | async-done | bytes 16416 | tf_op jit(solution)/shard_map/all_to_all | solution.py:224
  27.1 1.4 %slice_reduce_fusion = (s32[128,16]{1,0:T(8,128)}, s32[128,16]{1,0:T(8,128)}, s32[1,128,16]{2,0,1:T(1,128)}) fusion(s32[2,128,16]{2,0,1:T(2,128)S(1)} %all-to-all-done), kind=kLoop, calls=%fused_computation.13 | loop fusion | bytes 40960 | tf_op jit(solution)/shard_map/slice | solution.py:226
  28.5 0.9 reshape_squeeze.3
  29.4 0.9 eq.17
  30.3 0.0 copy-done.3
  30.3 0.0 copy-start.7
  30.3 0.0 copy-start.8
  30.3 9.1 %fusion = f32[2048,258]{0,1:T(8,128)S(1)} fusion(s32[2048]{0:T(1024)S(1)} %eq.17, bf16[4096,1]{1,0:T(8,128)(2,1)S(1)} %broadcast_in_dim.14, bf16[4096,1]{1,0:T(8,128)(2,1)} %broadcast_in_dim.6, bf16[4096,256]{1,0:T(8,128)(2,1)S(1)} %copy-done.3), kind=kOutput, calls=%fused_computation.1 | convolution fusion | flops 4343250944 | bytes 4235264 | tf_op jit(solution)/shard_map/dot_general | solution.py:184
  39.5 0.1 slice.49
  39.7 3.7 %cosine_convert_fusion = bf16[2048,128]{0,1:T(8,128)(2,1)S(1)} fusion(f32[128]{0:T(128)S(1)} %copy-done.7, f32[128]{0:T(128)S(1)} %copy-done.8, f32[2048]{0:T(1024)S(1)} %bitcast.16), kind=kLoop, calls=%fused_computation.11 | loop fusion | flops 786432 | bytes 533504 | tf_op jit(solution)/shard_map/convert_element_type | solution.py:10
  43.4 0.1 pad_maximum_fusion
  43.5 1.6 %copy.24 = bf16[2048,384]{1,0:T(8,128)(2,1)} copy(bf16[2048,384]{0,1:T(8,128)(2,1)S(1)} %pad_maximum_fusion) | data formatting | bytes 3145728 | tf_op jit(solution)/shard_map/concatenate | solution.py:188
  45.1 4.3 %all-to-all-start.1 = ((bf16[128,16,384]{2,1,0:T(8,128)(2,1)}), bf16[128,16,384]{2,1,0:T(8,128)(2,1)S(1)}, u32[]{:S(2)}, u32[]{:S(2)}) async-start(bf16[128,16,384]{2,1,0:T(8,128)(2,1)} %bitcast.5), calls=%async_computation.1 | async-start | bytes 3145728 | tf_op jit(solution)/shard_map/all_to_all | solution.py:228
  49.4 0.0 copy-done
  49.4 2.2 %convolution_add_fusion.edge_ref = f32[512,512]{1,0:T(8,128)} fusion(bf16[512,256]{1,0:T(8,128)(2,1)S(1)} %copy-done, f32[512]{0:T(512)S(1)} %copy-done.6, bf16[896,512]{1,0:T(8,128)(2,1)} %w_in_ref.1), kind=kOutput, calls=%fused_computation.10 | convolution fusion | flops 134479872 | bytes 1574912 | tf_op jit(solution)/shard_map/dot_general | solution.py:221
  51.6 22.8 %all-to-all-done.1 = bf16[128,16,384]{2,1,0:T(8,128)(2,1)S(1)} async-done(((bf16[128,16,384]{2,1,0:T(8,128)(2,1)}), bf16[128,16,384]{2,1,0:T(8,128)(2,1)S(1)}, u32[]{:S(2)}, u32[]{:S(2)}) %all-to-all-start.1) | async-done | bytes 1572896 | tf_op jit(solution)/shard_map/all_to_all | solution.py:228
  74.4 1.1 copy-done.1
  75.6 8.2 %shard_map.155 = bf16[2048,256]{1,0:T(8,128)(2,1)} custom-call(s32[512,2]{1,0:T(8,128)} %get-tuple-element.9.col_ref, s32[2,512]{1,0:T(2,128)} %get-tuple-element.10.row_ref, bf16[2048,384]{1,0:T(8,128)(2,1)} %bitcast.12, f32[512,512]{1,0:T(8,128)} %convolution_add_fusion.edge_ref, bf16[896,512]{1,0:T(8,128)(2,1)} %w_in_ref.1, bf16[512,256]{1,0:T(8,128)(2,1)} %w_out_ref.1), custom_call_target="tpu_custom_call" | custom-call | tf_op jit(solution)/shard_map/pallas_call | solution.py:107
  83.8 3.9 %all-to-all-start.2 = ((bf16[128,16,256]{2,1,0:T(8,128)(2,1)}), bf16[128,16,256]{2,1,0:T(8,128)(2,1)S(1)}, u32[]{:S(2)}, u32[]{:S(2)}) async-start(bf16[128,16,256]{2,1,0:T(8,128)(2,1)} %bitcast.14), calls=%async_computation.2 | async-start | bytes 2097152 | tf_op jit(solution)/shard_map/all_to_all | solution.py:230
  87.6 0.6 reshape.28.bin_ref
  88.2 0.7 reshape_reshape_squeeze.3.rows_ref
  88.9 18.2 %all-to-all-done.2 = bf16[128,16,256]{2,1,0:T(8,128)(2,1)S(1)} async-done(((bf16[128,16,256]{2,1,0:T(8,128)(2,1)}), bf16[128,16,256]{2,1,0:T(8,128)(2,1)S(1)}, u32[]{:S(2)}, u32[]{:S(2)}) %all-to-all-start.2) | async-done | bytes 1048608 | tf_op jit(solution)/shard_map/all_to_all | solution.py:230
  107.2 1.0 copy-done.2
  108.1 16.1 %shard_map.156 = bf16[4096,256]{1,0:T(8,128)(2,1)} custom-call(s32[1,2048]{1,0:T(1,128)} %reshape_reshape_squeeze.3.rows_ref, bf16[2048,256]{1,0:T(8,128)(2,1)} %bitcast.13, bf16[4096,256]{1,0:T(8,128)(2,1)} %mem_ref.1, bf16[256,768]{1,0:T(8,128)(2,1)} %win_ref.1, f32[1,768]{1,0:T(1,128)} %reshape.28.bin_ref, bf16[256,768]{1,0:T(8,128)(2,1)} %whid_ref.1), custom_call_target="tpu_custom_call" | custom-call | tf_op jit(solution)/shard_map/pallas_call | solution.py:52
  (13 shorter events, 0.1 us)
Async XLA Ops:
  0.0 49.4 %copy-start = (bf16[512,256]{1,0:T(8,128)(2,1)S(1)}, bf16[512,256]{1,0:T(8,128)(2,1)}, u32[]{:S(2)}) copy-start(bf16[512,256]{1,0:T(8,128)(2,1)} %param.21) | copy-start | bytes 786436
  0.0 30.3 %copy-start.3 = (bf16[4096,256]{1,0:T(8,128)(2,1)S(1)}, bf16[4096,256]{1,0:T(8,128)(2,1)}, u32[]{:S(2)}) copy-start(bf16[4096,256]{1,0:T(8,128)(2,1)} %mem_ref.1) | copy-start | bytes 6291460
  5.7 21.3 %all-to-all-start = ((s32[2,128,16]{2,0,1:T(2,128)}), s32[2,128,16]{2,0,1:T(2,128)S(1)}, u32[]{:S(2)}, u32[]{:S(2)}) async-start(s32[2,128,16]{2,0,1:T(2,128)} %copy.21), calls=%async_computation | async-start | bytes 262144 | tf_op jit(solution)/shard_map/all_to_all | solution.py:224
  30.3 9.3 %copy-start.7 = (f32[128]{0:T(128)S(1)}, f32[128]{0:T(128)}, u32[]{:S(2)}) copy-start(f32[128]{0:T(128)} %param.25) | copy-start | bytes 1540
  30.3 9.3 %copy-start.8 = (f32[128]{0:T(128)S(1)}, f32[128]{0:T(128)}, u32[]{:S(2)}) copy-start(f32[128]{0:T(128)} %param.24) | copy-start | bytes 1540
  45.1 4.3 %copy-start.6 = (f32[512]{0:T(512)S(1)}, f32[512]{0:T(512)}, u32[]{:S(2)}) copy-start(f32[512]{0:T(512)} %param.27) | copy-start | bytes 6148
  45.1 29.4 %all-to-all-start.1 = ((bf16[128,16,384]{2,1,0:T(8,128)(2,1)}), bf16[128,16,384]{2,1,0:T(8,128)(2,1)S(1)}, u32[]{:S(2)}, u32[]{:S(2)}) async-start(bf16[128,16,384]{2,1,0:T(8,128)(2,1)} %bitcast.5), calls=%async_computation.1 | async-start | bytes 3145728 | tf_op jit(solution)/shard_map/all_to_all | solution.py:228
  74.4 1.1 copy-start.1
  75.6 12.0 %copy-start.5 = (f32[768]{0:T(1024)S(1)}, f32[768]{0:T(1024)}, u32[]{:S(2)}) copy-start(f32[768]{0:T(1024)} %param.30) | copy-start | bytes 9220
  75.6 12.6 %copy-start.4 = (s32[128,16]{1,0:T(8,128)S(1)}, s32[128,16]{1,0:T(8,128)}, u32[]{:S(2)}) copy-start(s32[128,16]{1,0:T(8,128)} %get-tuple-element.12) | copy-start | bytes 24580
  83.8 23.4 %all-to-all-start.2 = ((bf16[128,16,256]{2,1,0:T(8,128)(2,1)}), bf16[128,16,256]{2,1,0:T(8,128)(2,1)S(1)}, u32[]{:S(2)}, u32[]{:S(2)}) async-start(bf16[128,16,256]{2,1,0:T(8,128)(2,1)} %bitcast.14), calls=%async_computation.2 | async-start | bytes 2097152 | tf_op jit(solution)/shard_map/all_to_all | solution.py:230
  107.2 1.0 copy-start.2

commit v11 on v10

--- a/solution.py
+++ b/solution.py
@@ -65,7 +65,9 @@
     )(row_flat.reshape(1, slots), msg_flat, memory, w_gru_in, b_gru_in.reshape(1, gates), w_gru_hid)
 
 
-def message_kernel(col_ref, row_ref, fetched_ref, edge_ref, w_in_ref, w_out_ref, out_ref):
+def message_kernel(
+    col_ref, row_ref, fetched_ref, edge_ref, time_ref, freq_ref, phase_ref, w_in_ref, w_out_ref, out_ref
+):
     events = edge_ref.shape[0]
     slot_total = fetched_ref.shape[0]
     width = out_ref.shape[1]
@@ -75,9 +77,13 @@
     for side in range(2):
         pick = (lane_ids == col_ref[:, side : side + 1]).astype(jnp.bfloat16)
         rows = jnp.dot(pick, fetched_ref[...], preferred_element_type=jnp.float32)
-        picked.append(rows.astype(jnp.bfloat16))
-    mem_src, enc_src = picked[0][:, :width], picked[0][:, width:]
-    mem_dst, enc_dst = picked[1][:, :width], picked[1][:, width:]
+        stamp = rows[:, width : width + 1].astype(jnp.int32) * 64
+        stamp = stamp + rows[:, width + 1 : width + 2].astype(jnp.int32)
+        delta = (time_ref[...] - stamp).astype(jnp.float32)
+        encoded = jnp.cos(delta * freq_ref[...] + phase_ref[...]).astype(jnp.bfloat16)
+        picked.append((rows[:, :width].astype(jnp.bfloat16), encoded))
+    mem_src, enc_src = picked[0]
+    mem_dst, enc_dst = picked[1]
     w_self = w_in_ref[:width]
     w_other = w_in_ref[width : 2 * width]
     w_time = w_in_ref[2 * width : 2 * width + time_width]
@@ -101,13 +107,25 @@
     out_ref[...] = out.astype(out_ref.dtype)
 
 
-def event_messages(slot_ids, slot_cols, fetched, edge_part, w_msg_in, w_msg_out):
+def event_messages(
+    slot_ids, slot_cols, fetched, edge_part, event_time, time_freq, time_phase, w_msg_in, w_msg_out
+):
     slot_total = fetched.shape[0]
     msg_width = w_msg_out.shape[1]
     return pl.pallas_call(
         message_kernel,
         out_shape=jax.ShapeDtypeStruct((slot_total, msg_width), jnp.bfloat16),
-    )(slot_cols, slot_ids, fetched, edge_part, w_msg_in, w_msg_out)
+    )(
+        slot_cols,
+        slot_ids,
+        fetched,
+        edge_part,
+        event_time.reshape(-1, 1),
+        time_freq.reshape(1, -1),
+        time_phase.reshape(1, -1),
+        w_msg_in,
+        w_msg_out,
+    )
 
 
 def prologue_kernel(owner_ref, src_row_ref, dst_row_ref, time_ref, slot_ref, slot_t_ref, request_ref):
@@ -174,18 +192,18 @@
     return owner_ids * capacity + position
 
 
-def owner_lookup(row_request, time_request, memory, last_update, time_freq, time_phase):
+def owner_lookup(row_request, memory, last_update, time_width):
     rows_count, width = memory.shape
     row_range = jnp.arange(rows_count, dtype=jnp.int32)
     select = (row_request[:, None] == row_range[None, :]).astype(jnp.bfloat16)
-    high = (last_update // 64).astype(jnp.bfloat16)
-    low = (last_update % 64).astype(jnp.bfloat16)
-    table = jnp.concatenate([memory, high[:, None], low[:, None]], axis=1)
-    fetched = jnp.dot(select, table, preferred_element_type=jnp.float32)
-    mem_rows = fetched[:, :width].astype(jnp.bfloat16)
-    stamp = fetched[:, width].astype(jnp.int32) * 64 + fetched[:, width + 1].astype(jnp.int32)
-    encoded = encode(time_request - stamp, time_freq, time_phase)
-    return jnp.concatenate([mem_rows, encoded], axis=-1)
+    digit_cols = jnp.arange(time_width, dtype=jnp.int32)
+    digits = jnp.where(
+        digit_cols[None, :] == 0,
+        last_update[:, None] // 64,
+        jnp.where(digit_cols[None, :] == 1, last_update[:, None] % 64, 0),
+    ).astype(jnp.bfloat16)
+    table = jnp.concatenate([memory, digits], axis=1)
+    return jnp.dot(select, table, preferred_element_type=jnp.float32).astype(jnp.bfloat16)
 
 
 def local(
@@ -223,10 +241,11 @@
     )
     received = lax.all_to_all(request, ("ev", "node"), split_axis=1, concat_axis=1, tiled=True)
     rows_held = received[0].reshape(-1)
-    times_held = received[1].reshape(-1)
-    served = owner_lookup(rows_held, times_held, memory, last_update, time_freq, time_phase)
+    served = owner_lookup(rows_held, memory, last_update, time_width)
     returned = lax.all_to_all(served, ("ev", "node"), split_axis=0, concat_axis=0, tiled=True)
-    outgoing = event_messages(slot_ids, slot_cols, returned, edge_part, w_msg_in, w_msg_out)
+    outgoing = event_messages(
+        slot_ids, slot_cols, returned, edge_part, event_time, time_freq, time_phase, w_msg_in, w_msg_out
+    )
     arrived = lax.all_to_all(outgoing, ("ev", "node"), split_axis=0, concat_axis=0, tiled=True)
     return owner_update(rows_held, arrived, memory, w_gru_in, b_gru_in, w_gru_hid)
 

time: 125 us -> 120 us (0.960)
  local copies, waits for them, and re-layouts: 12.1 us -> 8.11 us
  other arithmetic: 6.06 us -> 3.57 us
    convert_element_type x3 -> x1, other arithmetic: 4.51 us -> 1.39 us  [owner_lookup(): digits = jnp.where(digit_cols[None, :] == 0, last_update[:, None] // 64,...]
    broadcast_in_dim x2 -> x0, local copies, waits for them, and re-layouts: 2.18 us -> none  [owner_lookup(): table = jnp.concatenate([memory, high[:, None], low[:, None]], axis=1)]
    concatenate x1 -> x0, local copies, waits for them, and re-layouts: 1.57 us -> none  [owner_lookup(): return jnp.concatenate([mem_rows, encoded], axis=-1)]
where the time goes in v11:
time: 120 us; the launch traced here: 119 us
  waiting for transfers between devices  47.9 us (40%)
  Pallas kernels  27.7 us (23%)
  starting transfers between devices  19.7 us (16%)
  matrix products  12.2 us (10%)
  local copies, waits for them, and re-layouts  8.11 us (7%)
  other arithmetic  3.57 us (3%)
    all_to_all x1, waiting for transfers between devices, local(): lax.all_to_all(served, ('ev', 'node'), split_axis=0, concat_axis=0, tiled...  22 us
    all_to_all x1, waiting for transfers between devices, local(): lax.all_to_all(outgoing, ('ev', 'node'), split_axis=0, concat_axis=0, til...  18.3 us
    pallas_call x1, Pallas kernels, owner_update(): pl.pallas_call(update_kernel, grid=(rows_count // block,), in_specs=[pl.B...  16.1 us
    all_to_all x1, starting transfers between devices, local(): lax.all_to_all(request, ('ev', 'node'), split_axis=1, concat_axis=1, tile...  11.5 us
    dot_general x1, matrix products, owner_lookup(): jnp.dot(select, table, preferred_element_type=jnp.float32)  9.97 us
    pallas_call x1, Pallas kernels, event_messages(): pl.pallas_call(message_kernel, out_shape=jax.ShapeDtypeStruct((slot_total...  8.99 us
    all_to_all x1, waiting for transfers between devices, local(): lax.all_to_all(request, ('ev', 'node'), split_axis=1, concat_axis=1, tile...  7.69 us
    all_to_all x1, starting transfers between devices, local(): lax.all_to_all(served, ('ev', 'node'), split_axis=0, concat_axis=0, tiled...  4.26 us
  transfers between devices with their start and end apart: 3, of which 3 were waited for; matrix products, arithmetic and copies ran while one was open for 5% of the time, Pallas kernels for 0%

profile of v11, /device:TPU:1, one launch (start us, length us, event | category | flops | bytes accessed | tf_op | source)
XLA Modules:
  0.0 119.4 jit_solution(15996583706943583336)
XLA Ops:
  0.0 0.0 copy-start
  0.0 0.0 copy-start.3
  0.0 1.4 %add_bitcast_fusion.owner_ref = s32[2,512]{1,0:T(2,128)} fusion(s32[512,1]{0,1:T(1,128)} %param.18, s32[512,1]{0,1:T(1,128)} %param.16), kind=kLoop, calls=%fused_computation.18 | loop fusion | flops 1024 | bytes 8192 | tf_op jit(solution)/shard_map/transpose | solution.py:173
  1.4 2.7 %shard_map.154 = (s32[2,512]{1,0:T(2,128)}, s32[512,2]{1,0:T(8,128)}, s32[2,2048]{1,0:T(2,128)}) custom-call(s32[2,512]{1,0:T(2,128)} %add_bitcast_fusion.owner_ref, s32[1,512]{1,0:T(1,128)} %bitcast.21, s32[1,512]{1,0:T(1,128)} %bitcast.22, s32[1,512]{1,0:T(1,128)} %bitcast.19), custom_call_target="tpu_custom_call" | custom-call | tf_op jit(solution)/shard_map/pallas_call | solution.py:174
  4.1 0.8 reshape.69
  5.0 0.8 copy.18
  5.7 11.5 %all-to-all-start = ((s32[2,128,16]{2,0,1:T(2,128)}), s32[2,128,16]{2,0,1:T(2,128)S(1)}, u32[]{:S(2)}, u32[]{:S(2)}) async-start(s32[2,128,16]{2,0,1:T(2,128)} %copy.18), calls=%async_computation | async-start | bytes 262144 | tf_op jit(solution)/shard_map/all_to_all | solution.py:242
  17.2 0.7 add_select_fusion.1
  18.0 1.4 %select_convert_fusion = bf16[4096,128]{1,0:T(8,128)(2,1)S(1)} fusion(s32[4096]{0:T(1024)S(1)} %get-tuple-element.14, s32[4096]{0:T(1024)S(1)} %get-tuple-element.13, pred[128]{0:T(512)(128)(4,1)S(1)} %get-tuple-element.15, pred[128]{0:T(512)(128)(4,1)S(1)} %get-tuple-element.16), kind=kLoop, calls=%fused_computation.7 | loop fusion | flops 1572864 | bytes 1081600 | tf_op jit(solution)/shard_map/convert_element_type | solution.py:204
  19.4 7.7 %all-to-all-done = s32[2,128,16]{2,0,1:T(2,128)S(1)} async-done(((s32[2,128,16]{2,0,1:T(2,128)}), s32[2,128,16]{2,0,1:T(2,128)S(1)}, u32[]{:S(2)}, u32[]{:S(2)}) %all-to-all-start) | async-done | bytes 16416 | tf_op jit(solution)/shard_map/all_to_all | solution.py:242
  27.1 1.3 %fusion.12 = (s32[1,128,16]{2,0,1:T(1,128)}, s32[128,16]{1,0:T(8,128)}) fusion(s32[2,128,16]{2,0,1:T(2,128)S(1)} %all-to-all-done), kind=kLoop, calls=%fused_computation.23 | loop fusion | bytes 24576 | tf_op jit(solution)/shard_map/slice | solution.py:243
  28.4 0.9 eq.39
  29.3 0.0 copy-done.3
  29.3 10.0 %fusion.5 = bf16[2048,384]{1,0:T(8,128)(2,1)} fusion(bf16[4096,128]{1,0:T(8,128)(2,1)S(1)} %select_convert_fusion, bf16[4096,256]{1,0:T(8,128)(2,1)S(1)} %copy-done.3, s32[2048]{0:T(1024)S(1)} %eq.39), kind=kOutput, calls=%fused_computation.6 | convolution fusion | flops 6457917440 | bytes 4726784 | tf_op jit(solution)/shard_map/dot_general | solution.py:206
  39.3 0.0 copy-start.5
  39.3 4.3 %all-to-all-start.1 = ((bf16[128,16,384]{2,1,0:T(8,128)(2,1)}), bf16[128,16,384]{2,1,0:T(8,128)(2,1)S(1)}, u32[]{:S(2)}, u32[]{:S(2)}) async-start(bf16[128,16,384]{2,1,0:T(8,128)(2,1)} %bitcast.17), calls=%async_computation.1 | async-start | bytes 3145728 | tf_op jit(solution)/shard_map/all_to_all | solution.py:245
  43.6 0.0 copy-done.5
  43.6 0.9 copy.19.time_ref
  44.4 0.0 copy-done
  44.4 0.0 copy-done.7
  44.4 2.2 %convolution_add_fusion.edge_ref = f32[512,512]{1,0:T(8,128)} fusion(bf16[512,256]{1,0:T(8,128)(2,1)S(1)} %copy-done, f32[512]{0:T(512)S(1)} %copy-done.7, bf16[896,512]{1,0:T(8,128)(2,1)} %w_in_ref.1), kind=kOutput, calls=%fused_computation.8 | convolution fusion | flops 134479872 | bytes 1574912 | tf_op jit(solution)/shard_map/dot_general | solution.py:239
  46.7 22.0 %all-to-all-done.1 = bf16[128,16,384]{2,1,0:T(8,128)(2,1)S(1)} async-done(((bf16[128,16,384]{2,1,0:T(8,128)(2,1)}), bf16[128,16,384]{2,1,0:T(8,128)(2,1)S(1)}, u32[]{:S(2)}, u32[]{:S(2)}) %all-to-all-start.1) | async-done | bytes 1572896 | tf_op jit(solution)/shard_map/all_to_all | solution.py:245
  68.6 1.1 copy-done.1
  69.8 9.0 %shard_map.155 = bf16[2048,256]{1,0:T(8,128)(2,1)} custom-call(s32[512,2]{1,0:T(8,128)} %get-tuple-element.9.col_ref, s32[2,512]{1,0:T(2,128)} %get-tuple-element.10.row_ref, bf16[2048,384]{1,0:T(8,128)(2,1)} %bitcast.14, f32[512,512]{1,0:T(8,128)} %convolution_add_fusion.edge_ref, s32[512,1]{1,0:T(8,128)} %copy.19.time_ref, f32[1,128]{1,0:T(1,128)} %bitcast.23, ...), custom_call_target="tpu_custom_call" | custom-call | tf_op jit(solution)/shard_map/pallas_call | solution.py:115
  78.8 4.0 %all-to-all-start.2 = ((bf16[128,16,256]{2,1,0:T(8,128)(2,1)}), bf16[128,16,256]{2,1,0:T(8,128)(2,1)S(1)}, u32[]{:S(2)}, u32[]{:S(2)}) async-start(bf16[128,16,256]{2,1,0:T(8,128)(2,1)} %bitcast.15), calls=%async_computation.2 | async-start | bytes 2097152 | tf_op jit(solution)/shard_map/all_to_all | solution.py:249
  82.7 0.0 copy-done.6
  82.8 0.6 reshape.73.bin_ref
  83.3 0.0 copy-done.4
  83.3 0.7 reshape_reshape_squeeze.3.rows_ref
  84.0 18.3 %all-to-all-done.2 = bf16[128,16,256]{2,1,0:T(8,128)(2,1)S(1)} async-done(((bf16[128,16,256]{2,1,0:T(8,128)(2,1)}), bf16[128,16,256]{2,1,0:T(8,128)(2,1)S(1)}, u32[]{:S(2)}, u32[]{:S(2)}) %all-to-all-start.2) | async-done | bytes 1048608 | tf_op jit(solution)/shard_map/all_to_all | solution.py:249
  102.3 1.0 copy-done.2
  103.3 16.1 %shard_map.156 = bf16[4096,256]{1,0:T(8,128)(2,1)} custom-call(s32[1,2048]{1,0:T(1,128)} %reshape_reshape_squeeze.3.rows_ref, bf16[2048,256]{1,0:T(8,128)(2,1)} %bitcast.16, bf16[4096,256]{1,0:T(8,128)(2,1)} %mem_ref.1, bf16[256,768]{1,0:T(8,128)(2,1)} %win_ref.1, f32[1,768]{1,0:T(1,128)} %reshape.73.bin_ref, bf16[256,768]{1,0:T(8,128)(2,1)} %whid_ref.1), custom_call_target="tpu_custom_call" | custom-call | tf_op jit(solution)/shard_map/pallas_call | solution.py:52
  (6 shorter events, 0.0 us)
Async XLA Ops:
  0.0 44.4 %copy-start = (bf16[512,256]{1,0:T(8,128)(2,1)S(1)}, bf16[512,256]{1,0:T(8,128)(2,1)}, u32[]{:S(2)}) copy-start(bf16[512,256]{1,0:T(8,128)(2,1)} %param.21) | copy-start | bytes 786436
  0.0 29.3 %copy-start.3 = (bf16[4096,256]{1,0:T(8,128)(2,1)S(1)}, bf16[4096,256]{1,0:T(8,128)(2,1)}, u32[]{:S(2)}) copy-start(bf16[4096,256]{1,0:T(8,128)(2,1)} %mem_ref.1) | copy-start | bytes 6291460
  5.7 21.3 %all-to-all-start = ((s32[2,128,16]{2,0,1:T(2,128)}), s32[2,128,16]{2,0,1:T(2,128)S(1)}, u32[]{:S(2)}, u32[]{:S(2)}) async-start(s32[2,128,16]{2,0,1:T(2,128)} %copy.18), calls=%async_computation | async-start | bytes 262144 | tf_op jit(solution)/shard_map/all_to_all | solution.py:242
  39.3 4.3 %copy-start.5 = (s32[512]{0:T(512)S(1)}, s32[512]{0:T(512)}, u32[]{:S(2)}) copy-start(s32[512]{0:T(512)} %param.20) | copy-start | bytes 6148
  39.3 5.1 %copy-start.7 = (f32[512]{0:T(512)S(1)}, f32[512]{0:T(512)}, u32[]{:S(2)}) copy-start(f32[512]{0:T(512)} %param.27) | copy-start | bytes 6148
  39.3 29.4 %all-to-all-start.1 = ((bf16[128,16,384]{2,1,0:T(8,128)(2,1)}), bf16[128,16,384]{2,1,0:T(8,128)(2,1)S(1)}, u32[]{:S(2)}, u32[]{:S(2)}) async-start(bf16[128,16,384]{2,1,0:T(8,128)(2,1)} %bitcast.17), calls=%async_computation.1 | async-start | bytes 3145728 | tf_op jit(solution)/shard_map/all_to_all | solution.py:245
  68.6 1.1 copy-start.1
  78.8 4.0 %copy-start.6 = (f32[768]{0:T(1024)S(1)}, f32[768]{0:T(1024)}, u32[]{:S(2)}) copy-start(f32[768]{0:T(1024)} %param.30) | copy-start | bytes 9220
  78.8 4.6 %copy-start.4 = (s32[128,16]{1,0:T(8,128)S(1)}, s32[128,16]{1,0:T(8,128)}, u32[]{:S(2)}) copy-start(s32[128,16]{1,0:T(8,128)} %get-tuple-element.12) | copy-start | bytes 24580
  78.8 23.5 %all-to-all-start.2 = ((bf16[128,16,256]{2,1,0:T(8,128)(2,1)}), bf16[128,16,256]{2,1,0:T(8,128)(2,1)S(1)}, u32[]{:S(2)}, u32[]{:S(2)}) async-start(bf16[128,16,256]{2,1,0:T(8,128)(2,1)} %bitcast.15), calls=%async_computation.2 | async-start | bytes 2097152 | tf_op jit(solution)/shard_map/all_to_all | solution.py:249
  102.3 1.0 copy-start.2

commit v12 on v11

--- a/solution.py
+++ b/solution.py
@@ -162,8 +162,7 @@
     got = jnp.dot(digits.astype(jnp.bfloat16), placed, preferred_element_type=jnp.float32)
     got = got.astype(jnp.int32)
     row_request = jnp.where(got[4:5] > 0, got[0:1] * 64 + got[1:2], -1)
-    time_request = got[2:3] * 64 + got[3:4]
-    request_ref[...] = jnp.concatenate([row_request, time_request], axis=0)
+    request_ref[...] = row_request
     slot_ref[...] = jnp.concatenate(slots, axis=0)
     slot_t_ref[...] = jnp.concatenate([columns[:events, 0:1], columns[events:, 0:1]], axis=1)
 
@@ -176,7 +175,7 @@
         out_shape=[
             jax.ShapeDtypeStruct((2, events), jnp.int32),
             jax.ShapeDtypeStruct((events, 2), jnp.int32),
-            jax.ShapeDtypeStruct((2, slot_total), jnp.int32),
+            jax.ShapeDtypeStruct((1, slot_total), jnp.int32),
         ],
     )(owner_pair, src_row.reshape(1, events), dst_row.reshape(1, events), event_time.reshape(1, events))
 
@@ -234,13 +233,12 @@
     slot_ids, slot_cols, request = build_requests(
         src_owner, src_row, dst_owner, dst_row, event_time, slot_total
     )
-    request = request.reshape(2, devices_all, chunk)
+    request = request.reshape(slot_total)
     edge_part = (
         jnp.dot(edge_feat, w_msg_in[2 * width + time_width :], preferred_element_type=jnp.float32)
         + b_msg
     )
-    received = lax.all_to_all(request, ("ev", "node"), split_axis=1, concat_axis=1, tiled=True)
-    rows_held = received[0].reshape(-1)
+    rows_held = lax.all_to_all(request, ("ev", "node"), split_axis=0, concat_axis=0, tiled=True)
     served = owner_lookup(rows_held, memory, last_update, time_width)
     returned = lax.all_to_all(served, ("ev", "node"), split_axis=0, concat_axis=0, tiled=True)
     outgoing = event_messages(

time: 120 us -> 120 us (level)
  local copies, waits for them, and re-layouts: 8.11 us -> 5.56 us
  other arithmetic: 3.57 us -> 5.49 us
  matrix products: 12.2 us -> 13.8 us
    dot_general x1, matrix products: 9.97 us -> 11.6 us  [owner_lookup(): jnp.dot(select, table, preferred_element_type=jnp.float32)]
    slice x1 -> x0, local copies, waits for them, and re-layouts: 1.33 us -> none  [local(): rows_held = received[0].reshape(-1)]
    pallas_call x0 -> x1, other arithmetic: none -> 1.29 us  [build_requests(): pl.pallas_call(prologue_kernel, out_shape=[jax.ShapeDtypeStruct((2, event...]
  transfers between devices with their start and end apart: 3 -> 3, of which waited for: 3 -> 3; matrix products, arithmetic and copies ran while one was open for 5% -> 6% of each run, Pallas kernels for 0% -> 0%
where the time goes in v12:
time: 120 us; the launch traced here: 119 us
  waiting for transfers between devices  46.9 us (39%)
  Pallas kernels  27.7 us (23%)
  starting transfers between devices  19.8 us (16%)
  matrix products  13.8 us (12%)
  local copies, waits for them, and re-layouts  5.56 us (5%)
  other arithmetic  5.49 us (5%)
    all_to_all x1, waiting for transfers between devices, local(): lax.all_to_all(served, ('ev', 'node'), split_axis=0, concat_axis=0, tiled...  21.9 us
    all_to_all x1, waiting for transfers between devices, local(): lax.all_to_all(outgoing, ('ev', 'node'), split_axis=0, concat_axis=0, til...  17.5 us
    pallas_call x1, Pallas kernels, owner_update(): pl.pallas_call(update_kernel, grid=(rows_count // block,), in_specs=[pl.B...  16.1 us
    dot_general x1, matrix products, owner_lookup(): jnp.dot(select, table, preferred_element_type=jnp.float32)  11.6 us
    all_to_all x1, starting transfers between devices, local(): lax.all_to_all(request, ('ev', 'node'), split_axis=0, concat_axis=0, tile...  11.5 us
    pallas_call x1, Pallas kernels, event_messages(): pl.pallas_call(message_kernel, out_shape=jax.ShapeDtypeStruct((slot_total...  8.97 us
    all_to_all x1, waiting for transfers between devices, local(): lax.all_to_all(request, ('ev', 'node'), split_axis=0, concat_axis=0, tile...  7.41 us
    all_to_all x1, starting transfers between devices, local(): lax.all_to_all(served, ('ev', 'node'), split_axis=0, concat_axis=0, tiled...  4.31 us
  transfers between devices with their start and end apart: 3, of which 3 were waited for; matrix products, arithmetic and copies ran while one was open for 6% of the time, Pallas kernels for 0%

profile of v12, /device:TPU:1, one launch (start us, length us, event | category | flops | bytes accessed | tf_op | source)
XLA Modules:
  0.0 119.3 jit_solution(5141940611438306999)
XLA Ops:
  0.0 0.0 copy-start
  0.0 1.3 %add_bitcast_fusion.owner_ref = s32[2,512]{1,0:T(2,128)} fusion(s32[512,1]{0,1:T(1,128)} %param.18, s32[512,1]{0,1:T(1,128)} %param.16), kind=kLoop, calls=%fused_computation.18 | loop fusion | flops 1024 | bytes 8192 | tf_op jit(solution)/shard_map/transpose | solution.py:172
  1.3 2.7 %shard_map.154 = (s32[2,512]{1,0:T(2,128)}, s32[512,2]{1,0:T(8,128)}, s32[1,2048]{1,0:T(1,128)}) custom-call(s32[2,512]{1,0:T(2,128)} %add_bitcast_fusion.owner_ref, s32[1,512]{1,0:T(1,128)} %bitcast.22, s32[1,512]{1,0:T(1,128)} %bitcast.23, s32[1,512]{1,0:T(1,128)} %bitcast.20), custom_call_target="tpu_custom_call" | custom-call | tf_op jit(solution)/shard_map/pallas_call | solution.py:173
  4.0 0.5 broadcast.50
  4.5 1.3 %reduce.8 = s32[2048]{0:T(1024)S(1)} reduce(s32[1,2048]{1,0:T(1,128)} %get-tuple-element.8, s32[]{:T(128)} %broadcast.50), dimensions={0}, to_apply=%get-tuple-element.8.reduce_sub_computation.3 | reduce | bytes 16388 | tf_op jit(solution)/shard_map/pallas_call | solution.py:173
  5.8 0.7 all_to_all.20
  6.5 11.5 %all-to-all-start = ((s32[128,16,1]{1,2,0:T(1,128)}), s32[128,16,1]{1,2,0:T(1,128)S(1)}, u32[]{:S(2)}, u32[]{:S(2)}) async-start(s32[128,16,1]{1,2,0:T(1,128)} %bitcast.4), calls=%async_computation | async-start | bytes 131072 | tf_op jit(solution)/shard_map/all_to_all | solution.py:241
  18.0 0.7 add_select_fusion.1
  18.8 1.4 %select_convert_fusion = bf16[4096,128]{1,0:T(8,128)(2,1)S(1)} fusion(s32[4096]{0:T(1024)S(1)} %get-tuple-element.12, s32[4096]{0:T(1024)S(1)} %get-tuple-element.11, pred[128]{0:T(512)(128)(4,1)S(1)} %get-tuple-element.13, pred[128]{0:T(512)(128)(4,1)S(1)} %get-tuple-element.14), kind=kLoop, calls=%fused_computation.7 | loop fusion | flops 1572864 | bytes 1081600 | tf_op jit(solution)/shard_map/convert_element_type | solution.py:203
  20.2 7.4 %all-to-all-done = s32[128,16,1]{1,2,0:T(1,128)S(1)} async-done(((s32[128,16,1]{1,2,0:T(1,128)}), s32[128,16,1]{1,2,0:T(1,128)S(1)}, u32[]{:S(2)}, u32[]{:S(2)}) %all-to-all-start) | async-done | bytes 8224 | tf_op jit(solution)/shard_map/all_to_all | solution.py:241
  27.6 0.1 eq.39
  27.7 11.6 %fusion.5 = bf16[2048,384]{1,0:T(8,128)(2,1)} fusion(bf16[4096,128]{1,0:T(8,128)(2,1)S(1)} %select_convert_fusion, bf16[4096,256]{1,0:T(8,128)(2,1)} %mem_ref.1, s32[2048]{0:T(1024)S(1)} %eq.39), kind=kOutput, calls=%fused_computation.6 | convolution fusion | flops 6457917440 | bytes 4726784 | tf_op jit(solution)/shard_map/dot_general | solution.py:205
  39.2 0.0 copy-start.3
  39.2 0.0 copy-start.5
  39.2 4.3 %all-to-all-start.1 = ((bf16[128,16,384]{2,1,0:T(8,128)(2,1)}), bf16[128,16,384]{2,1,0:T(8,128)(2,1)S(1)}, u32[]{:S(2)}, u32[]{:S(2)}) async-start(bf16[128,16,384]{2,1,0:T(8,128)(2,1)} %bitcast.5), calls=%async_computation.1 | async-start | bytes 3145728 | tf_op jit(solution)/shard_map/all_to_all | solution.py:243
  43.5 0.0 copy-done.3
  43.6 0.9 copy.19.time_ref
  44.4 0.0 copy-done
  44.4 0.0 copy-done.5
  44.4 2.3 %convolution_add_fusion.edge_ref = f32[512,512]{1,0:T(8,128)} fusion(bf16[512,256]{1,0:T(8,128)(2,1)S(1)} %copy-done, f32[512]{0:T(512)S(1)} %copy-done.5, bf16[896,512]{1,0:T(8,128)(2,1)} %w_in_ref.1), kind=kOutput, calls=%fused_computation.8 | convolution fusion | flops 134479872 | bytes 1574912 | tf_op jit(solution)/shard_map/dot_general | solution.py:238
  46.7 21.9 %all-to-all-done.1 = bf16[128,16,384]{2,1,0:T(8,128)(2,1)S(1)} async-done(((bf16[128,16,384]{2,1,0:T(8,128)(2,1)}), bf16[128,16,384]{2,1,0:T(8,128)(2,1)S(1)}, u32[]{:S(2)}, u32[]{:S(2)}) %all-to-all-start.1) | async-done | bytes 1572896 | tf_op jit(solution)/shard_map/all_to_all | solution.py:243
  68.6 0.0 copy-start.1
  68.6 1.1 copy-done.1
  69.8 9.0 %shard_map.155 = bf16[2048,256]{1,0:T(8,128)(2,1)} custom-call(s32[512,2]{1,0:T(8,128)} %get-tuple-element.9.col_ref, s32[2,512]{1,0:T(2,128)} %get-tuple-element.10.row_ref, bf16[2048,384]{1,0:T(8,128)(2,1)} %bitcast.16, f32[512,512]{1,0:T(8,128)} %convolution_add_fusion.edge_ref, s32[512,1]{1,0:T(8,128)} %copy.19.time_ref, f32[1,128]{1,0:T(1,128)} %bitcast.24, ...), custom_call_target="tpu_custom_call" | custom-call | tf_op jit(solution)/shard_map/pallas_call | solution.py:115
  78.7 3.9 %all-to-all-start.2 = ((bf16[128,16,256]{2,1,0:T(8,128)(2,1)}), bf16[128,16,256]{2,1,0:T(8,128)(2,1)S(1)}, u32[]{:S(2)}, u32[]{:S(2)}) async-start(bf16[128,16,256]{2,1,0:T(8,128)(2,1)} %bitcast.17), calls=%async_computation.2 | async-start | bytes 2097152 | tf_op jit(solution)/shard_map/all_to_all | solution.py:247
  82.7 0.0 copy-done.4
  82.7 0.6 reshape.79.bin_ref
  83.3 0.7 reduce.9
  84.0 0.7 reshape.75.rows_ref
  84.7 17.5 %all-to-all-done.2 = bf16[128,16,256]{2,1,0:T(8,128)(2,1)S(1)} async-done(((bf16[128,16,256]{2,1,0:T(8,128)(2,1)}), bf16[128,16,256]{2,1,0:T(8,128)(2,1)S(1)}, u32[]{:S(2)}, u32[]{:S(2)}) %all-to-all-start.2) | async-done | bytes 1048608 | tf_op jit(solution)/shard_map/all_to_all | solution.py:247
  102.3 1.0 copy-done.2
  103.2 16.1 %shard_map.156 = bf16[4096,256]{1,0:T(8,128)(2,1)} custom-call(s32[1,2048]{1,0:T(1,128)} %reshape.75.rows_ref, bf16[2048,256]{1,0:T(8,128)(2,1)} %bitcast.18, bf16[4096,256]{1,0:T(8,128)(2,1)} %mem_ref.1, bf16[256,768]{1,0:T(8,128)(2,1)} %win_ref.1, f32[1,768]{1,0:T(1,128)} %reshape.79.bin_ref, bf16[256,768]{1,0:T(8,128)(2,1)} %whid_ref.1), custom_call_target="tpu_custom_call" | custom-call | tf_op jit(solution)/shard_map/pallas_call | solution.py:52
  (3 shorter events, 0.0 us)
Async XLA Ops:
  0.0 44.4 %copy-start = (bf16[512,256]{1,0:T(8,128)(2,1)S(1)}, bf16[512,256]{1,0:T(8,128)(2,1)}, u32[]{:S(2)}) copy-start(bf16[512,256]{1,0:T(8,128)(2,1)} %param.21) | copy-start | bytes 786436
  6.5 21.1 %all-to-all-start = ((s32[128,16,1]{1,2,0:T(1,128)}), s32[128,16,1]{1,2,0:T(1,128)S(1)}, u32[]{:S(2)}, u32[]{:S(2)}) async-start(s32[128,16,1]{1,2,0:T(1,128)} %bitcast.4), calls=%async_computation | async-start | bytes 131072 | tf_op jit(solution)/shard_map/all_to_all | solution.py:241
  39.2 4.3 %copy-start.3 = (s32[512]{0:T(512)S(1)}, s32[512]{0:T(512)}, u32[]{:S(2)}) copy-start(s32[512]{0:T(512)} %param.20) | copy-start | bytes 6148
  39.2 5.2 %copy-start.5 = (f32[512]{0:T(512)S(1)}, f32[512]{0:T(512)}, u32[]{:S(2)}) copy-start(f32[512]{0:T(512)} %param.27) | copy-start | bytes 6148
  39.2 29.4 %all-to-all-start.1 = ((bf16[128,16,384]{2,1,0:T(8,128)(2,1)}), bf16[128,16,384]{2,1,0:T(8,128)(2,1)S(1)}, u32[]{:S(2)}, u32[]{:S(2)}) async-start(bf16[128,16,384]{2,1,0:T(8,128)(2,1)} %bitcast.5), calls=%async_computation.1 | async-start | bytes 3145728 | tf_op jit(solution)/shard_map/all_to_all | solution.py:243
  68.6 1.1 copy-start.1
  78.7 4.0 %copy-start.4 = (f32[768]{0:T(1024)S(1)}, f32[768]{0:T(1024)}, u32[]{:S(2)}) copy-start(f32[768]{0:T(1024)} %param.30) | copy-start | bytes 9220
  78.7 23.5 %all-to-all-start.2 = ((bf16[128,16,256]{2,1,0:T(8,128)(2,1)}), bf16[128,16,256]{2,1,0:T(8,128)(2,1)S(1)}, u32[]{:S(2)}, u32[]{:S(2)}) async-start(bf16[128,16,256]{2,1,0:T(8,128)(2,1)} %bitcast.17), calls=%async_computation.2 | async-start | bytes 2097152 | tf_op jit(solution)/shard_map/all_to_all | solution.py:247
  102.2 1.0 copy-start.2

commit v13 on v12

--- a/solution.py
+++ b/solution.py
@@ -24,15 +24,14 @@
     return 0.5 + 0.5 * jnp.tanh(0.5 * x)
 
 
-def update_kernel(rows_ref, msg_ref, mem_ref, win_ref, bin_ref, whid_ref, out_ref):
+def update_kernel(rows_ref, count_ref, msg_ref, mem_ref, win_ref, bin_ref, whid_ref, out_ref):
     block = out_ref.shape[0]
     slots = rows_ref.shape[1]
     width = mem_ref.shape[1]
     ids = pl.program_id(0) * block + lax.broadcasted_iota(jnp.int32, (block, slots), 0)
     onehot = (ids == rows_ref[...]).astype(jnp.bfloat16)
     total = jnp.dot(onehot, msg_ref[...], preferred_element_type=jnp.float32)
-    ones = jnp.ones((slots, 128), jnp.bfloat16)
-    count = jnp.dot(onehot, ones, preferred_element_type=jnp.float32)[:, :1]
+    count = count_ref[...]
     mean_msg = (total / jnp.maximum(count, 1.0)).astype(jnp.bfloat16)
     state = mem_ref[...]
     input_part = jnp.dot(mean_msg, win_ref[...], preferred_element_type=jnp.float32) + bin_ref[...]
@@ -49,11 +48,15 @@
     slots, msg_width = msg_flat.shape
     block = 1024
     gates = w_gru_in.shape[1]
+    row_range = jnp.arange(rows_count, dtype=jnp.int32)
+    hits = row_range[:, None] == row_flat[None, :]
+    count = jnp.sum(hits.astype(jnp.float32), axis=1, keepdims=True)
     return pl.pallas_call(
         update_kernel,
         grid=(rows_count // block,),
         in_specs=[
             pl.BlockSpec((1, slots), lambda i: (0, 0)),
+            pl.BlockSpec((block, 1), lambda i: (i, 0)),
             pl.BlockSpec((slots, msg_width), lambda i: (0, 0)),
             pl.BlockSpec((block, width), lambda i: (i, 0)),
             pl.BlockSpec((msg_width, gates), lambda i: (0, 0)),
@@ -62,7 +65,7 @@
         ],
         out_specs=pl.BlockSpec((block, width), lambda i: (i, 0)),
         out_shape=jax.ShapeDtypeStruct(memory.shape, memory.dtype),
-    )(row_flat.reshape(1, slots), msg_flat, memory, w_gru_in, b_gru_in.reshape(1, gates), w_gru_hid)
+    )(row_flat.reshape(1, slots), count, msg_flat, memory, w_gru_in, b_gru_in.reshape(1, gates), w_gru_hid)
 
 
 def message_kernel(

time: 120 us -> 121 us (level)
  waiting for transfers between devices: 46.9 us -> 41.6 us
  other arithmetic: 5.49 us -> 8.86 us
  local copies, waits for them, and re-layouts: 5.56 us -> 7.59 us
  Pallas kernels: 27.7 us -> 29.2 us
    all_to_all x1, waiting for transfers between devices: 17.5 us -> 12.1 us  [local(): lax.all_to_all(outgoing, ('ev', 'node'), split_axis=0, concat_axis=0, til...]
    reduce_sum x0 -> x1, other arithmetic: none -> 3.4 us  [owner_update(): count = jnp.sum(hits.astype(jnp.float32), axis=1, keepdims=True)]
    broadcast_in_dim x0 -> x1, local copies, waits for them, and re-layouts: none -> 2.01 us  [owner_update(): count = jnp.sum(hits.astype(jnp.float32), axis=1, keepdims=True)]
    pallas_call x1, Pallas kernels: 16.1 us -> 17.6 us  [owner_update(): pl.pallas_call(update_kernel, grid=(rows_count // block,), in_specs=[pl.B...]
  transfers between devices with their start and end apart: 3 -> 3, of which waited for: 3 -> 3; matrix products, arithmetic and copies ran while one was open for 6% -> 10% of each run, Pallas kernels for 0% -> 0%
where the time goes in v13:
time: 121 us
  waiting for transfers between devices  41.6 us (34%)
  Pallas kernels  29.2 us (24%)
  starting transfers between devices  19.8 us (16%)
  matrix products  13.8 us (11%)
  other arithmetic  8.86 us (7%)
  local copies, waits for them, and re-layouts  7.59 us (6%)
    all_to_all x1, waiting for transfers between devices, local(): lax.all_to_all(served, ('ev', 'node'), split_axis=0, concat_axis=0, tiled...  22 us
    pallas_call x1, Pallas kernels, owner_update(): pl.pallas_call(update_kernel, grid=(rows_count // block,), in_specs=[pl.B...  17.6 us
    all_to_all x1, waiting for transfers between devices, local(): lax.all_to_all(outgoing, ('ev', 'node'), split_axis=0, concat_axis=0, til...  12.1 us
    dot_general x1, matrix products, owner_lookup(): jnp.dot(select, table, preferred_element_type=jnp.float32)  11.6 us
    all_to_all x1, starting transfers between devices, local(): lax.all_to_all(request, ('ev', 'node'), split_axis=0, concat_axis=0, tile...  11.5 us
    pallas_call x1, Pallas kernels, event_messages(): pl.pallas_call(message_kernel, out_shape=jax.ShapeDtypeStruct((slot_total...  9.01 us
    all_to_all x1, waiting for transfers between devices, local(): lax.all_to_all(request, ('ev', 'node'), split_axis=0, concat_axis=0, tile...  7.41 us
    all_to_all x1, starting transfers between devices, local(): lax.all_to_all(served, ('ev', 'node'), split_axis=0, concat_axis=0, tiled...  4.31 us
  transfers between devices with their start and end apart: 3, of which 3 were waited for; matrix products, arithmetic and copies ran while one was open for 10% of the time, Pallas kernels for 0%

profile of v13, /device:TPU:1, one launch (start us, length us, event | category | flops | bytes accessed | tf_op | source)
XLA Modules:
  0.0 120.8 jit_solution(1311825521712021712)
XLA Ops:
  0.0 0.0 copy-start
  0.0 1.3 %add_bitcast_fusion.owner_ref = s32[2,512]{1,0:T(2,128)} fusion(s32[512,1]{0,1:T(1,128)} %param.18, s32[512,1]{0,1:T(1,128)} %param.16), kind=kLoop, calls=%fused_computation.20 | loop fusion | flops 1024 | bytes 8192 | tf_op jit(solution)/shard_map/transpose | solution.py:175
  1.3 2.7 %shard_map.154 = (s32[2,512]{1,0:T(2,128)}, s32[512,2]{1,0:T(8,128)}, s32[1,2048]{1,0:T(1,128)}) custom-call(s32[2,512]{1,0:T(2,128)} %add_bitcast_fusion.owner_ref, s32[1,512]{1,0:T(1,128)} %bitcast.24, s32[1,512]{1,0:T(1,128)} %bitcast.25, s32[1,512]{1,0:T(1,128)} %bitcast.22), custom_call_target="tpu_custom_call" | custom-call | tf_op jit(solution)/shard_map/pallas_call | solution.py:176
  4.0 0.5 broadcast.50
  4.5 1.3 %reduce.8 = s32[2048]{0:T(1024)S(1)} reduce(s32[1,2048]{1,0:T(1,128)} %get-tuple-element.8, s32[]{:T(128)} %broadcast.50), dimensions={0}, to_apply=%get-tuple-element.8.reduce_sub_computation.3 | reduce | bytes 16388 | tf_op jit(solution)/shard_map/pallas_call | solution.py:176
  5.8 0.7 all_to_all.20
  6.5 11.5 %all-to-all-start = ((s32[128,16,1]{1,2,0:T(1,128)}), s32[128,16,1]{1,2,0:T(1,128)S(1)}, u32[]{:S(2)}, u32[]{:S(2)}) async-start(s32[128,16,1]{1,2,0:T(1,128)} %bitcast.4), calls=%async_computation | async-start | bytes 131072 | tf_op jit(solution)/shard_map/all_to_all | solution.py:244
  18.0 0.7 add_select_fusion.1
  18.8 1.4 %select_convert_fusion = bf16[4096,128]{1,0:T(8,128)(2,1)S(1)} fusion(s32[4096]{0:T(1024)S(1)} %get-tuple-element.12, s32[4096]{0:T(1024)S(1)} %get-tuple-element.11, pred[128]{0:T(512)(128)(4,1)S(1)} %get-tuple-element.13, pred[128]{0:T(512)(128)(4,1)S(1)} %get-tuple-element.14), kind=kLoop, calls=%fused_computation.9 | loop fusion | flops 1572864 | bytes 1081600 | tf_op jit(solution)/shard_map/convert_element_type | solution.py:206
  20.2 7.4 %all-to-all-done = s32[128,16,1]{1,2,0:T(1,128)S(1)} async-done(((s32[128,16,1]{1,2,0:T(1,128)}), s32[128,16,1]{1,2,0:T(1,128)S(1)}, u32[]{:S(2)}, u32[]{:S(2)}) %all-to-all-start) | async-done | bytes 8224 | tf_op jit(solution)/shard_map/all_to_all | solution.py:244
  27.6 0.1 eq.53
  27.6 11.6 %fusion.5 = bf16[2048,384]{1,0:T(8,128)(2,1)} fusion(bf16[4096,128]{1,0:T(8,128)(2,1)S(1)} %select_convert_fusion, bf16[4096,256]{1,0:T(8,128)(2,1)} %mem_ref.1, s32[2048]{0:T(1024)S(1)} %eq.53), kind=kOutput, calls=%fused_computation.8 | convolution fusion | flops 6457917440 | bytes 4726784 | tf_op jit(solution)/shard_map/dot_general | solution.py:208
  39.2 0.0 copy-start.3
  39.2 4.3 %all-to-all-start.1 = ((bf16[128,16,384]{2,1,0:T(8,128)(2,1)}), bf16[128,16,384]{2,1,0:T(8,128)(2,1)S(1)}, u32[]{:S(2)}, u32[]{:S(2)}) async-start(bf16[128,16,384]{2,1,0:T(8,128)(2,1)} %bitcast.6), calls=%async_computation.1 | async-start | bytes 3145728 | tf_op jit(solution)/shard_map/all_to_all | solution.py:246
  43.5 0.0 copy-done.3
  43.5 0.9 copy.23.time_ref
  44.4 0.0 copy-done
  44.4 0.0 copy-done.5
  44.4 2.2 %convolution_add_fusion.edge_ref = f32[512,512]{1,0:T(8,128)} fusion(bf16[512,256]{1,0:T(8,128)(2,1)S(1)} %copy-done, f32[512]{0:T(512)S(1)} %copy-done.5, bf16[896,512]{1,0:T(8,128)(2,1)} %w_in_ref.1), kind=kOutput, calls=%fused_computation.10 | convolution fusion | flops 134479872 | bytes 1574912 | tf_op jit(solution)/shard_map/dot_general | solution.py:241
  46.6 22.0 %all-to-all-done.1 = bf16[128,16,384]{2,1,0:T(8,128)(2,1)S(1)} async-done(((bf16[128,16,384]{2,1,0:T(8,128)(2,1)}), bf16[128,16,384]{2,1,0:T(8,128)(2,1)S(1)}, u32[]{:S(2)}, u32[]{:S(2)}) %all-to-all-start.1) | async-done | bytes 1572896 | tf_op jit(solution)/shard_map/all_to_all | solution.py:246
  68.6 1.1 copy-done.1
  69.8 9.0 %shard_map.155 = bf16[2048,256]{1,0:T(8,128)(2,1)} custom-call(s32[512,2]{1,0:T(8,128)} %get-tuple-element.9.col_ref, s32[2,512]{1,0:T(2,128)} %get-tuple-element.10.row_ref, bf16[2048,384]{1,0:T(8,128)(2,1)} %bitcast.17, f32[512,512]{1,0:T(8,128)} %convolution_add_fusion.edge_ref, s32[512,1]{1,0:T(8,128)} %copy.23.time_ref, f32[1,128]{1,0:T(1,128)} %bitcast.26, ...), custom_call_target="tpu_custom_call" | custom-call | tf_op jit(solution)/shard_map/pallas_call | solution.py:118
  78.8 3.9 %all-to-all-start.2 = ((bf16[128,16,256]{2,1,0:T(8,128)(2,1)}), bf16[128,16,256]{2,1,0:T(8,128)(2,1)S(1)}, u32[]{:S(2)}, u32[]{:S(2)}) async-start(bf16[128,16,256]{2,1,0:T(8,128)(2,1)} %bitcast.18), calls=%async_computation.2 | async-start | bytes 2097152 | tf_op jit(solution)/shard_map/all_to_all | solution.py:250
  82.7 0.0 copy-done.4
  82.7 0.6 reshape.80.bin_ref
  83.3 0.7 reduce.9
  84.0 0.7 reshape.76.rows_ref
  84.7 3.4 %convert_reduce_fusion = f32[4096]{0:T(1024)S(1)} fusion(s32[2048]{0:T(1024)S(1)} %eq.53), kind=kLoop, calls=%fused_computation.1 | loop fusion | flops 25161728 | bytes 24576 | tf_op jit(solution)/shard_map/reduce_sum | solution.py:53
  88.1 2.0 %copy.24.count_ref = f32[4096,1]{1,0:T(8,128)} copy(f32[4096,1]{0,1:T(1,128)S(1)} %bitcast.21) | data formatting | bytes 32768 | tf_op jit(solution)/shard_map/broadcast_in_dim | solution.py:53
  90.1 12.1 %all-to-all-done.2 = bf16[128,16,256]{2,1,0:T(8,128)(2,1)S(1)} async-done(((bf16[128,16,256]{2,1,0:T(8,128)(2,1)}), bf16[128,16,256]{2,1,0:T(8,128)(2,1)S(1)}, u32[]{:S(2)}, u32[]{:S(2)}) %all-to-all-start.2) | async-done | bytes 1048608 | tf_op jit(solution)/shard_map/all_to_all | solution.py:250
  102.3 1.0 copy-done.2
  103.3 17.6 %shard_map.156 = bf16[4096,256]{1,0:T(8,128)(2,1)} custom-call(s32[1,2048]{1,0:T(1,128)} %reshape.76.rows_ref, f32[4096,1]{1,0:T(8,128)} %copy.24.count_ref, bf16[2048,256]{1,0:T(8,128)(2,1)} %bitcast.19, bf16[4096,256]{1,0:T(8,128)(2,1)} %mem_ref.1, bf16[256,768]{1,0:T(8,128)(2,1)} %win_ref.1, f32[1,768]{1,0:T(1,128)} %reshape.80.bin_ref, ...), custom_call_target="tpu_custom_call" | custom-call | tf_op jit(solution)/shard_map/pallas_call | solution.py:54
  (5 shorter events, 0.0 us)
Async XLA Ops:
  0.0 44.4 %copy-start = (bf16[512,256]{1,0:T(8,128)(2,1)S(1)}, bf16[512,256]{1,0:T(8,128)(2,1)}, u32[]{:S(2)}) copy-start(bf16[512,256]{1,0:T(8,128)(2,1)} %param.21) | copy-start | bytes 786436
  6.5 21.1 %all-to-all-start = ((s32[128,16,1]{1,2,0:T(1,128)}), s32[128,16,1]{1,2,0:T(1,128)S(1)}, u32[]{:S(2)}, u32[]{:S(2)}) async-start(s32[128,16,1]{1,2,0:T(1,128)} %bitcast.4), calls=%async_computation | async-start | bytes 131072 | tf_op jit(solution)/shard_map/all_to_all | solution.py:244
  39.2 4.3 %copy-start.3 = (s32[512]{0:T(512)S(1)}, s32[512]{0:T(512)}, u32[]{:S(2)}) copy-start(s32[512]{0:T(512)} %param.20) | copy-start | bytes 6148
  39.2 5.2 %copy-start.5 = (f32[512]{0:T(512)S(1)}, f32[512]{0:T(512)}, u32[]{:S(2)}) copy-start(f32[512]{0:T(512)} %param.27) | copy-start | bytes 6148
  39.2 29.4 %all-to-all-start.1 = ((bf16[128,16,384]{2,1,0:T(8,128)(2,1)}), bf16[128,16,384]{2,1,0:T(8,128)(2,1)S(1)}, u32[]{:S(2)}, u32[]{:S(2)}) async-start(bf16[128,16,384]{2,1,0:T(8,128)(2,1)} %bitcast.6), calls=%async_computation.1 | async-start | bytes 3145728 | tf_op jit(solution)/shard_map/all_to_all | solution.py:246
  68.6 1.1 copy-start.1
  78.8 4.0 %copy-start.4 = (f32[768]{0:T(1024)S(1)}, f32[768]{0:T(1024)}, u32[]{:S(2)}) copy-start(f32[768]{0:T(1024)} %param.30) | copy-start | bytes 9220
  78.8 23.5 %all-to-all-start.2 = ((bf16[128,16,256]{2,1,0:T(8,128)(2,1)}), bf16[128,16,256]{2,1,0:T(8,128)(2,1)S(1)}, u32[]{:S(2)}, u32[]{:S(2)}) async-start(bf16[128,16,256]{2,1,0:T(8,128)(2,1)} %bitcast.18), calls=%async_computation.2 | async-start | bytes 2097152 | tf_op jit(solution)/shard_map/all_to_all | solution.py:250
  102.3 1.0 copy-start.2

commit v14 on v12

--- a/solution.py
+++ b/solution.py
@@ -47,7 +47,7 @@
 def owner_update(row_flat, msg_flat, memory, w_gru_in, b_gru_in, w_gru_hid):
     rows_count, width = memory.shape
     slots, msg_width = msg_flat.shape
-    block = 1024
+    block = 2048
     gates = w_gru_in.shape[1]
     return pl.pallas_call(
         update_kernel,

time: 120 us -> 120 us (level)
  no operation moved by 1% of the time
where the time goes in v14:
time: 120 us
  waiting for transfers between devices  46.9 us (39%)
  Pallas kernels  27.9 us (23%)
  starting transfers between devices  19.8 us (16%)
  matrix products  13.8 us (12%)
  local copies, waits for them, and re-layouts  5.56 us (5%)
  other arithmetic  5.49 us (5%)
    all_to_all x1, waiting for transfers between devices, local(): lax.all_to_all(served, ('ev', 'node'), split_axis=0, concat_axis=0, tiled...  21.9 us
    all_to_all x1, waiting for transfers between devices, local(): lax.all_to_all(outgoing, ('ev', 'node'), split_axis=0, concat_axis=0, til...  17.5 us
    pallas_call x1, Pallas kernels, owner_update(): pl.pallas_call(update_kernel, grid=(rows_count // block,), in_specs=[pl.B...  16.3 us
    dot_general x1, matrix products, owner_lookup(): jnp.dot(select, table, preferred_element_type=jnp.float32)  11.6 us
    all_to_all x1, starting transfers between devices, local(): lax.all_to_all(request, ('ev', 'node'), split_axis=0, concat_axis=0, tile...  11.5 us
    pallas_call x1, Pallas kernels, event_messages(): pl.pallas_call(message_kernel, out_shape=jax.ShapeDtypeStruct((slot_total...  8.97 us
    all_to_all x1, waiting for transfers between devices, local(): lax.all_to_all(request, ('ev', 'node'), split_axis=0, concat_axis=0, tile...  7.41 us
    all_to_all x1, starting transfers between devices, local(): lax.all_to_all(served, ('ev', 'node'), split_axis=0, concat_axis=0, tiled...  4.31 us
  transfers between devices with their start and end apart: 3, of which 3 were waited for; matrix products, arithmetic and copies ran while one was open for 6% of the time, Pallas kernels for 0%

profile of v14, /device:TPU:1, one launch (start us, length us, event | category | flops | bytes accessed | tf_op | source)
XLA Modules:
  0.0 119.5 jit_solution(15791033251225779125)
XLA Ops:
  0.0 0.0 copy-start
  0.0 1.3 %add_bitcast_fusion.owner_ref = s32[2,512]{1,0:T(2,128)} fusion(s32[512,1]{0,1:T(1,128)} %param.18, s32[512,1]{0,1:T(1,128)} %param.16), kind=kLoop, calls=%fused_computation.18 | loop fusion | flops 1024 | bytes 8192 | tf_op jit(solution)/shard_map/transpose | solution.py:172
  1.3 2.7 %shard_map.154 = (s32[2,512]{1,0:T(2,128)}, s32[512,2]{1,0:T(8,128)}, s32[1,2048]{1,0:T(1,128)}) custom-call(s32[2,512]{1,0:T(2,128)} %add_bitcast_fusion.owner_ref, s32[1,512]{1,0:T(1,128)} %bitcast.22, s32[1,512]{1,0:T(1,128)} %bitcast.23, s32[1,512]{1,0:T(1,128)} %bitcast.20), custom_call_target="tpu_custom_call" | custom-call | tf_op jit(solution)/shard_map/pallas_call | solution.py:173
  4.0 0.5 broadcast.50
  4.5 1.3 %reduce.8 = s32[2048]{0:T(1024)S(1)} reduce(s32[1,2048]{1,0:T(1,128)} %get-tuple-element.8, s32[]{:T(128)} %broadcast.50), dimensions={0}, to_apply=%get-tuple-element.8.reduce_sub_computation.3 | reduce | bytes 16388 | tf_op jit(solution)/shard_map/pallas_call | solution.py:173
  5.8 0.7 all_to_all.20
  6.5 11.5 %all-to-all-start = ((s32[128,16,1]{1,2,0:T(1,128)}), s32[128,16,1]{1,2,0:T(1,128)S(1)}, u32[]{:S(2)}, u32[]{:S(2)}) async-start(s32[128,16,1]{1,2,0:T(1,128)} %bitcast.4), calls=%async_computation | async-start | bytes 131072 | tf_op jit(solution)/shard_map/all_to_all | solution.py:241
  18.0 0.7 add_select_fusion.1
  18.8 1.4 %select_convert_fusion = bf16[4096,128]{1,0:T(8,128)(2,1)S(1)} fusion(s32[4096]{0:T(1024)S(1)} %get-tuple-element.12, s32[4096]{0:T(1024)S(1)} %get-tuple-element.11, pred[128]{0:T(512)(128)(4,1)S(1)} %get-tuple-element.13, pred[128]{0:T(512)(128)(4,1)S(1)} %get-tuple-element.14), kind=kLoop, calls=%fused_computation.7 | loop fusion | flops 1572864 | bytes 1081600 | tf_op jit(solution)/shard_map/convert_element_type | solution.py:203
  20.2 7.4 %all-to-all-done = s32[128,16,1]{1,2,0:T(1,128)S(1)} async-done(((s32[128,16,1]{1,2,0:T(1,128)}), s32[128,16,1]{1,2,0:T(1,128)S(1)}, u32[]{:S(2)}, u32[]{:S(2)}) %all-to-all-start) | async-done | bytes 8224 | tf_op jit(solution)/shard_map/all_to_all | solution.py:241
  27.6 0.1 eq.39
  27.7 11.6 %fusion.5 = bf16[2048,384]{1,0:T(8,128)(2,1)} fusion(bf16[4096,128]{1,0:T(8,128)(2,1)S(1)} %select_convert_fusion, bf16[4096,256]{1,0:T(8,128)(2,1)} %mem_ref.1, s32[2048]{0:T(1024)S(1)} %eq.39), kind=kOutput, calls=%fused_computation.6 | convolution fusion | flops 6457917440 | bytes 4726784 | tf_op jit(solution)/shard_map/dot_general | solution.py:205
  39.2 0.0 copy-start.3
  39.2 0.0 copy-start.5
  39.2 4.3 %all-to-all-start.1 = ((bf16[128,16,384]{2,1,0:T(8,128)(2,1)}), bf16[128,16,384]{2,1,0:T(8,128)(2,1)S(1)}, u32[]{:S(2)}, u32[]{:S(2)}) async-start(bf16[128,16,384]{2,1,0:T(8,128)(2,1)} %bitcast.5), calls=%async_computation.1 | async-start | bytes 3145728 | tf_op jit(solution)/shard_map/all_to_all | solution.py:243
  43.5 0.0 copy-done.3
  43.6 0.9 copy.19.time_ref
  44.4 0.0 copy-done
  44.4 0.0 copy-done.5
  44.4 2.3 %convolution_add_fusion.edge_ref = f32[512,512]{1,0:T(8,128)} fusion(bf16[512,256]{1,0:T(8,128)(2,1)S(1)} %copy-done, f32[512]{0:T(512)S(1)} %copy-done.5, bf16[896,512]{1,0:T(8,128)(2,1)} %w_in_ref.1), kind=kOutput, calls=%fused_computation.8 | convolution fusion | flops 134479872 | bytes 1574912 | tf_op jit(solution)/shard_map/dot_general | solution.py:238
  46.7 21.9 %all-to-all-done.1 = bf16[128,16,384]{2,1,0:T(8,128)(2,1)S(1)} async-done(((bf16[128,16,384]{2,1,0:T(8,128)(2,1)}), bf16[128,16,384]{2,1,0:T(8,128)(2,1)S(1)}, u32[]{:S(2)}, u32[]{:S(2)}) %all-to-all-start.1) | async-done | bytes 1572896 | tf_op jit(solution)/shard_map/all_to_all | solution.py:243
  68.6 0.0 copy-start.1
  68.6 1.1 copy-done.1
  69.8 9.0 %shard_map.155 = bf16[2048,256]{1,0:T(8,128)(2,1)} custom-call(s32[512,2]{1,0:T(8,128)} %get-tuple-element.9.col_ref, s32[2,512]{1,0:T(2,128)} %get-tuple-element.10.row_ref, bf16[2048,384]{1,0:T(8,128)(2,1)} %bitcast.16, f32[512,512]{1,0:T(8,128)} %convolution_add_fusion.edge_ref, s32[512,1]{1,0:T(8,128)} %copy.19.time_ref, f32[1,128]{1,0:T(1,128)} %bitcast.24, ...), custom_call_target="tpu_custom_call" | custom-call | tf_op jit(solution)/shard_map/pallas_call | solution.py:115
  78.7 3.9 %all-to-all-start.2 = ((bf16[128,16,256]{2,1,0:T(8,128)(2,1)}), bf16[128,16,256]{2,1,0:T(8,128)(2,1)S(1)}, u32[]{:S(2)}, u32[]{:S(2)}) async-start(bf16[128,16,256]{2,1,0:T(8,128)(2,1)} %bitcast.17), calls=%async_computation.2 | async-start | bytes 2097152 | tf_op jit(solution)/shard_map/all_to_all | solution.py:247
  82.7 0.0 copy-done.4
  82.7 0.6 reshape.79.bin_ref
  83.3 0.7 reduce.9
  84.0 0.7 reshape.75.rows_ref
  84.7 17.5 %all-to-all-done.2 = bf16[128,16,256]{2,1,0:T(8,128)(2,1)S(1)} async-done(((bf16[128,16,256]{2,1,0:T(8,128)(2,1)}), bf16[128,16,256]{2,1,0:T(8,128)(2,1)S(1)}, u32[]{:S(2)}, u32[]{:S(2)}) %all-to-all-start.2) | async-done | bytes 1048608 | tf_op jit(solution)/shard_map/all_to_all | solution.py:247
  102.3 1.0 copy-done.2
  103.2 16.3 %shard_map.156 = bf16[4096,256]{1,0:T(8,128)(2,1)} custom-call(s32[1,2048]{1,0:T(1,128)} %reshape.75.rows_ref, bf16[2048,256]{1,0:T(8,128)(2,1)} %bitcast.18, bf16[4096,256]{1,0:T(8,128)(2,1)} %mem_ref.1, bf16[256,768]{1,0:T(8,128)(2,1)} %win_ref.1, f32[1,768]{1,0:T(1,128)} %reshape.79.bin_ref, bf16[256,768]{1,0:T(8,128)(2,1)} %whid_ref.1), custom_call_target="tpu_custom_call" | custom-call | tf_op jit(solution)/shard_map/pallas_call | solution.py:52
  (3 shorter events, 0.0 us)
Async XLA Ops:
  0.0 44.4 %copy-start = (bf16[512,256]{1,0:T(8,128)(2,1)S(1)}, bf16[512,256]{1,0:T(8,128)(2,1)}, u32[]{:S(2)}) copy-start(bf16[512,256]{1,0:T(8,128)(2,1)} %param.21) | copy-start | bytes 786436
  6.5 21.1 %all-to-all-start = ((s32[128,16,1]{1,2,0:T(1,128)}), s32[128,16,1]{1,2,0:T(1,128)S(1)}, u32[]{:S(2)}, u32[]{:S(2)}) async-start(s32[128,16,1]{1,2,0:T(1,128)} %bitcast.4), calls=%async_computation | async-start | bytes 131072 | tf_op jit(solution)/shard_map/all_to_all | solution.py:241
  39.2 4.3 %copy-start.3 = (s32[512]{0:T(512)S(1)}, s32[512]{0:T(512)}, u32[]{:S(2)}) copy-start(s32[512]{0:T(512)} %param.20) | copy-start | bytes 6148
  39.2 5.2 %copy-start.5 = (f32[512]{0:T(512)S(1)}, f32[512]{0:T(512)}, u32[]{:S(2)}) copy-start(f32[512]{0:T(512)} %param.27) | copy-start | bytes 6148
  39.2 29.4 %all-to-all-start.1 = ((bf16[128,16,384]{2,1,0:T(8,128)(2,1)}), bf16[128,16,384]{2,1,0:T(8,128)(2,1)S(1)}, u32[]{:S(2)}, u32[]{:S(2)}) async-start(bf16[128,16,384]{2,1,0:T(8,128)(2,1)} %bitcast.5), calls=%async_computation.1 | async-start | bytes 3145728 | tf_op jit(solution)/shard_map/all_to_all | solution.py:243
  68.6 1.1 copy-start.1
  78.7 4.0 %copy-start.4 = (f32[768]{0:T(1024)S(1)}, f32[768]{0:T(1024)}, u32[]{:S(2)}) copy-start(f32[768]{0:T(1024)} %param.30) | copy-start | bytes 9220
  78.7 23.5 %all-to-all-start.2 = ((bf16[128,16,256]{2,1,0:T(8,128)(2,1)}), bf16[128,16,256]{2,1,0:T(8,128)(2,1)S(1)}, u32[]{:S(2)}, u32[]{:S(2)}) async-start(bf16[128,16,256]{2,1,0:T(8,128)(2,1)} %bitcast.17), calls=%async_computation.2 | async-start | bytes 2097152 | tf_op jit(solution)/shard_map/all_to_all | solution.py:247
  102.2 1.0 copy-start.2

commit v15 on v12

--- a/solution.py
+++ b/solution.py
@@ -2,6 +2,7 @@
 import jax.numpy as jnp
 from jax import lax
 from jax.experimental import pallas as pl
+from jax.experimental.pallas import tpu as pltpu
 from jax.sharding import PartitionSpec as P
 
 
@@ -66,8 +67,28 @@
 
 
 def message_kernel(
-    col_ref, row_ref, fetched_ref, edge_ref, time_ref, freq_ref, phase_ref, w_in_ref, w_out_ref, out_ref
+    col_ref,
+    row_ref,
+    fetched_ref,
+    edge_hbm,
+    time_ref,
+    freq_ref,
+    phase_ref,
+    w_in_hbm,
+    w_out_hbm,
+    out_ref,
+    edge_ref,
+    w_in_ref,
+    w_out_ref,
+    sems,
 ):
+    copies = [
+        pltpu.make_async_copy(edge_hbm, edge_ref, sems.at[0]),
+        pltpu.make_async_copy(w_in_hbm, w_in_ref, sems.at[1]),
+        pltpu.make_async_copy(w_out_hbm, w_out_ref, sems.at[2]),
+    ]
+    for copy in copies:
+        copy.start()
     events = edge_ref.shape[0]
     slot_total = fetched_ref.shape[0]
     width = out_ref.shape[1]
@@ -84,6 +105,8 @@
         picked.append((rows[:, :width].astype(jnp.bfloat16), encoded))
     mem_src, enc_src = picked[0]
     mem_dst, enc_dst = picked[1]
+    for copy in copies:
+        copy.wait()
     w_self = w_in_ref[:width]
     w_other = w_in_ref[width : 2 * width]
     w_time = w_in_ref[2 * width : 2 * width + time_width]
@@ -112,8 +135,18 @@
 ):
     slot_total = fetched.shape[0]
     msg_width = w_msg_out.shape[1]
+    here = pl.BlockSpec(memory_space=pltpu.VMEM)
+    away = pl.BlockSpec(memory_space=pl.ANY)
     return pl.pallas_call(
         message_kernel,
+        in_specs=[here, here, here, away, here, here, here, away, away],
+        out_specs=here,
+        scratch_shapes=[
+            pltpu.VMEM(edge_part.shape, edge_part.dtype),
+            pltpu.VMEM(w_msg_in.shape, w_msg_in.dtype),
+            pltpu.VMEM(w_msg_out.shape, w_msg_out.dtype),
+            pltpu.SemaphoreType.DMA((3,)),
+        ],
         out_shape=jax.ShapeDtypeStruct((slot_total, msg_width), jnp.bfloat16),
     )(
         slot_cols,

time: 120 us -> 120 us (level)
  no operation moved by 1% of the time
where the time goes in v15:
time: 120 us
  waiting for transfers between devices  46.9 us (39%)
  Pallas kernels  28.2 us (24%)
  starting transfers between devices  19.7 us (16%)
  matrix products  13.8 us (12%)
  local copies, waits for them, and re-layouts  5.57 us (5%)
  other arithmetic  5.49 us (5%)
    all_to_all x1, waiting for transfers between devices, local(): lax.all_to_all(served, ('ev', 'node'), split_axis=0, concat_axis=0, tiled...  21.9 us
    all_to_all x1, waiting for transfers between devices, local(): lax.all_to_all(outgoing, ('ev', 'node'), split_axis=0, concat_axis=0, til...  17.5 us
    pallas_call x1, Pallas kernels, owner_update(): pl.pallas_call(update_kernel, grid=(rows_count // block,), in_specs=[pl.B...  16.1 us
    dot_general x1, matrix products, owner_lookup(): jnp.dot(select, table, preferred_element_type=jnp.float32)  11.6 us
    all_to_all x1, starting transfers between devices, local(): lax.all_to_all(request, ('ev', 'node'), split_axis=0, concat_axis=0, tile...  11.5 us
    pallas_call x1, Pallas kernels, event_messages(): pl.pallas_call(message_kernel, in_specs=[here, here, here, away, here, he...  9.47 us
    all_to_all x1, waiting for transfers between devices, local(): lax.all_to_all(request, ('ev', 'node'), split_axis=0, concat_axis=0, tile...  7.41 us
    all_to_all x1, starting transfers between devices, local(): lax.all_to_all(served, ('ev', 'node'), split_axis=0, concat_axis=0, tiled...  4.31 us
  transfers between devices with their start and end apart: 3, of which 3 were waited for; matrix products, arithmetic and copies ran while one was open for 6% of the time, Pallas kernels for 0%

profile of v15, /device:TPU:1, one launch (start us, length us, event | category | flops | bytes accessed | tf_op | source)
XLA Modules:
  0.0 119.7 jit_solution(3198202967006193619)
XLA Ops:
  0.0 0.0 copy-start
  0.0 1.3 %add_bitcast_fusion.owner_ref = s32[2,512]{1,0:T(2,128)} fusion(s32[512,1]{0,1:T(1,128)} %param.18, s32[512,1]{0,1:T(1,128)} %param.16), kind=kLoop, calls=%fused_computation.18 | loop fusion | flops 1024 | bytes 8192 | tf_op jit(solution)/shard_map/transpose | solution.py:205
  1.3 2.7 %shard_map.154 = (s32[2,512]{1,0:T(2,128)}, s32[512,2]{1,0:T(8,128)}, s32[1,2048]{1,0:T(1,128)}) custom-call(s32[2,512]{1,0:T(2,128)} %add_bitcast_fusion.owner_ref, s32[1,512]{1,0:T(1,128)} %bitcast.22, s32[1,512]{1,0:T(1,128)} %bitcast.23, s32[1,512]{1,0:T(1,128)} %bitcast.20), custom_call_target="tpu_custom_call" | custom-call | tf_op jit(solution)/shard_map/pallas_call | solution.py:206
  4.0 0.5 broadcast.50
  4.5 1.3 %reduce.8 = s32[2048]{0:T(1024)S(1)} reduce(s32[1,2048]{1,0:T(1,128)} %get-tuple-element.8, s32[]{:T(128)} %broadcast.50), dimensions={0}, to_apply=%get-tuple-element.8.reduce_sub_computation.3 | reduce | bytes 16388 | tf_op jit(solution)/shard_map/pallas_call | solution.py:206
  5.8 0.7 all_to_all.20
  6.5 11.5 %all-to-all-start = ((s32[128,16,1]{1,2,0:T(1,128)}), s32[128,16,1]{1,2,0:T(1,128)S(1)}, u32[]{:S(2)}, u32[]{:S(2)}) async-start(s32[128,16,1]{1,2,0:T(1,128)} %bitcast.4), calls=%async_computation | async-start | bytes 131072 | tf_op jit(solution)/shard_map/all_to_all | solution.py:274
  18.0 0.7 add_select_fusion.1
  18.8 1.4 %select_convert_fusion = bf16[4096,128]{1,0:T(8,128)(2,1)S(1)} fusion(s32[4096]{0:T(1024)S(1)} %get-tuple-element.12, s32[4096]{0:T(1024)S(1)} %get-tuple-element.11, pred[128]{0:T(512)(128)(4,1)S(1)} %get-tuple-element.13, pred[128]{0:T(512)(128)(4,1)S(1)} %get-tuple-element.14), kind=kLoop, calls=%fused_computation.7 | loop fusion | flops 1572864 | bytes 1081600 | tf_op jit(solution)/shard_map/convert_element_type | solution.py:236
  20.2 7.4 %all-to-all-done = s32[128,16,1]{1,2,0:T(1,128)S(1)} async-done(((s32[128,16,1]{1,2,0:T(1,128)}), s32[128,16,1]{1,2,0:T(1,128)S(1)}, u32[]{:S(2)}, u32[]{:S(2)}) %all-to-all-start) | async-done | bytes 8224 | tf_op jit(solution)/shard_map/all_to_all | solution.py:274
  27.6 0.1 eq.39
  27.7 11.6 %fusion.5 = bf16[2048,384]{1,0:T(8,128)(2,1)} fusion(bf16[4096,128]{1,0:T(8,128)(2,1)S(1)} %select_convert_fusion, bf16[4096,256]{1,0:T(8,128)(2,1)} %mem_ref.1, s32[2048]{0:T(1024)S(1)} %eq.39), kind=kOutput, calls=%fused_computation.6 | convolution fusion | flops 6457917440 | bytes 4726784 | tf_op jit(solution)/shard_map/dot_general | solution.py:238
  39.2 0.0 copy-start.3
  39.2 4.3 %all-to-all-start.1 = ((bf16[128,16,384]{2,1,0:T(8,128)(2,1)}), bf16[128,16,384]{2,1,0:T(8,128)(2,1)S(1)}, u32[]{:S(2)}, u32[]{:S(2)}) async-start(bf16[128,16,384]{2,1,0:T(8,128)(2,1)} %bitcast.5), calls=%async_computation.1 | async-start | bytes 3145728 | tf_op jit(solution)/shard_map/all_to_all | solution.py:276
  43.5 0.0 copy-done.3
  43.6 0.9 copy.19.time_ref
  44.4 0.0 copy-done
  44.4 0.0 copy-done.5
  44.4 2.3 %convolution_add_fusion.edge_hbm = f32[512,512]{1,0:T(8,128)} fusion(bf16[512,256]{1,0:T(8,128)(2,1)S(1)} %copy-done, f32[512]{0:T(512)S(1)} %copy-done.5, bf16[896,512]{1,0:T(8,128)(2,1)} %w_in_hbm.1), kind=kOutput, calls=%fused_computation.8 | convolution fusion | flops 134479872 | bytes 1574912 | tf_op jit(solution)/shard_map/dot_general | solution.py:271
  46.7 21.9 %all-to-all-done.1 = bf16[128,16,384]{2,1,0:T(8,128)(2,1)S(1)} async-done(((bf16[128,16,384]{2,1,0:T(8,128)(2,1)}), bf16[128,16,384]{2,1,0:T(8,128)(2,1)S(1)}, u32[]{:S(2)}, u32[]{:S(2)}) %all-to-all-start.1) | async-done | bytes 1572896 | tf_op jit(solution)/shard_map/all_to_all | solution.py:276
  68.6 0.0 copy-start.1
  68.6 1.1 copy-done.1
  69.8 9.5 %shard_map.155 = bf16[2048,256]{1,0:T(8,128)(2,1)} custom-call(s32[512,2]{1,0:T(8,128)} %get-tuple-element.9.col_ref, s32[2,512]{1,0:T(2,128)} %get-tuple-element.10.row_ref, bf16[2048,384]{1,0:T(8,128)(2,1)} %bitcast.16, f32[512,512]{1,0:T(8,128)} %convolution_add_fusion.edge_hbm, s32[512,1]{1,0:T(8,128)} %copy.19.time_ref, f32[1,128]{1,0:T(1,128)} %bitcast.24, ...), custom_call_target="tpu_custom_call" | custom-call | tf_op jit(solution)/shard_map/pallas_call | solution.py:140
  79.2 0.0 copy-start.4
  79.3 3.9 %all-to-all-start.2 = ((bf16[128,16,256]{2,1,0:T(8,128)(2,1)}), bf16[128,16,256]{2,1,0:T(8,128)(2,1)S(1)}, u32[]{:S(2)}, u32[]{:S(2)}) async-start(bf16[128,16,256]{2,1,0:T(8,128)(2,1)} %bitcast.17), calls=%async_computation.2 | async-start | bytes 2097152 | tf_op jit(solution)/shard_map/all_to_all | solution.py:280
  83.1 0.0 copy-done.4
  83.1 0.6 reshape.79.bin_ref
  83.7 0.7 reduce.9
  84.5 0.7 reshape.75.rows_ref
  85.2 17.5 %all-to-all-done.2 = bf16[128,16,256]{2,1,0:T(8,128)(2,1)S(1)} async-done(((bf16[128,16,256]{2,1,0:T(8,128)(2,1)}), bf16[128,16,256]{2,1,0:T(8,128)(2,1)S(1)}, u32[]{:S(2)}, u32[]{:S(2)}) %all-to-all-start.2) | async-done | bytes 1048608 | tf_op jit(solution)/shard_map/all_to_all | solution.py:280
  102.7 1.0 copy-done.2
  103.6 16.1 %shard_map.156 = bf16[4096,256]{1,0:T(8,128)(2,1)} custom-call(s32[1,2048]{1,0:T(1,128)} %reshape.75.rows_ref, bf16[2048,256]{1,0:T(8,128)(2,1)} %bitcast.18, bf16[4096,256]{1,0:T(8,128)(2,1)} %mem_ref.1, bf16[256,768]{1,0:T(8,128)(2,1)} %win_ref.1, f32[1,768]{1,0:T(1,128)} %reshape.79.bin_ref, bf16[256,768]{1,0:T(8,128)(2,1)} %whid_ref.1), custom_call_target="tpu_custom_call" | custom-call | tf_op jit(solution)/shard_map/pallas_call | solution.py:53
  (3 shorter events, 0.0 us)
Async XLA Ops:
  0.0 44.4 %copy-start = (bf16[512,256]{1,0:T(8,128)(2,1)S(1)}, bf16[512,256]{1,0:T(8,128)(2,1)}, u32[]{:S(2)}) copy-start(bf16[512,256]{1,0:T(8,128)(2,1)} %param.21) | copy-start | bytes 786436
  6.5 21.1 %all-to-all-start = ((s32[128,16,1]{1,2,0:T(1,128)}), s32[128,16,1]{1,2,0:T(1,128)S(1)}, u32[]{:S(2)}, u32[]{:S(2)}) async-start(s32[128,16,1]{1,2,0:T(1,128)} %bitcast.4), calls=%async_computation | async-start | bytes 131072 | tf_op jit(solution)/shard_map/all_to_all | solution.py:274
  39.2 4.3 %copy-start.3 = (s32[512]{0:T(512)S(1)}, s32[512]{0:T(512)}, u32[]{:S(2)}) copy-start(s32[512]{0:T(512)} %param.20) | copy-start | bytes 6148
  39.2 5.2 %copy-start.5 = (f32[512]{0:T(512)S(1)}, f32[512]{0:T(512)}, u32[]{:S(2)}) copy-start(f32[512]{0:T(512)} %param.27) | copy-start | bytes 6148
  39.2 29.4 %all-to-all-start.1 = ((bf16[128,16,384]{2,1,0:T(8,128)(2,1)}), bf16[128,16,384]{2,1,0:T(8,128)(2,1)S(1)}, u32[]{:S(2)}, u32[]{:S(2)}) async-start(bf16[128,16,384]{2,1,0:T(8,128)(2,1)} %bitcast.5), calls=%async_computation.1 | async-start | bytes 3145728 | tf_op jit(solution)/shard_map/all_to_all | solution.py:276
  68.6 1.1 copy-start.1
  79.2 3.9 %copy-start.4 = (f32[768]{0:T(1024)S(1)}, f32[768]{0:T(1024)}, u32[]{:S(2)}) copy-start(f32[768]{0:T(1024)} %param.30) | copy-start | bytes 9220
  79.3 23.4 %all-to-all-start.2 = ((bf16[128,16,256]{2,1,0:T(8,128)(2,1)}), bf16[128,16,256]{2,1,0:T(8,128)(2,1)S(1)}, u32[]{:S(2)}, u32[]{:S(2)}) async-start(bf16[128,16,256]{2,1,0:T(8,128)(2,1)} %bitcast.17), calls=%async_computation.2 | async-start | bytes 2097152 | tf_op jit(solution)/shard_map/all_to_all | solution.py:280
  102.7 1.0 copy-start.2

commit v16 on v12

--- a/solution.py
+++ b/solution.py
@@ -132,7 +132,7 @@
     events = owner_ref.shape[1]
     owners = 128
     capacity = 8
-    slot_total = request_ref.shape[1]
+    slot_total = request_ref.shape[-1]
     chunk = slot_total // owners
     upper = (
         lax.broadcasted_iota(jnp.int32, (events, events), 0)
@@ -162,7 +162,7 @@
     got = jnp.dot(digits.astype(jnp.bfloat16), placed, preferred_element_type=jnp.float32)
     got = got.astype(jnp.int32)
     row_request = jnp.where(got[4:5] > 0, got[0:1] * 64 + got[1:2], -1)
-    request_ref[...] = row_request
+    request_ref[...] = row_request.reshape(request_ref.shape)
     slot_ref[...] = jnp.concatenate(slots, axis=0)
     slot_t_ref[...] = jnp.concatenate([columns[:events, 0:1], columns[events:, 0:1]], axis=1)
 
@@ -175,7 +175,7 @@
         out_shape=[
             jax.ShapeDtypeStruct((2, events), jnp.int32),
             jax.ShapeDtypeStruct((events, 2), jnp.int32),
-            jax.ShapeDtypeStruct((1, slot_total), jnp.int32),
+            jax.ShapeDtypeStruct((slot_total,), jnp.int32),
         ],
     )(owner_pair, src_row.reshape(1, events), dst_row.reshape(1, events), event_time.reshape(1, events))
 

time: 120 us -> 119 us (level)
  other arithmetic: 5.49 us -> 4.28 us
    pallas_call x1 -> x0, other arithmetic: 1.29 us -> none  [build_requests(): pl.pallas_call(prologue_kernel, out_shape=[jax.ShapeDtypeStruct((2, event...]
    all_to_all x1 -> x2, local copies, waits for them, and re-layouts: 0.71 us -> 1.92 us  [local(): lax.all_to_all(request, ('ev', 'node'), split_axis=0, concat_axis=0, tile...]
  transfers between devices with their start and end apart: 3 -> 3, of which waited for: 3 -> 3; matrix products, arithmetic and copies ran while one was open for 6% -> 7% of each run, Pallas kernels for 0% -> 0%
where the time goes in v16:
time: 119 us; the launch traced here: 118 us
  waiting for transfers between devices  46.3 us (39%)
  Pallas kernels  27.7 us (23%)
  starting transfers between devices  19.7 us (17%)
  matrix products  13.8 us (12%)
  local copies, waits for them, and re-layouts  6.26 us (5%)
  other arithmetic  4.28 us (4%)
    all_to_all x1, waiting for transfers between devices, local(): lax.all_to_all(served, ('ev', 'node'), split_axis=0, concat_axis=0, tiled...  22 us
    all_to_all x1, waiting for transfers between devices, local(): lax.all_to_all(outgoing, ('ev', 'node'), split_axis=0, concat_axis=0, til...  16.9 us
    pallas_call x1, Pallas kernels, owner_update(): pl.pallas_call(update_kernel, grid=(rows_count // block,), in_specs=[pl.B...  16.1 us
    dot_general x1, matrix products, owner_lookup(): jnp.dot(select, table, preferred_element_type=jnp.float32)  11.6 us
    all_to_all x1, starting transfers between devices, local(): lax.all_to_all(request, ('ev', 'node'), split_axis=0, concat_axis=0, tile...  11.5 us
    pallas_call x1, Pallas kernels, event_messages(): pl.pallas_call(message_kernel, out_shape=jax.ShapeDtypeStruct((slot_total...  8.98 us
    all_to_all x1, waiting for transfers between devices, local(): lax.all_to_all(request, ('ev', 'node'), split_axis=0, concat_axis=0, tile...  7.41 us
    all_to_all x1, starting transfers between devices, local(): lax.all_to_all(served, ('ev', 'node'), split_axis=0, concat_axis=0, tiled...  4.31 us
  transfers between devices with their start and end apart: 3, of which 3 were waited for; matrix products, arithmetic and copies ran while one was open for 7% of the time, Pallas kernels for 0%

profile of v16, /device:TPU:1, one launch (start us, length us, event | category | flops | bytes accessed | tf_op | source)
XLA Modules:
  0.0 118.2 jit_solution(17470300936672480263)
XLA Ops:
  0.0 0.0 copy-start
  0.0 1.3 %add_bitcast_fusion.owner_ref = s32[2,512]{1,0:T(2,128)} fusion(s32[512,1]{0,1:T(1,128)} %param.18, s32[512,1]{0,1:T(1,128)} %param.16), kind=kLoop, calls=%fused_computation.18 | loop fusion | flops 1024 | bytes 8192 | tf_op jit(solution)/shard_map/transpose | solution.py:172
  1.3 2.7 %shard_map.154 = (s32[2,512]{1,0:T(2,128)}, s32[512,2]{1,0:T(8,128)}, s32[2048]{0:T(1024)}) custom-call(s32[2,512]{1,0:T(2,128)} %add_bitcast_fusion.owner_ref, s32[1,512]{1,0:T(1,128)} %bitcast.22, s32[1,512]{1,0:T(1,128)} %bitcast.23, s32[1,512]{1,0:T(1,128)} %bitcast.20), custom_call_target="tpu_custom_call" | custom-call | tf_op jit(solution)/shard_map/pallas_call | solution.py:173
  4.0 1.4 %all_to_all.20 = s32[128,16,1]{1,0,2:T(8,128)} reshape(s32[2048]{0:T(1024)} %get-tuple-element.8) | data formatting | bytes 16384 | tf_op jit(solution)/shard_map/all_to_all | solution.py:241
  5.4 11.5 %all-to-all-start = ((s32[128,16,1]{1,2,0:T(1,128)}), s32[128,16,1]{1,2,0:T(1,128)S(1)}, u32[]{:S(2)}, u32[]{:S(2)}) async-start(s32[128,16,1]{1,2,0:T(1,128)} %bitcast.4), calls=%async_computation | async-start | bytes 131072 | tf_op jit(solution)/shard_map/all_to_all | solution.py:241
  16.9 0.7 add_select_fusion.1
  17.7 1.4 %select_convert_fusion = bf16[4096,128]{1,0:T(8,128)(2,1)S(1)} fusion(s32[4096]{0:T(1024)S(1)} %get-tuple-element.12, s32[4096]{0:T(1024)S(1)} %get-tuple-element.11, pred[128]{0:T(512)(128)(4,1)S(1)} %get-tuple-element.13, pred[128]{0:T(512)(128)(4,1)S(1)} %get-tuple-element.14), kind=kLoop, calls=%fused_computation.7 | loop fusion | flops 1572864 | bytes 1081600 | tf_op jit(solution)/shard_map/convert_element_type | solution.py:203
  19.1 7.4 %all-to-all-done = s32[128,16,1]{1,2,0:T(1,128)S(1)} async-done(((s32[128,16,1]{1,2,0:T(1,128)}), s32[128,16,1]{1,2,0:T(1,128)S(1)}, u32[]{:S(2)}, u32[]{:S(2)}) %all-to-all-start) | async-done | bytes 8224 | tf_op jit(solution)/shard_map/all_to_all | solution.py:241
  26.5 0.1 eq.39
  26.6 11.6 %fusion.5 = bf16[2048,384]{1,0:T(8,128)(2,1)} fusion(bf16[4096,128]{1,0:T(8,128)(2,1)S(1)} %select_convert_fusion, bf16[4096,256]{1,0:T(8,128)(2,1)} %mem_ref.1, s32[2048]{0:T(1024)S(1)} %eq.39), kind=kOutput, calls=%fused_computation.6 | convolution fusion | flops 6457917440 | bytes 4726784 | tf_op jit(solution)/shard_map/dot_general | solution.py:205
  38.1 0.0 copy-start.3
  38.1 0.0 copy-start.5
  38.1 4.3 %all-to-all-start.1 = ((bf16[128,16,384]{2,1,0:T(8,128)(2,1)}), bf16[128,16,384]{2,1,0:T(8,128)(2,1)S(1)}, u32[]{:S(2)}, u32[]{:S(2)}) async-start(bf16[128,16,384]{2,1,0:T(8,128)(2,1)} %bitcast.5), calls=%async_computation.1 | async-start | bytes 3145728 | tf_op jit(solution)/shard_map/all_to_all | solution.py:243
  42.4 0.0 copy-done.3
  42.5 0.9 copy.19.time_ref
  43.3 0.0 copy-done
  43.3 0.0 copy-done.5
  43.3 2.2 %convolution_add_fusion.edge_ref = f32[512,512]{1,0:T(8,128)} fusion(bf16[512,256]{1,0:T(8,128)(2,1)S(1)} %copy-done, f32[512]{0:T(512)S(1)} %copy-done.5, bf16[896,512]{1,0:T(8,128)(2,1)} %w_in_ref.1), kind=kOutput, calls=%fused_computation.8 | convolution fusion | flops 134479872 | bytes 1574912 | tf_op jit(solution)/shard_map/dot_general | solution.py:238
  45.6 22.0 %all-to-all-done.1 = bf16[128,16,384]{2,1,0:T(8,128)(2,1)S(1)} async-done(((bf16[128,16,384]{2,1,0:T(8,128)(2,1)}), bf16[128,16,384]{2,1,0:T(8,128)(2,1)S(1)}, u32[]{:S(2)}, u32[]{:S(2)}) %all-to-all-start.1) | async-done | bytes 1572896 | tf_op jit(solution)/shard_map/all_to_all | solution.py:243
  67.5 0.0 copy-start.1
  67.5 1.1 copy-done.1
  68.7 9.0 %shard_map.155 = bf16[2048,256]{1,0:T(8,128)(2,1)} custom-call(s32[512,2]{1,0:T(8,128)} %get-tuple-element.9.col_ref, s32[2,512]{1,0:T(2,128)} %get-tuple-element.10.row_ref, bf16[2048,384]{1,0:T(8,128)(2,1)} %bitcast.16, f32[512,512]{1,0:T(8,128)} %convolution_add_fusion.edge_ref, s32[512,1]{1,0:T(8,128)} %copy.19.time_ref, f32[1,128]{1,0:T(1,128)} %bitcast.24, ...), custom_call_target="tpu_custom_call" | custom-call | tf_op jit(solution)/shard_map/pallas_call | solution.py:115
  77.7 0.0 copy-start.4
  77.7 3.9 %all-to-all-start.2 = ((bf16[128,16,256]{2,1,0:T(8,128)(2,1)}), bf16[128,16,256]{2,1,0:T(8,128)(2,1)S(1)}, u32[]{:S(2)}, u32[]{:S(2)}) async-start(bf16[128,16,256]{2,1,0:T(8,128)(2,1)} %bitcast.17), calls=%async_computation.2 | async-start | bytes 2097152 | tf_op jit(solution)/shard_map/all_to_all | solution.py:247
  81.6 0.0 copy-done.4
  81.6 0.6 reshape.77.bin_ref
  82.2 0.5 broadcast.47
  82.7 0.8 reduce.5
  83.5 0.7 reshape.73.rows_ref
  84.2 16.9 %all-to-all-done.2 = bf16[128,16,256]{2,1,0:T(8,128)(2,1)S(1)} async-done(((bf16[128,16,256]{2,1,0:T(8,128)(2,1)}), bf16[128,16,256]{2,1,0:T(8,128)(2,1)S(1)}, u32[]{:S(2)}, u32[]{:S(2)}) %all-to-all-start.2) | async-done | bytes 1048608 | tf_op jit(solution)/shard_map/all_to_all | solution.py:247
  101.2 1.0 copy-done.2
  102.1 16.1 %shard_map.156 = bf16[4096,256]{1,0:T(8,128)(2,1)} custom-call(s32[1,2048]{1,0:T(1,128)} %reshape.73.rows_ref, bf16[2048,256]{1,0:T(8,128)(2,1)} %bitcast.18, bf16[4096,256]{1,0:T(8,128)(2,1)} %mem_ref.1, bf16[256,768]{1,0:T(8,128)(2,1)} %win_ref.1, f32[1,768]{1,0:T(1,128)} %reshape.77.bin_ref, bf16[256,768]{1,0:T(8,128)(2,1)} %whid_ref.1), custom_call_target="tpu_custom_call" | custom-call | tf_op jit(solution)/shard_map/pallas_call | solution.py:52
  (2 shorter events, 0.0 us)
Async XLA Ops:
  0.0 43.3 %copy-start = (bf16[512,256]{1,0:T(8,128)(2,1)S(1)}, bf16[512,256]{1,0:T(8,128)(2,1)}, u32[]{:S(2)}) copy-start(bf16[512,256]{1,0:T(8,128)(2,1)} %param.21) | copy-start | bytes 786436
  5.4 21.1 %all-to-all-start = ((s32[128,16,1]{1,2,0:T(1,128)}), s32[128,16,1]{1,2,0:T(1,128)S(1)}, u32[]{:S(2)}, u32[]{:S(2)}) async-start(s32[128,16,1]{1,2,0:T(1,128)} %bitcast.4), calls=%async_computation | async-start | bytes 131072 | tf_op jit(solution)/shard_map/all_to_all | solution.py:241
  38.1 4.3 %copy-start.3 = (s32[512]{0:T(512)S(1)}, s32[512]{0:T(512)}, u32[]{:S(2)}) copy-start(s32[512]{0:T(512)} %param.20) | copy-start | bytes 6148
  38.1 5.2 %copy-start.5 = (f32[512]{0:T(512)S(1)}, f32[512]{0:T(512)}, u32[]{:S(2)}) copy-start(f32[512]{0:T(512)} %param.27) | copy-start | bytes 6148
  38.1 29.4 %all-to-all-start.1 = ((bf16[128,16,384]{2,1,0:T(8,128)(2,1)}), bf16[128,16,384]{2,1,0:T(8,128)(2,1)S(1)}, u32[]{:S(2)}, u32[]{:S(2)}) async-start(bf16[128,16,384]{2,1,0:T(8,128)(2,1)} %bitcast.5), calls=%async_computation.1 | async-start | bytes 3145728 | tf_op jit(solution)/shard_map/all_to_all | solution.py:243
  67.5 1.1 copy-start.1
  77.7 4.0 %copy-start.4 = (f32[768]{0:T(1024)S(1)}, f32[768]{0:T(1024)}, u32[]{:S(2)}) copy-start(f32[768]{0:T(1024)} %param.30) | copy-start | bytes 9220
  77.7 23.5 %all-to-all-start.2 = ((bf16[128,16,256]{2,1,0:T(8,128)(2,1)}), bf16[128,16,256]{2,1,0:T(8,128)(2,1)S(1)}, u32[]{:S(2)}, u32[]{:S(2)}) async-start(bf16[128,16,256]{2,1,0:T(8,128)(2,1)} %bitcast.17), calls=%async_computation.2 | async-start | bytes 2097152 | tf_op jit(solution)/shard_map/all_to_all | solution.py:247
  101.2 1.0 copy-start.2

commit v17 on v16

--- a/solution.py
+++ b/solution.py
@@ -128,8 +128,10 @@
     )
 
 
-def prologue_kernel(owner_ref, src_row_ref, dst_row_ref, time_ref, slot_ref, slot_t_ref, request_ref):
-    events = owner_ref.shape[1]
+def prologue_kernel(
+    src_owner_ref, dst_owner_ref, src_row_ref, dst_row_ref, time_ref, slot_ref, slot_t_ref, request_ref
+):
+    events = src_owner_ref.shape[1]
     owners = 128
     capacity = 8
     slot_total = request_ref.shape[-1]
@@ -141,7 +143,7 @@
     owner_ids = lax.broadcasted_iota(jnp.int32, (owners, events), 0)
     slots = []
     for side in range(2):
-        owner_row = owner_ref[side : side + 1, :]
+        owner_row = (src_owner_ref, dst_owner_ref)[side][...]
         onehot = owner_ids == owner_row
         earlier = jnp.dot(onehot.astype(jnp.bfloat16), upper, preferred_element_type=jnp.float32)
         position = jnp.sum(jnp.where(onehot, earlier, 0.0), axis=0, keepdims=True)
@@ -169,7 +171,6 @@
 
 def build_requests(src_owner, src_row, dst_owner, dst_row, event_time, slot_total):
     events = src_row.shape[0]
-    owner_pair = jnp.concatenate([src_owner, dst_owner], axis=1).T
     return pl.pallas_call(
         prologue_kernel,
         out_shape=[
@@ -177,7 +178,10 @@
             jax.ShapeDtypeStruct((events, 2), jnp.int32),
             jax.ShapeDtypeStruct((slot_total,), jnp.int32),
         ],
-    )(owner_pair, src_row.reshape(1, events), dst_row.reshape(1, events), event_time.reshape(1, events))
+    )(
+        src_owner.reshape(1, events),
+        dst_owner.reshape(1, events),
+        src_row.reshape(1, events), dst_row.reshape(1, events), event_time.reshape(1, events))
 
 
 def slot_of(owner_ids, owner_count, capacity):

time: 119 us -> 117 us (0.983)
  other arithmetic: 4.28 us -> 2.94 us
    transpose x1 -> x0, other arithmetic: 1.34 us -> none  [build_requests(): owner_pair = jnp.concatenate([src_owner, dst_owner], axis=1).T]
where the time goes in v17:
time: 117 us
  waiting for transfers between devices  46.3 us (40%)
  Pallas kernels  27.8 us (24%)
  starting transfers between devices  19.8 us (17%)
  matrix products  13.8 us (12%)
  local copies, waits for them, and re-layouts  6.26 us (5%)
  other arithmetic  2.94 us (3%)
    all_to_all x1, waiting for transfers between devices, local(): lax.all_to_all(served, ('ev', 'node'), split_axis=0, concat_axis=0, tiled...  22 us
    all_to_all x1, waiting for transfers between devices, local(): lax.all_to_all(outgoing, ('ev', 'node'), split_axis=0, concat_axis=0, til...  16.9 us
    pallas_call x1, Pallas kernels, owner_update(): pl.pallas_call(update_kernel, grid=(rows_count // block,), in_specs=[pl.B...  16.1 us
    dot_general x1, matrix products, owner_lookup(): jnp.dot(select, table, preferred_element_type=jnp.float32)  11.6 us
    all_to_all x1, starting transfers between devices, local(): lax.all_to_all(request, ('ev', 'node'), split_axis=0, concat_axis=0, tile...  11.5 us
    pallas_call x1, Pallas kernels, event_messages(): pl.pallas_call(message_kernel, out_shape=jax.ShapeDtypeStruct((slot_total...  8.98 us
    all_to_all x1, waiting for transfers between devices, local(): lax.all_to_all(request, ('ev', 'node'), split_axis=0, concat_axis=0, tile...  7.41 us
    all_to_all x1, starting transfers between devices, local(): lax.all_to_all(served, ('ev', 'node'), split_axis=0, concat_axis=0, tiled...  4.31 us
  transfers between devices with their start and end apart: 3, of which 3 were waited for; matrix products, arithmetic and copies ran while one was open for 7% of the time, Pallas kernels for 0%

profile of v17, /device:TPU:1, one launch (start us, length us, event | category | flops | bytes accessed | tf_op | source)
XLA Modules:
  0.0 116.9 jit_solution(7021294210895806550)
XLA Ops:
  0.0 0.0 copy-start
  0.0 2.7 %shard_map.154 = (s32[2,512]{1,0:T(2,128)}, s32[512,2]{1,0:T(8,128)}, s32[2048]{0:T(1024)}) custom-call(s32[1,512]{1,0:T(1,128)} %bitcast.22, s32[1,512]{1,0:T(1,128)} %bitcast.23, s32[1,512]{1,0:T(1,128)} %bitcast.24, s32[1,512]{1,0:T(1,128)} %bitcast.25, s32[1,512]{1,0:T(1,128)} %bitcast.20), custom_call_target="tpu_custom_call" | custom-call | tf_op jit(solution)/shard_map/pallas_call | solution.py:174
  2.7 1.4 %all_to_all.20 = s32[128,16,1]{1,0,2:T(8,128)} reshape(s32[2048]{0:T(1024)} %get-tuple-element.8) | data formatting | bytes 16384 | tf_op jit(solution)/shard_map/all_to_all | solution.py:245
  4.1 11.5 %all-to-all-start = ((s32[128,16,1]{1,2,0:T(1,128)}), s32[128,16,1]{1,2,0:T(1,128)S(1)}, u32[]{:S(2)}, u32[]{:S(2)}) async-start(s32[128,16,1]{1,2,0:T(1,128)} %bitcast.5), calls=%async_computation | async-start | bytes 131072 | tf_op jit(solution)/shard_map/all_to_all | solution.py:245
  15.7 0.7 add_select_fusion.1
  16.4 1.4 %select_convert_fusion = bf16[4096,128]{1,0:T(8,128)(2,1)S(1)} fusion(s32[4096]{0:T(1024)S(1)} %get-tuple-element.12, s32[4096]{0:T(1024)S(1)} %get-tuple-element.11, pred[128]{0:T(512)(128)(4,1)S(1)} %get-tuple-element.13, pred[128]{0:T(512)(128)(4,1)S(1)} %get-tuple-element.14), kind=kLoop, calls=%fused_computation.7 | loop fusion | flops 1572864 | bytes 1081600 | tf_op jit(solution)/shard_map/convert_element_type | solution.py:207
  17.8 7.4 %all-to-all-done = s32[128,16,1]{1,2,0:T(1,128)S(1)} async-done(((s32[128,16,1]{1,2,0:T(1,128)}), s32[128,16,1]{1,2,0:T(1,128)S(1)}, u32[]{:S(2)}, u32[]{:S(2)}) %all-to-all-start) | async-done | bytes 8224 | tf_op jit(solution)/shard_map/all_to_all | solution.py:245
  25.2 0.1 eq.39
  25.3 11.6 %fusion.5 = bf16[2048,384]{1,0:T(8,128)(2,1)} fusion(bf16[4096,128]{1,0:T(8,128)(2,1)S(1)} %select_convert_fusion, bf16[4096,256]{1,0:T(8,128)(2,1)} %mem_ref.1, s32[2048]{0:T(1024)S(1)} %eq.39), kind=kOutput, calls=%fused_computation.6 | convolution fusion | flops 6457917440 | bytes 4726784 | tf_op jit(solution)/shard_map/dot_general | solution.py:209
  36.8 0.0 copy-start.3
  36.8 0.0 copy-start.5
  36.8 4.3 %all-to-all-start.1 = ((bf16[128,16,384]{2,1,0:T(8,128)(2,1)}), bf16[128,16,384]{2,1,0:T(8,128)(2,1)S(1)}, u32[]{:S(2)}, u32[]{:S(2)}) async-start(bf16[128,16,384]{2,1,0:T(8,128)(2,1)} %bitcast.6), calls=%async_computation.1 | async-start | bytes 3145728 | tf_op jit(solution)/shard_map/all_to_all | solution.py:247
  41.2 0.0 copy-done.3
  41.2 0.9 copy.19.time_ref
  42.0 0.0 copy-done
  42.0 0.0 copy-done.5
  42.0 2.2 %convolution_add_fusion.edge_ref = f32[512,512]{1,0:T(8,128)} fusion(bf16[512,256]{1,0:T(8,128)(2,1)S(1)} %copy-done, f32[512]{0:T(512)S(1)} %copy-done.5, bf16[896,512]{1,0:T(8,128)(2,1)} %w_in_ref.1), kind=kOutput, calls=%fused_computation.8 | convolution fusion | flops 134479872 | bytes 1574912 | tf_op jit(solution)/shard_map/dot_general | solution.py:242
  44.3 22.0 %all-to-all-done.1 = bf16[128,16,384]{2,1,0:T(8,128)(2,1)S(1)} async-done(((bf16[128,16,384]{2,1,0:T(8,128)(2,1)}), bf16[128,16,384]{2,1,0:T(8,128)(2,1)S(1)}, u32[]{:S(2)}, u32[]{:S(2)}) %all-to-all-start.1) | async-done | bytes 1572896 | tf_op jit(solution)/shard_map/all_to_all | solution.py:247
  66.2 0.0 copy-start.1
  66.2 1.1 copy-done.1
  67.4 9.0 %shard_map.155 = bf16[2048,256]{1,0:T(8,128)(2,1)} custom-call(s32[512,2]{1,0:T(8,128)} %get-tuple-element.9.col_ref, s32[2,512]{1,0:T(2,128)} %get-tuple-element.10.row_ref, bf16[2048,384]{1,0:T(8,128)(2,1)} %bitcast.16, f32[512,512]{1,0:T(8,128)} %convolution_add_fusion.edge_ref, s32[512,1]{1,0:T(8,128)} %copy.19.time_ref, f32[1,128]{1,0:T(1,128)} %bitcast.26, ...), custom_call_target="tpu_custom_call" | custom-call | tf_op jit(solution)/shard_map/pallas_call | solution.py:115
  76.4 0.0 copy-start.4
  76.4 3.9 %all-to-all-start.2 = ((bf16[128,16,256]{2,1,0:T(8,128)(2,1)}), bf16[128,16,256]{2,1,0:T(8,128)(2,1)S(1)}, u32[]{:S(2)}, u32[]{:S(2)}) async-start(bf16[128,16,256]{2,1,0:T(8,128)(2,1)} %bitcast.17), calls=%async_computation.2 | async-start | bytes 2097152 | tf_op jit(solution)/shard_map/all_to_all | solution.py:251
  80.3 0.0 copy-done.4
  80.3 0.6 reshape.85.bin_ref
  80.9 0.5 broadcast.47
  81.4 0.8 reduce.5
  82.3 0.7 reshape.81.rows_ref
  82.9 16.9 %all-to-all-done.2 = bf16[128,16,256]{2,1,0:T(8,128)(2,1)S(1)} async-done(((bf16[128,16,256]{2,1,0:T(8,128)(2,1)}), bf16[128,16,256]{2,1,0:T(8,128)(2,1)S(1)}, u32[]{:S(2)}, u32[]{:S(2)}) %all-to-all-start.2) | async-done | bytes 1048608 | tf_op jit(solution)/shard_map/all_to_all | solution.py:251
  99.9 0.0 copy-start.2
  99.9 1.0 copy-done.2
  100.9 16.1 %shard_map.156 = bf16[4096,256]{1,0:T(8,128)(2,1)} custom-call(s32[1,2048]{1,0:T(1,128)} %reshape.81.rows_ref, bf16[2048,256]{1,0:T(8,128)(2,1)} %bitcast.18, bf16[4096,256]{1,0:T(8,128)(2,1)} %mem_ref.1, bf16[256,768]{1,0:T(8,128)(2,1)} %win_ref.1, f32[1,768]{1,0:T(1,128)} %reshape.85.bin_ref, bf16[256,768]{1,0:T(8,128)(2,1)} %whid_ref.1), custom_call_target="tpu_custom_call" | custom-call | tf_op jit(solution)/shard_map/pallas_call | solution.py:52
  (1 shorter events, 0.0 us)
Async XLA Ops:
  0.0 42.0 %copy-start = (bf16[512,256]{1,0:T(8,128)(2,1)S(1)}, bf16[512,256]{1,0:T(8,128)(2,1)}, u32[]{:S(2)}) copy-start(bf16[512,256]{1,0:T(8,128)(2,1)} %param.21) | copy-start | bytes 786436
  4.1 21.1 %all-to-all-start = ((s32[128,16,1]{1,2,0:T(1,128)}), s32[128,16,1]{1,2,0:T(1,128)S(1)}, u32[]{:S(2)}, u32[]{:S(2)}) async-start(s32[128,16,1]{1,2,0:T(1,128)} %bitcast.5), calls=%async_computation | async-start | bytes 131072 | tf_op jit(solution)/shard_map/all_to_all | solution.py:245
  36.8 4.3 %copy-start.3 = (s32[512]{0:T(512)S(1)}, s32[512]{0:T(512)}, u32[]{:S(2)}) copy-start(s32[512]{0:T(512)} %param.20) | copy-start | bytes 6148
  36.8 5.2 %copy-start.5 = (f32[512]{0:T(512)S(1)}, f32[512]{0:T(512)}, u32[]{:S(2)}) copy-start(f32[512]{0:T(512)} %param.27) | copy-start | bytes 6148
  36.8 29.4 %all-to-all-start.1 = ((bf16[128,16,384]{2,1,0:T(8,128)(2,1)}), bf16[128,16,384]{2,1,0:T(8,128)(2,1)S(1)}, u32[]{:S(2)}, u32[]{:S(2)}) async-start(bf16[128,16,384]{2,1,0:T(8,128)(2,1)} %bitcast.6), calls=%async_computation.1 | async-start | bytes 3145728 | tf_op jit(solution)/shard_map/all_to_all | solution.py:247
  66.2 1.1 copy-start.1
  76.4 4.0 %copy-start.4 = (f32[768]{0:T(1024)S(1)}, f32[768]{0:T(1024)}, u32[]{:S(2)}) copy-start(f32[768]{0:T(1024)} %param.30) | copy-start | bytes 9220
  76.4 23.5 %all-to-all-start.2 = ((bf16[128,16,256]{2,1,0:T(8,128)(2,1)}), bf16[128,16,256]{2,1,0:T(8,128)(2,1)S(1)}, u32[]{:S(2)}, u32[]{:S(2)}) async-start(bf16[128,16,256]{2,1,0:T(8,128)(2,1)} %bitcast.17), calls=%async_computation.2 | async-start | bytes 2097152 | tf_op jit(solution)/shard_map/all_to_all | solution.py:251
  99.9 1.0 copy-start.2

commit v18 on v17

--- a/solution.py
+++ b/solution.py
@@ -100,10 +100,11 @@
         return jnp.dot(hidden, w_out_ref[...], preferred_element_type=jnp.float32).astype(jnp.bfloat16)
 
     sent = (message(mem_src, mem_dst, enc_src), message(mem_dst, mem_src, enc_dst))
-    sub_ids = lax.broadcasted_iota(jnp.int32, (slot_total, events), 0)
-    placed = [(sub_ids == row_ref[side : side + 1, :]).astype(jnp.bfloat16) for side in range(2)]
-    out = jnp.dot(placed[0], sent[0], preferred_element_type=jnp.float32)
-    out = out + jnp.dot(placed[1], sent[1], preferred_element_type=jnp.float32)
+    sub_ids = lax.broadcasted_iota(jnp.int32, (slot_total, 2 * events), 0)
+    slot_row = jnp.concatenate([row_ref[0:1, :], row_ref[1:2, :]], axis=1)
+    placed = (sub_ids == slot_row).astype(jnp.bfloat16)
+    both = jnp.concatenate(sent, axis=0)
+    out = jnp.dot(placed, both, preferred_element_type=jnp.float32)
     out_ref[...] = out.astype(out_ref.dtype)
 
 

time: 117 us -> 117 us (level)
  no operation moved by 1% of the time
where the time goes in v18:
time: 117 us
  waiting for transfers between devices  46.3 us (40%)
  Pallas kernels  27.6 us (24%)
  starting transfers between devices  19.8 us (17%)
  matrix products  13.8 us (12%)
  local copies, waits for them, and re-layouts  6.26 us (5%)
  other arithmetic  2.94 us (3%)
    all_to_all x1, waiting for transfers between devices, local(): lax.all_to_all(served, ('ev', 'node'), split_axis=0, concat_axis=0, tiled...  22 us
    all_to_all x1, waiting for transfers between devices, local(): lax.all_to_all(outgoing, ('ev', 'node'), split_axis=0, concat_axis=0, til...  16.9 us
    pallas_call x1, Pallas kernels, owner_update(): pl.pallas_call(update_kernel, grid=(rows_count // block,), in_specs=[pl.B...  16.1 us
    dot_general x1, matrix products, owner_lookup(): jnp.dot(select, table, preferred_element_type=jnp.float32)  11.6 us
    all_to_all x1, starting transfers between devices, local(): lax.all_to_all(request, ('ev', 'node'), split_axis=0, concat_axis=0, tile...  11.5 us
    pallas_call x1, Pallas kernels, event_messages(): pl.pallas_call(message_kernel, out_shape=jax.ShapeDtypeStruct((slot_total...  8.81 us
    all_to_all x1, waiting for transfers between devices, local(): lax.all_to_all(request, ('ev', 'node'), split_axis=0, concat_axis=0, tile...  7.41 us
    all_to_all x1, starting transfers between devices, local(): lax.all_to_all(served, ('ev', 'node'), split_axis=0, concat_axis=0, tiled...  4.31 us
  transfers between devices with their start and end apart: 3, of which 3 were waited for; matrix products, arithmetic and copies ran while one was open for 7% of the time, Pallas kernels for 0%

profile of v18, /device:TPU:1, one launch (start us, length us, event | category | flops | bytes accessed | tf_op | source)
XLA Modules:
  0.0 116.8 jit_solution(14575715227939102297)
XLA Ops:
  0.0 0.0 copy-start
  0.0 2.7 %shard_map.154 = (s32[2,512]{1,0:T(2,128)}, s32[512,2]{1,0:T(8,128)}, s32[2048]{0:T(1024)}) custom-call(s32[1,512]{1,0:T(1,128)} %bitcast.22, s32[1,512]{1,0:T(1,128)} %bitcast.23, s32[1,512]{1,0:T(1,128)} %bitcast.24, s32[1,512]{1,0:T(1,128)} %bitcast.25, s32[1,512]{1,0:T(1,128)} %bitcast.20), custom_call_target="tpu_custom_call" | custom-call | tf_op jit(solution)/shard_map/pallas_call | solution.py:175
  2.7 1.4 %all_to_all.20 = s32[128,16,1]{1,0,2:T(8,128)} reshape(s32[2048]{0:T(1024)} %get-tuple-element.8) | data formatting | bytes 16384 | tf_op jit(solution)/shard_map/all_to_all | solution.py:246
  4.1 11.5 %all-to-all-start = ((s32[128,16,1]{1,2,0:T(1,128)}), s32[128,16,1]{1,2,0:T(1,128)S(1)}, u32[]{:S(2)}, u32[]{:S(2)}) async-start(s32[128,16,1]{1,2,0:T(1,128)} %bitcast.5), calls=%async_computation | async-start | bytes 131072 | tf_op jit(solution)/shard_map/all_to_all | solution.py:246
  15.7 0.7 add_select_fusion.1
  16.4 1.4 %select_convert_fusion = bf16[4096,128]{1,0:T(8,128)(2,1)S(1)} fusion(s32[4096]{0:T(1024)S(1)} %get-tuple-element.12, s32[4096]{0:T(1024)S(1)} %get-tuple-element.11, pred[128]{0:T(512)(128)(4,1)S(1)} %get-tuple-element.13, pred[128]{0:T(512)(128)(4,1)S(1)} %get-tuple-element.14), kind=kLoop, calls=%fused_computation.7 | loop fusion | flops 1572864 | bytes 1081600 | tf_op jit(solution)/shard_map/convert_element_type | solution.py:208
  17.8 7.4 %all-to-all-done = s32[128,16,1]{1,2,0:T(1,128)S(1)} async-done(((s32[128,16,1]{1,2,0:T(1,128)}), s32[128,16,1]{1,2,0:T(1,128)S(1)}, u32[]{:S(2)}, u32[]{:S(2)}) %all-to-all-start) | async-done | bytes 8224 | tf_op jit(solution)/shard_map/all_to_all | solution.py:246
  25.2 0.1 eq.39
  25.3 11.6 %fusion.5 = bf16[2048,384]{1,0:T(8,128)(2,1)} fusion(bf16[4096,128]{1,0:T(8,128)(2,1)S(1)} %select_convert_fusion, bf16[4096,256]{1,0:T(8,128)(2,1)} %mem_ref.1, s32[2048]{0:T(1024)S(1)} %eq.39), kind=kOutput, calls=%fused_computation.6 | convolution fusion | flops 6457917440 | bytes 4726784 | tf_op jit(solution)/shard_map/dot_general | solution.py:210
  36.8 0.0 copy-start.3
  36.8 0.0 copy-start.5
  36.8 4.3 %all-to-all-start.1 = ((bf16[128,16,384]{2,1,0:T(8,128)(2,1)}), bf16[128,16,384]{2,1,0:T(8,128)(2,1)S(1)}, u32[]{:S(2)}, u32[]{:S(2)}) async-start(bf16[128,16,384]{2,1,0:T(8,128)(2,1)} %bitcast.6), calls=%async_computation.1 | async-start | bytes 3145728 | tf_op jit(solution)/shard_map/all_to_all | solution.py:248
  41.2 0.0 copy-done.3
  41.2 0.9 copy.19.time_ref
  42.0 0.0 copy-done
  42.0 0.0 copy-done.5
  42.0 2.2 %convolution_add_fusion.edge_ref = f32[512,512]{1,0:T(8,128)} fusion(bf16[512,256]{1,0:T(8,128)(2,1)S(1)} %copy-done, f32[512]{0:T(512)S(1)} %copy-done.5, bf16[896,512]{1,0:T(8,128)(2,1)} %w_in_ref.1), kind=kOutput, calls=%fused_computation.8 | convolution fusion | flops 134479872 | bytes 1574912 | tf_op jit(solution)/shard_map/dot_general | solution.py:243
  44.3 22.0 %all-to-all-done.1 = bf16[128,16,384]{2,1,0:T(8,128)(2,1)S(1)} async-done(((bf16[128,16,384]{2,1,0:T(8,128)(2,1)}), bf16[128,16,384]{2,1,0:T(8,128)(2,1)S(1)}, u32[]{:S(2)}, u32[]{:S(2)}) %all-to-all-start.1) | async-done | bytes 1572896 | tf_op jit(solution)/shard_map/all_to_all | solution.py:248
  66.2 0.0 copy-start.1
  66.2 1.1 copy-done.1
  67.4 8.8 %shard_map.155 = bf16[2048,256]{1,0:T(8,128)(2,1)} custom-call(s32[512,2]{1,0:T(8,128)} %get-tuple-element.9.col_ref, s32[2,512]{1,0:T(2,128)} %get-tuple-element.10.row_ref, bf16[2048,384]{1,0:T(8,128)(2,1)} %bitcast.16, f32[512,512]{1,0:T(8,128)} %convolution_add_fusion.edge_ref, s32[512,1]{1,0:T(8,128)} %copy.19.time_ref, f32[1,128]{1,0:T(1,128)} %bitcast.26, ...), custom_call_target="tpu_custom_call" | custom-call | tf_op jit(solution)/shard_map/pallas_call | solution.py:116
  76.2 0.0 copy-start.4
  76.2 3.9 %all-to-all-start.2 = ((bf16[128,16,256]{2,1,0:T(8,128)(2,1)}), bf16[128,16,256]{2,1,0:T(8,128)(2,1)S(1)}, u32[]{:S(2)}, u32[]{:S(2)}) async-start(bf16[128,16,256]{2,1,0:T(8,128)(2,1)} %bitcast.17), calls=%async_computation.2 | async-start | bytes 2097152 | tf_op jit(solution)/shard_map/all_to_all | solution.py:252
  80.2 0.0 copy-done.4
  80.2 0.6 reshape.85.bin_ref
  80.8 0.5 broadcast.47
  81.3 0.8 reduce.5
  82.1 0.7 reshape.81.rows_ref
  82.8 16.9 %all-to-all-done.2 = bf16[128,16,256]{2,1,0:T(8,128)(2,1)S(1)} async-done(((bf16[128,16,256]{2,1,0:T(8,128)(2,1)}), bf16[128,16,256]{2,1,0:T(8,128)(2,1)S(1)}, u32[]{:S(2)}, u32[]{:S(2)}) %all-to-all-start.2) | async-done | bytes 1048608 | tf_op jit(solution)/shard_map/all_to_all | solution.py:252
  99.7 0.0 copy-start.2
  99.7 1.0 copy-done.2
  100.7 16.1 %shard_map.156 = bf16[4096,256]{1,0:T(8,128)(2,1)} custom-call(s32[1,2048]{1,0:T(1,128)} %reshape.81.rows_ref, bf16[2048,256]{1,0:T(8,128)(2,1)} %bitcast.18, bf16[4096,256]{1,0:T(8,128)(2,1)} %mem_ref.1, bf16[256,768]{1,0:T(8,128)(2,1)} %win_ref.1, f32[1,768]{1,0:T(1,128)} %reshape.85.bin_ref, bf16[256,768]{1,0:T(8,128)(2,1)} %whid_ref.1), custom_call_target="tpu_custom_call" | custom-call | tf_op jit(solution)/shard_map/pallas_call | solution.py:52
  (1 shorter events, 0.0 us)
Async XLA Ops:
  0.0 42.0 %copy-start = (bf16[512,256]{1,0:T(8,128)(2,1)S(1)}, bf16[512,256]{1,0:T(8,128)(2,1)}, u32[]{:S(2)}) copy-start(bf16[512,256]{1,0:T(8,128)(2,1)} %param.21) | copy-start | bytes 786436
  4.1 21.1 %all-to-all-start = ((s32[128,16,1]{1,2,0:T(1,128)}), s32[128,16,1]{1,2,0:T(1,128)S(1)}, u32[]{:S(2)}, u32[]{:S(2)}) async-start(s32[128,16,1]{1,2,0:T(1,128)} %bitcast.5), calls=%async_computation | async-start | bytes 131072 | tf_op jit(solution)/shard_map/all_to_all | solution.py:246
  36.8 4.3 %copy-start.3 = (s32[512]{0:T(512)S(1)}, s32[512]{0:T(512)}, u32[]{:S(2)}) copy-start(s32[512]{0:T(512)} %param.20) | copy-start | bytes 6148
  36.8 5.2 %copy-start.5 = (f32[512]{0:T(512)S(1)}, f32[512]{0:T(512)}, u32[]{:S(2)}) copy-start(f32[512]{0:T(512)} %param.27) | copy-start | bytes 6148
  36.8 29.4 %all-to-all-start.1 = ((bf16[128,16,384]{2,1,0:T(8,128)(2,1)}), bf16[128,16,384]{2,1,0:T(8,128)(2,1)S(1)}, u32[]{:S(2)}, u32[]{:S(2)}) async-start(bf16[128,16,384]{2,1,0:T(8,128)(2,1)} %bitcast.6), calls=%async_computation.1 | async-start | bytes 3145728 | tf_op jit(solution)/shard_map/all_to_all | solution.py:248
  66.2 1.1 copy-start.1
  76.2 4.0 %copy-start.4 = (f32[768]{0:T(1024)S(1)}, f32[768]{0:T(1024)}, u32[]{:S(2)}) copy-start(f32[768]{0:T(1024)} %param.30) | copy-start | bytes 9220
  76.2 23.5 %all-to-all-start.2 = ((bf16[128,16,256]{2,1,0:T(8,128)(2,1)}), bf16[128,16,256]{2,1,0:T(8,128)(2,1)S(1)}, u32[]{:S(2)}, u32[]{:S(2)}) async-start(bf16[128,16,256]{2,1,0:T(8,128)(2,1)} %bitcast.17), calls=%async_computation.2 | async-start | bytes 2097152 | tf_op jit(solution)/shard_map/all_to_all | solution.py:252
  99.7 1.0 copy-start.2

commit v19 on v17

--- a/solution.py
+++ b/solution.py
@@ -28,8 +28,8 @@
     block = out_ref.shape[0]
     slots = rows_ref.shape[1]
     width = mem_ref.shape[1]
-    ids = pl.program_id(0) * block + lax.broadcasted_iota(jnp.int32, (block, slots), 0)
-    onehot = (ids == rows_ref[...]).astype(jnp.bfloat16)
+    ids = lax.broadcasted_iota(jnp.int32, (block, slots), 0)
+    onehot = (ids == rows_ref[...] - pl.program_id(0) * block).astype(jnp.bfloat16)
     total = jnp.dot(onehot, msg_ref[...], preferred_element_type=jnp.float32)
     ones = jnp.ones((slots, 128), jnp.bfloat16)
     count = jnp.dot(onehot, ones, preferred_element_type=jnp.float32)[:, :1]

time: 117 us -> 117 us (level)
  no operation moved by 1% of the time
where the time goes in v19:
time: 117 us
  waiting for transfers between devices  46.3 us (40%)
  Pallas kernels  27.8 us (24%)
  starting transfers between devices  19.8 us (17%)
  matrix products  13.8 us (12%)
  local copies, waits for them, and re-layouts  6.26 us (5%)
  other arithmetic  2.94 us (3%)
    all_to_all x1, waiting for transfers between devices, local(): lax.all_to_all(served, ('ev', 'node'), split_axis=0, concat_axis=0, tiled...  22 us
    all_to_all x1, waiting for transfers between devices, local(): lax.all_to_all(outgoing, ('ev', 'node'), split_axis=0, concat_axis=0, til...  16.9 us
    pallas_call x1, Pallas kernels, owner_update(): pl.pallas_call(update_kernel, grid=(rows_count // block,), in_specs=[pl.B...  16.1 us
    dot_general x1, matrix products, owner_lookup(): jnp.dot(select, table, preferred_element_type=jnp.float32)  11.6 us
    all_to_all x1, starting transfers between devices, local(): lax.all_to_all(request, ('ev', 'node'), split_axis=0, concat_axis=0, tile...  11.5 us
    pallas_call x1, Pallas kernels, event_messages(): pl.pallas_call(message_kernel, out_shape=jax.ShapeDtypeStruct((slot_total...  8.98 us
    all_to_all x1, waiting for transfers between devices, local(): lax.all_to_all(request, ('ev', 'node'), split_axis=0, concat_axis=0, tile...  7.41 us
    all_to_all x1, starting transfers between devices, local(): lax.all_to_all(served, ('ev', 'node'), split_axis=0, concat_axis=0, tiled...  4.31 us
  transfers between devices with their start and end apart: 3, of which 3 were waited for; matrix products, arithmetic and copies ran while one was open for 7% of the time, Pallas kernels for 0%

profile of v19, /device:TPU:1, one launch (start us, length us, event | category | flops | bytes accessed | tf_op | source)
XLA Modules:
  0.0 116.9 jit_solution(12520060862066245086)
XLA Ops:
  0.0 0.0 copy-start
  0.0 2.7 %shard_map.154 = (s32[2,512]{1,0:T(2,128)}, s32[512,2]{1,0:T(8,128)}, s32[2048]{0:T(1024)}) custom-call(s32[1,512]{1,0:T(1,128)} %bitcast.22, s32[1,512]{1,0:T(1,128)} %bitcast.23, s32[1,512]{1,0:T(1,128)} %bitcast.24, s32[1,512]{1,0:T(1,128)} %bitcast.25, s32[1,512]{1,0:T(1,128)} %bitcast.20), custom_call_target="tpu_custom_call" | custom-call | tf_op jit(solution)/shard_map/pallas_call | solution.py:174
  2.7 1.4 %all_to_all.20 = s32[128,16,1]{1,0,2:T(8,128)} reshape(s32[2048]{0:T(1024)} %get-tuple-element.8) | data formatting | bytes 16384 | tf_op jit(solution)/shard_map/all_to_all | solution.py:245
  4.1 11.5 %all-to-all-start = ((s32[128,16,1]{1,2,0:T(1,128)}), s32[128,16,1]{1,2,0:T(1,128)S(1)}, u32[]{:S(2)}, u32[]{:S(2)}) async-start(s32[128,16,1]{1,2,0:T(1,128)} %bitcast.5), calls=%async_computation | async-start | bytes 131072 | tf_op jit(solution)/shard_map/all_to_all | solution.py:245
  15.7 0.7 add_select_fusion.1
  16.4 1.4 %select_convert_fusion = bf16[4096,128]{1,0:T(8,128)(2,1)S(1)} fusion(s32[4096]{0:T(1024)S(1)} %get-tuple-element.12, s32[4096]{0:T(1024)S(1)} %get-tuple-element.11, pred[128]{0:T(512)(128)(4,1)S(1)} %get-tuple-element.13, pred[128]{0:T(512)(128)(4,1)S(1)} %get-tuple-element.14), kind=kLoop, calls=%fused_computation.7 | loop fusion | flops 1572864 | bytes 1081600 | tf_op jit(solution)/shard_map/convert_element_type | solution.py:207
  17.8 7.4 %all-to-all-done = s32[128,16,1]{1,2,0:T(1,128)S(1)} async-done(((s32[128,16,1]{1,2,0:T(1,128)}), s32[128,16,1]{1,2,0:T(1,128)S(1)}, u32[]{:S(2)}, u32[]{:S(2)}) %all-to-all-start) | async-done | bytes 8224 | tf_op jit(solution)/shard_map/all_to_all | solution.py:245
  25.2 0.1 eq.39
  25.3 11.6 %fusion.5 = bf16[2048,384]{1,0:T(8,128)(2,1)} fusion(bf16[4096,128]{1,0:T(8,128)(2,1)S(1)} %select_convert_fusion, bf16[4096,256]{1,0:T(8,128)(2,1)} %mem_ref.1, s32[2048]{0:T(1024)S(1)} %eq.39), kind=kOutput, calls=%fused_computation.6 | convolution fusion | flops 6457917440 | bytes 4726784 | tf_op jit(solution)/shard_map/dot_general | solution.py:209
  36.8 0.0 copy-start.3
  36.8 0.0 copy-start.5
  36.8 4.3 %all-to-all-start.1 = ((bf16[128,16,384]{2,1,0:T(8,128)(2,1)}), bf16[128,16,384]{2,1,0:T(8,128)(2,1)S(1)}, u32[]{:S(2)}, u32[]{:S(2)}) async-start(bf16[128,16,384]{2,1,0:T(8,128)(2,1)} %bitcast.6), calls=%async_computation.1 | async-start | bytes 3145728 | tf_op jit(solution)/shard_map/all_to_all | solution.py:247
  41.2 0.0 copy-done.3
  41.2 0.9 copy.19.time_ref
  42.0 0.0 copy-done
  42.0 0.0 copy-done.5
  42.0 2.2 %convolution_add_fusion.edge_ref = f32[512,512]{1,0:T(8,128)} fusion(bf16[512,256]{1,0:T(8,128)(2,1)S(1)} %copy-done, f32[512]{0:T(512)S(1)} %copy-done.5, bf16[896,512]{1,0:T(8,128)(2,1)} %w_in_ref.1), kind=kOutput, calls=%fused_computation.8 | convolution fusion | flops 134479872 | bytes 1574912 | tf_op jit(solution)/shard_map/dot_general | solution.py:242
  44.3 22.0 %all-to-all-done.1 = bf16[128,16,384]{2,1,0:T(8,128)(2,1)S(1)} async-done(((bf16[128,16,384]{2,1,0:T(8,128)(2,1)}), bf16[128,16,384]{2,1,0:T(8,128)(2,1)S(1)}, u32[]{:S(2)}, u32[]{:S(2)}) %all-to-all-start.1) | async-done | bytes 1572896 | tf_op jit(solution)/shard_map/all_to_all | solution.py:247
  66.2 0.0 copy-start.1
  66.2 1.1 copy-done.1
  67.4 9.0 %shard_map.155 = bf16[2048,256]{1,0:T(8,128)(2,1)} custom-call(s32[512,2]{1,0:T(8,128)} %get-tuple-element.9.col_ref, s32[2,512]{1,0:T(2,128)} %get-tuple-element.10.row_ref, bf16[2048,384]{1,0:T(8,128)(2,1)} %bitcast.16, f32[512,512]{1,0:T(8,128)} %convolution_add_fusion.edge_ref, s32[512,1]{1,0:T(8,128)} %copy.19.time_ref, f32[1,128]{1,0:T(1,128)} %bitcast.26, ...), custom_call_target="tpu_custom_call" | custom-call | tf_op jit(solution)/shard_map/pallas_call | solution.py:115
  76.4 0.0 copy-start.4
  76.4 3.9 %all-to-all-start.2 = ((bf16[128,16,256]{2,1,0:T(8,128)(2,1)}), bf16[128,16,256]{2,1,0:T(8,128)(2,1)S(1)}, u32[]{:S(2)}, u32[]{:S(2)}) async-start(bf16[128,16,256]{2,1,0:T(8,128)(2,1)} %bitcast.17), calls=%async_computation.2 | async-start | bytes 2097152 | tf_op jit(solution)/shard_map/all_to_all | solution.py:251
  80.3 0.0 copy-done.4
  80.3 0.6 reshape.85.bin_ref
  80.9 0.5 broadcast.47
  81.4 0.8 reduce.5
  82.3 0.7 reshape.81.rows_ref
  82.9 16.9 %all-to-all-done.2 = bf16[128,16,256]{2,1,0:T(8,128)(2,1)S(1)} async-done(((bf16[128,16,256]{2,1,0:T(8,128)(2,1)}), bf16[128,16,256]{2,1,0:T(8,128)(2,1)S(1)}, u32[]{:S(2)}, u32[]{:S(2)}) %all-to-all-start.2) | async-done | bytes 1048608 | tf_op jit(solution)/shard_map/all_to_all | solution.py:251
  99.9 0.0 copy-start.2
  99.9 1.0 copy-done.2
  100.9 16.1 %shard_map.156 = bf16[4096,256]{1,0:T(8,128)(2,1)} custom-call(s32[1,2048]{1,0:T(1,128)} %reshape.81.rows_ref, bf16[2048,256]{1,0:T(8,128)(2,1)} %bitcast.18, bf16[4096,256]{1,0:T(8,128)(2,1)} %mem_ref.1, bf16[256,768]{1,0:T(8,128)(2,1)} %win_ref.1, f32[1,768]{1,0:T(1,128)} %reshape.85.bin_ref, bf16[256,768]{1,0:T(8,128)(2,1)} %whid_ref.1), custom_call_target="tpu_custom_call" | custom-call | tf_op jit(solution)/shard_map/pallas_call | solution.py:52
  (1 shorter events, 0.0 us)
Async XLA Ops:
  0.0 42.0 %copy-start = (bf16[512,256]{1,0:T(8,128)(2,1)S(1)}, bf16[512,256]{1,0:T(8,128)(2,1)}, u32[]{:S(2)}) copy-start(bf16[512,256]{1,0:T(8,128)(2,1)} %param.21) | copy-start | bytes 786436
  4.1 21.1 %all-to-all-start = ((s32[128,16,1]{1,2,0:T(1,128)}), s32[128,16,1]{1,2,0:T(1,128)S(1)}, u32[]{:S(2)}, u32[]{:S(2)}) async-start(s32[128,16,1]{1,2,0:T(1,128)} %bitcast.5), calls=%async_computation | async-start | bytes 131072 | tf_op jit(solution)/shard_map/all_to_all | solution.py:245
  36.8 4.3 %copy-start.3 = (s32[512]{0:T(512)S(1)}, s32[512]{0:T(512)}, u32[]{:S(2)}) copy-start(s32[512]{0:T(512)} %param.20) | copy-start | bytes 6148
  36.8 5.2 %copy-start.5 = (f32[512]{0:T(512)S(1)}, f32[512]{0:T(512)}, u32[]{:S(2)}) copy-start(f32[512]{0:T(512)} %param.27) | copy-start | bytes 6148
  36.8 29.4 %all-to-all-start.1 = ((bf16[128,16,384]{2,1,0:T(8,128)(2,1)}), bf16[128,16,384]{2,1,0:T(8,128)(2,1)S(1)}, u32[]{:S(2)}, u32[]{:S(2)}) async-start(bf16[128,16,384]{2,1,0:T(8,128)(2,1)} %bitcast.6), calls=%async_computation.1 | async-start | bytes 3145728 | tf_op jit(solution)/shard_map/all_to_all | solution.py:247
  66.2 1.1 copy-start.1
  76.4 4.0 %copy-start.4 = (f32[768]{0:T(1024)S(1)}, f32[768]{0:T(1024)}, u32[]{:S(2)}) copy-start(f32[768]{0:T(1024)} %param.30) | copy-start | bytes 9220
  76.4 23.5 %all-to-all-start.2 = ((bf16[128,16,256]{2,1,0:T(8,128)(2,1)}), bf16[128,16,256]{2,1,0:T(8,128)(2,1)S(1)}, u32[]{:S(2)}, u32[]{:S(2)}) async-start(bf16[128,16,256]{2,1,0:T(8,128)(2,1)} %bitcast.17), calls=%async_computation.2 | async-start | bytes 2097152 | tf_op jit(solution)/shard_map/all_to_all | solution.py:251
  99.9 1.0 copy-start.2

commit v20 on v17

--- a/solution.py
+++ b/solution.py
@@ -72,11 +72,13 @@
     slot_total = fetched_ref.shape[0]
     width = out_ref.shape[1]
     time_width = fetched_ref.shape[1] - width
-    lane_ids = lax.broadcasted_iota(jnp.int32, (events, slot_total), 1)
+    lane_ids = lax.broadcasted_iota(jnp.int32, (2 * events, slot_total), 1)
+    slot_col = jnp.concatenate([col_ref[:, 0:1], col_ref[:, 1:2]], axis=0)
+    pick = (lane_ids == slot_col).astype(jnp.bfloat16)
+    rows_both = jnp.dot(pick, fetched_ref[...], preferred_element_type=jnp.float32)
     picked = []
     for side in range(2):
-        pick = (lane_ids == col_ref[:, side : side + 1]).astype(jnp.bfloat16)
-        rows = jnp.dot(pick, fetched_ref[...], preferred_element_type=jnp.float32)
+        rows = rows_both[side * events : (side + 1) * events]
         stamp = rows[:, width : width + 1].astype(jnp.int32) * 64
         stamp = stamp + rows[:, width + 1 : width + 2].astype(jnp.int32)
         delta = (time_ref[...] - stamp).astype(jnp.float32)

time: 117 us -> 118 us (level)
  no operation moved by 1% of the time
where the time goes in v20:
time: 118 us; the launch traced here: 117 us
  waiting for transfers between devices  46.3 us (39%)
  Pallas kernels  28.2 us (24%)
  starting transfers between devices  19.8 us (17%)
  matrix products  13.8 us (12%)
  local copies, waits for them, and re-layouts  6.26 us (5%)
  other arithmetic  2.94 us (2%)
    all_to_all x1, waiting for transfers between devices, local(): lax.all_to_all(served, ('ev', 'node'), split_axis=0, concat_axis=0, tiled...  22 us
    all_to_all x1, waiting for transfers between devices, local(): lax.all_to_all(outgoing, ('ev', 'node'), split_axis=0, concat_axis=0, til...  16.9 us
    pallas_call x1, Pallas kernels, owner_update(): pl.pallas_call(update_kernel, grid=(rows_count // block,), in_specs=[pl.B...  16.1 us
    dot_general x1, matrix products, owner_lookup(): jnp.dot(select, table, preferred_element_type=jnp.float32)  11.6 us
    all_to_all x1, starting transfers between devices, local(): lax.all_to_all(request, ('ev', 'node'), split_axis=0, concat_axis=0, tile...  11.5 us
    pallas_call x1, Pallas kernels, event_messages(): pl.pallas_call(message_kernel, out_shape=jax.ShapeDtypeStruct((slot_total...  9.42 us
    all_to_all x1, waiting for transfers between devices, local(): lax.all_to_all(request, ('ev', 'node'), split_axis=0, concat_axis=0, tile...  7.41 us
    all_to_all x1, starting transfers between devices, local(): lax.all_to_all(served, ('ev', 'node'), split_axis=0, concat_axis=0, tiled...  4.31 us
  transfers between devices with their start and end apart: 3, of which 3 were waited for; matrix products, arithmetic and copies ran while one was open for 7% of the time, Pallas kernels for 0%

profile of v20, /device:TPU:1, one launch (start us, length us, event | category | flops | bytes accessed | tf_op | source)
XLA Modules:
  0.0 117.4 jit_solution(7932755355222862979)
XLA Ops:
  0.0 0.0 copy-start
  0.0 2.7 %shard_map.154 = (s32[2,512]{1,0:T(2,128)}, s32[512,2]{1,0:T(8,128)}, s32[2048]{0:T(1024)}) custom-call(s32[1,512]{1,0:T(1,128)} %bitcast.22, s32[1,512]{1,0:T(1,128)} %bitcast.23, s32[1,512]{1,0:T(1,128)} %bitcast.24, s32[1,512]{1,0:T(1,128)} %bitcast.25, s32[1,512]{1,0:T(1,128)} %bitcast.20), custom_call_target="tpu_custom_call" | custom-call | tf_op jit(solution)/shard_map/pallas_call | solution.py:176
  2.7 1.4 %all_to_all.20 = s32[128,16,1]{1,0,2:T(8,128)} reshape(s32[2048]{0:T(1024)} %get-tuple-element.8) | data formatting | bytes 16384 | tf_op jit(solution)/shard_map/all_to_all | solution.py:247
  4.1 11.5 %all-to-all-start = ((s32[128,16,1]{1,2,0:T(1,128)}), s32[128,16,1]{1,2,0:T(1,128)S(1)}, u32[]{:S(2)}, u32[]{:S(2)}) async-start(s32[128,16,1]{1,2,0:T(1,128)} %bitcast.5), calls=%async_computation | async-start | bytes 131072 | tf_op jit(solution)/shard_map/all_to_all | solution.py:247
  15.7 0.7 add_select_fusion.1
  16.4 1.4 %select_convert_fusion = bf16[4096,128]{1,0:T(8,128)(2,1)S(1)} fusion(s32[4096]{0:T(1024)S(1)} %get-tuple-element.12, s32[4096]{0:T(1024)S(1)} %get-tuple-element.11, pred[128]{0:T(512)(128)(4,1)S(1)} %get-tuple-element.13, pred[128]{0:T(512)(128)(4,1)S(1)} %get-tuple-element.14), kind=kLoop, calls=%fused_computation.7 | loop fusion | flops 1572864 | bytes 1081600 | tf_op jit(solution)/shard_map/convert_element_type | solution.py:209
  17.8 7.4 %all-to-all-done = s32[128,16,1]{1,2,0:T(1,128)S(1)} async-done(((s32[128,16,1]{1,2,0:T(1,128)}), s32[128,16,1]{1,2,0:T(1,128)S(1)}, u32[]{:S(2)}, u32[]{:S(2)}) %all-to-all-start) | async-done | bytes 8224 | tf_op jit(solution)/shard_map/all_to_all | solution.py:247
  25.2 0.1 eq.39
  25.3 11.6 %fusion.5 = bf16[2048,384]{1,0:T(8,128)(2,1)} fusion(bf16[4096,128]{1,0:T(8,128)(2,1)S(1)} %select_convert_fusion, bf16[4096,256]{1,0:T(8,128)(2,1)} %mem_ref.1, s32[2048]{0:T(1024)S(1)} %eq.39), kind=kOutput, calls=%fused_computation.6 | convolution fusion | flops 6457917440 | bytes 4726784 | tf_op jit(solution)/shard_map/dot_general | solution.py:211
  36.8 0.0 copy-start.3
  36.8 0.0 copy-start.5
  36.8 4.3 %all-to-all-start.1 = ((bf16[128,16,384]{2,1,0:T(8,128)(2,1)}), bf16[128,16,384]{2,1,0:T(8,128)(2,1)S(1)}, u32[]{:S(2)}, u32[]{:S(2)}) async-start(bf16[128,16,384]{2,1,0:T(8,128)(2,1)} %bitcast.6), calls=%async_computation.1 | async-start | bytes 3145728 | tf_op jit(solution)/shard_map/all_to_all | solution.py:249
  41.2 0.0 copy-done.3
  41.2 0.9 copy.19.time_ref
  42.0 0.0 copy-done
  42.0 0.0 copy-done.5
  42.0 2.2 %convolution_add_fusion.edge_ref = f32[512,512]{1,0:T(8,128)} fusion(bf16[512,256]{1,0:T(8,128)(2,1)S(1)} %copy-done, f32[512]{0:T(512)S(1)} %copy-done.5, bf16[896,512]{1,0:T(8,128)(2,1)} %w_in_ref.1), kind=kOutput, calls=%fused_computation.8 | convolution fusion | flops 134479872 | bytes 1574912 | tf_op jit(solution)/shard_map/dot_general | solution.py:244
  44.3 22.0 %all-to-all-done.1 = bf16[128,16,384]{2,1,0:T(8,128)(2,1)S(1)} async-done(((bf16[128,16,384]{2,1,0:T(8,128)(2,1)}), bf16[128,16,384]{2,1,0:T(8,128)(2,1)S(1)}, u32[]{:S(2)}, u32[]{:S(2)}) %all-to-all-start.1) | async-done | bytes 1572896 | tf_op jit(solution)/shard_map/all_to_all | solution.py:249
  66.2 0.0 copy-start.1
  66.2 1.1 copy-done.1
  67.4 9.4 %shard_map.155 = bf16[2048,256]{1,0:T(8,128)(2,1)} custom-call(s32[512,2]{1,0:T(8,128)} %get-tuple-element.9.col_ref, s32[2,512]{1,0:T(2,128)} %get-tuple-element.10.row_ref, bf16[2048,384]{1,0:T(8,128)(2,1)} %bitcast.16, f32[512,512]{1,0:T(8,128)} %convolution_add_fusion.edge_ref, s32[512,1]{1,0:T(8,128)} %copy.19.time_ref, f32[1,128]{1,0:T(1,128)} %bitcast.26, ...), custom_call_target="tpu_custom_call" | custom-call | tf_op jit(solution)/shard_map/pallas_call | solution.py:117
  76.8 0.0 copy-start.4
  76.8 4.0 %all-to-all-start.2 = ((bf16[128,16,256]{2,1,0:T(8,128)(2,1)}), bf16[128,16,256]{2,1,0:T(8,128)(2,1)S(1)}, u32[]{:S(2)}, u32[]{:S(2)}) async-start(bf16[128,16,256]{2,1,0:T(8,128)(2,1)} %bitcast.17), calls=%async_computation.2 | async-start | bytes 2097152 | tf_op jit(solution)/shard_map/all_to_all | solution.py:253
  80.8 0.0 copy-done.4
  80.8 0.6 reshape.85.bin_ref
  81.4 0.5 broadcast.47
  81.9 0.8 reduce.5
  82.7 0.7 reshape.81.rows_ref
  83.4 16.9 %all-to-all-done.2 = bf16[128,16,256]{2,1,0:T(8,128)(2,1)S(1)} async-done(((bf16[128,16,256]{2,1,0:T(8,128)(2,1)}), bf16[128,16,256]{2,1,0:T(8,128)(2,1)S(1)}, u32[]{:S(2)}, u32[]{:S(2)}) %all-to-all-start.2) | async-done | bytes 1048608 | tf_op jit(solution)/shard_map/all_to_all | solution.py:253
  100.3 0.0 copy-start.2
  100.3 1.0 copy-done.2
  101.3 16.1 %shard_map.156 = bf16[4096,256]{1,0:T(8,128)(2,1)} custom-call(s32[1,2048]{1,0:T(1,128)} %reshape.81.rows_ref, bf16[2048,256]{1,0:T(8,128)(2,1)} %bitcast.18, bf16[4096,256]{1,0:T(8,128)(2,1)} %mem_ref.1, bf16[256,768]{1,0:T(8,128)(2,1)} %win_ref.1, f32[1,768]{1,0:T(1,128)} %reshape.85.bin_ref, bf16[256,768]{1,0:T(8,128)(2,1)} %whid_ref.1), custom_call_target="tpu_custom_call" | custom-call | tf_op jit(solution)/shard_map/pallas_call | solution.py:52
  (1 shorter events, 0.0 us)
Async XLA Ops:
  0.0 42.0 %copy-start = (bf16[512,256]{1,0:T(8,128)(2,1)S(1)}, bf16[512,256]{1,0:T(8,128)(2,1)}, u32[]{:S(2)}) copy-start(bf16[512,256]{1,0:T(8,128)(2,1)} %param.21) | copy-start | bytes 786436
  4.1 21.1 %all-to-all-start = ((s32[128,16,1]{1,2,0:T(1,128)}), s32[128,16,1]{1,2,0:T(1,128)S(1)}, u32[]{:S(2)}, u32[]{:S(2)}) async-start(s32[128,16,1]{1,2,0:T(1,128)} %bitcast.5), calls=%async_computation | async-start | bytes 131072 | tf_op jit(solution)/shard_map/all_to_all | solution.py:247
  36.8 4.3 %copy-start.3 = (s32[512]{0:T(512)S(1)}, s32[512]{0:T(512)}, u32[]{:S(2)}) copy-start(s32[512]{0:T(512)} %param.20) | copy-start | bytes 6148
  36.8 5.2 %copy-start.5 = (f32[512]{0:T(512)S(1)}, f32[512]{0:T(512)}, u32[]{:S(2)}) copy-start(f32[512]{0:T(512)} %param.27) | copy-start | bytes 6148
  36.8 29.4 %all-to-all-start.1 = ((bf16[128,16,384]{2,1,0:T(8,128)(2,1)}), bf16[128,16,384]{2,1,0:T(8,128)(2,1)S(1)}, u32[]{:S(2)}, u32[]{:S(2)}) async-start(bf16[128,16,384]{2,1,0:T(8,128)(2,1)} %bitcast.6), calls=%async_computation.1 | async-start | bytes 3145728 | tf_op jit(solution)/shard_map/all_to_all | solution.py:249
  66.2 1.1 copy-start.1
  76.8 4.0 %copy-start.4 = (f32[768]{0:T(1024)S(1)}, f32[768]{0:T(1024)}, u32[]{:S(2)}) copy-start(f32[768]{0:T(1024)} %param.30) | copy-start | bytes 9220
  76.8 23.5 %all-to-all-start.2 = ((bf16[128,16,256]{2,1,0:T(8,128)(2,1)}), bf16[128,16,256]{2,1,0:T(8,128)(2,1)S(1)}, u32[]{:S(2)}, u32[]{:S(2)}) async-start(bf16[128,16,256]{2,1,0:T(8,128)(2,1)} %bitcast.17), calls=%async_computation.2 | async-start | bytes 2097152 | tf_op jit(solution)/shard_map/all_to_all | solution.py:253
  100.3 1.0 copy-start.2
